TPU v7x, 256 devices: a whole 4x4x8 slice. The times are simulated.
256 devices in a mesh: dp: 4 (over y_lo, core), ep: 64 (over y_hi, x, z).
Axes of the slice: x: 4, y: 4 (y_hi: 2, y_lo: 2; y = y_hi * 2 + y_lo), z: 8, core: 2. Of those that a mesh axis runs over, the one named last changes fastest.
Arguments:
- tokens: bfloat16 [32768, 2048], P(('dp', 'ep')), may hold values from -6 to 6
- expert_ids: int32 [32768, 6], P(('dp', 'ep')), may hold values from 0 to 63, all different within a row; in each aligned block of 128 rows (0 to 127, 128 to 255, ...) at most 13 rows name the same one
- gate_scales: float32 [32768, 6], P(('dp', 'ep')), may hold values from 0.05 to 0.5
- expert_slot: int32 [64], replicated, may hold values from 0 to 63, each once
- gate_weight: bfloat16 [64, 2048, 1408], P('ep', 'dp'), may hold values from -0.125 to 0.125
- up_weight: bfloat16 [64, 2048, 1408], P('ep', 'dp'), may hold values from -0.125 to 0.125
- down_weight: bfloat16 [64, 1408, 2048], P('ep', None, 'dp'), may hold values from -0.15625 to 0.15625
Outputs:
- mixed: bfloat16 [32768, 2048], P(('dp', 'ep'))
Inputs may be any that keep to these rules, and one draw needn't show every extreme that they name: `expert_ids`: among the 128 tokens of one device no expert is chosen by more than 13; the 6 experts of a token differ. `expert_slot`: each expert has exactly one slot.
All inputs are finite; a program needn't handle non-finite values.
Results may differ from a plain program's by a relative error of at most 0.0057.
Values may be sent and summed in bfloat16 or wider, within the bound.
No kernel may reach another device: no remote copies, remote signals or barrier semaphores. Data moves between devices by JAX's collectives and lax.ppermute only.
A program may use at most 128 MiB of HBM per device.

v0:
```python
import jax
import jax.numpy as jnp
from jax import lax
from jax.sharding import PartitionSpec as P

C = 13


def local(tokens, expert_ids, gate_scales, expert_slot, gate_weight, up_weight, down_weight):
    tok_rows = tokens.shape[0]
    width = tokens.shape[1]
    top = expert_ids.shape[1]
    experts = expert_slot.shape[0]
    exp_dev = gate_weight.shape[0]
    n_ep = lax.axis_size("ep")
    capacity = C
    ids = expert_ids.reshape(-1)
    onehot = (ids[:, None] == jnp.arange(experts, dtype=jnp.int32)[None, :]).astype(jnp.int32)
    earlier = jnp.cumsum(onehot, 0) - onehot
    rank = jnp.sum(earlier * onehot, 1)
    target = jnp.sum(onehot * expert_slot[None, :], 1)
    flat_slot = target * capacity + rank
    sources = jnp.repeat(tokens, top, axis=0)
    send = jnp.zeros((experts * capacity, width), jnp.bfloat16).at[flat_slot].set(sources)
    send = send.reshape(n_ep, exp_dev, capacity, width)
    received = lax.all_to_all(send, "ep", split_axis=0, concat_axis=0, tiled=True)
    gate = jnp.einsum(
        "secd,edf->secf",
        received,
        lax.all_gather(gate_weight, "dp", axis=1, tiled=True),
        preferred_element_type=jnp.float32,
    )
    up = jnp.einsum(
        "secd,edf->secf",
        received,
        lax.all_gather(up_weight, "dp", axis=1, tiled=True),
        preferred_element_type=jnp.float32,
    )
    gate, up = (gate, up)
    hidden = (jax.nn.silu(gate) * up).astype(jnp.bfloat16)
    expert_out = jnp.einsum(
        "secf,efd->secd",
        hidden,
        lax.all_gather(down_weight, "dp", axis=2, tiled=True),
        preferred_element_type=jnp.float32,
    ).astype(jnp.bfloat16)
    returned = lax.all_to_all(expert_out, "ep", split_axis=0, concat_axis=0, tiled=True)
    returned = returned.reshape(experts * capacity, width)
    picked = returned[flat_slot].reshape(tok_rows, top, width)
    mixed = jnp.sum(gate_scales[:, :, None] * picked.astype(jnp.float32), 1)
    return mixed.astype(jnp.bfloat16)


def solution(mesh):
    in_specs = (
        P(("dp", "ep"), None),
        P(("dp", "ep"), None),
        P(("dp", "ep"), None),
        P(),
        P("ep", "dp", None),
        P("ep", "dp", None),
        P("ep", None, "dp"),
    )
    out_specs = P(("dp", "ep"), None)
    return jax.shard_map(local, mesh=mesh, in_specs=in_specs, out_specs=out_specs, check_vma=False)
```

profile of v0, /device:TPU:38, one launch (start us, length us, event | category | flops | bytes accessed | tf_op | source)
XLA Modules:
  0.0 394.0 jit_solution(14019517613830099911)
XLA Ops:
  6.5 0.0 all-gather.6.cloned.1.call-start
  6.5 0.7 all-gather.6.cloned.1.call-update
  7.3 0.0 all-gather.4.cloned.1.call-start
  7.3 0.7 all-gather.4.cloned.1.call-update
  8.0 0.8 copy.16
  8.8 0.1 eq.29
  8.9 0.1 eq.25
  9.1 1.8 reduce-window.6
  10.9 0.3 slice_reduce_fusion
  11.2 0.0 copy-done
  11.2 2.7 broadcast_in_dim.5
  13.9 6.4 %reshape.99 = bf16[768,2048]{1,0:T(8,128)(2,1)} reshape(bf16[128,6,2048]{2,1,0:T(8,128)(2,1)} %broadcast_in_dim.5) | data formatting | bytes 6291456 | tf_op jit(solution)/shard_map/reshape | solution.py:23
  20.3 0.1 select_reduce_fusion
  20.5 8.9 %scatter_custom_fusion = bf16[832,2048]{1,0:T(8,128)(2,1)S(1)} fusion(s32[768]{0:T(1024)S(1)} %fusion.33, bf16[768,2048]{1,0:T(8,128)(2,1)} %reshape.99, bf16[]{:T(256)} %constant.6.clone.1), kind=kCustom, calls=%fused_computation.23 | custom fusion | bytes 3408384 | tf_op jit(solution)/shard_map/scatter | solution.py:24
  29.4 2.9 reshape.79
  32.3 14.6 %all-to-all-start = ((bf16[64,1,13,2048]{3,2,1,0:T(8,128)(2,1)}), bf16[64,1,13,2048]{3,2,1,0:T(8,128)(2,1)}, u32[]{:S(2)}, u32[]{:S(2)}) async-start(bf16[64,1,13,2048]{3,2,1,0:T(8,128)(2,1)} %bitcast.86), calls=%async_computation | async-start | bytes 8388608 | tf_op jit(solution)/shard_map/all_to_all | solution.py:26
  46.9 0.2 all-gather.8.cloned.1.call-start
  47.1 0.5 all-gather.8.cloned.1.call-update
  47.7 96.9 %all-to-all-done = bf16[64,1,13,2048]{3,2,1,0:T(8,128)(2,1)} async-done(((bf16[64,1,13,2048]{3,2,1,0:T(8,128)(2,1)}), bf16[64,1,13,2048]{3,2,1,0:T(8,128)(2,1)}, u32[]{:S(2)}, u32[]{:S(2)}) %all-to-all-start) | async-done | bytes 3407904 | tf_op jit(solution)/shard_map/all_to_all | solution.py:26
  144.5 12.7 %fusion.2 = f32[64,13,1408]{2,0,1:T(8,128)} fusion(bf16[1,2048,1408]{2,1,0:T(8,128)(2,1)} %all-gather.6.cloned.1.call-done, bf16[64,1,13,2048]{3,2,1,0:T(8,128)(2,1)} %all-to-all-done), kind=kOutput, calls=%fused_computation.5 | convolution fusion | flops 4798283776 | bytes 13860864 | tf_op jit(solution)/shard_map/secd,edf->secf/dot_general | solution.py:33
  157.2 21.4 %all-gather.4.cloned.1.call-done = bf16[1,2048,1408]{2,1,0:T(8,128)(2,1)} async-done(((bf16[1,512,1408]{2,1,0:T(8,128)(2,1)}), bf16[1,2048,1408]{2,1,0:T(8,128)(2,1)}) %all-gather.4.cloned.1.call-update) | async-done | bytes 5767184 | tf_op jit(solution)/shard_map/all_gather | solution.py:30
  178.7 12.3 %fusion.20 = bf16[64,13,1408]{2,0,1:T(8,128)(2,1)S(1)} fusion(f32[64,13,1408]{2,0,1:T(8,128)} %fusion.2, bf16[1,2048,1408]{2,1,0:T(8,128)(2,1)} %all-gather.4.cloned.1.call-done, bf16[64,1,13,2048]{3,2,1,0:T(8,128)(2,1)} %all-to-all-done), kind=kOutput, calls=%fused_computation.20 | convolution fusion | flops 4805312512 | bytes 16203776 | tf_op jit(solution)/shard_map/secd,edf->secf/dot_general | solution.py:27
  190.9 51.5 %all-gather.8.cloned.1.call-done = bf16[1,1408,2048]{2,1,0:T(8,128)(2,1)} async-done(((bf16[1,1408,512]{2,1,0:T(8,128)(2,1)}), bf16[1,1408,2048]{2,1,0:T(8,128)(2,1)}) %all-gather.8.cloned.1.call-update) | async-done | bytes 5767184 | tf_op jit(solution)/shard_map/all_gather | solution.py:44
  242.4 8.3 %fusion.17 = bf16[64,1,13,2048]{3,0,2,1:T(8,128)(2,1)S(1)} fusion(bf16[64,13,1408]{2,0,1:T(8,128)(2,1)S(1)} %fusion.20, bf16[1,1408,2048]{2,1,0:T(8,128)(2,1)} %all-gather.8.cloned.1.call-done), kind=kOutput, calls=%fused_computation.19 | convolution fusion | flops 4799987712 | bytes 11517952 | tf_op jit(solution)/shard_map/secf,efd->secd/dot_general | solution.py:41
  250.8 3.9 copy.21
  254.6 13.0 %all-to-all-start.1 = ((bf16[64,1,13,2048]{3,2,1,0:T(8,128)(2,1)}), bf16[64,1,13,2048]{3,2,1,0:T(8,128)(2,1)}, u32[]{:S(2)}, u32[]{:S(2)}) async-start(bf16[64,1,13,2048]{3,2,1,0:T(8,128)(2,1)} %copy.21), calls=%async_computation.1 | async-start | bytes 8388608 | tf_op jit(solution)/shard_map/all_to_all | solution.py:47
  267.6 0.1 copy.15
  267.8 98.0 %all-to-all-done.1 = bf16[64,1,13,2048]{3,2,1,0:T(8,128)(2,1)} async-done(((bf16[64,1,13,2048]{3,2,1,0:T(8,128)(2,1)}), bf16[64,1,13,2048]{3,2,1,0:T(8,128)(2,1)}, u32[]{:S(2)}, u32[]{:S(2)}) %all-to-all-start.1) | async-done | bytes 3407904 | tf_op jit(solution)/shard_map/all_to_all | solution.py:47
  365.7 3.4 reshape.85
  369.2 4.3 %gather_fusion = bf16[768,2048]{1,0:T(8,128)(2,1)} fusion(bf16[832,2048]{1,0:T(8,128)(2,1)S(1)} %reshape.85, s32[1024]{0:T(1024)S(1)} %pad_clamp_fusion), kind=kCustom, calls=%fused_computation | custom fusion | bytes 6294528 | tf_op jit(solution)/shard_map/gather | solution.py:49
  373.5 6.6 %reshape.86 = f32[128,6,2048]{2,1,0:T(8,128)} reshape(bf16[768,2048]{1,0:T(8,128)(2,1)} %gather_fusion) | data formatting | bytes 9437184 | tf_op jit(solution)/shard_map/convert_element_type | solution.py:50
  380.1 7.4 %multiply_reduce_fusion = bf16[128,2048]{1,0:T(8,128)(2,1)} fusion(f32[128,6,2048]{2,1,0:T(8,128)} %reshape.86, f32[128,6]{1,0:T(8,128)S(1)} %copy.15), kind=kLoop, calls=%fused_computation.2 | loop fusion | flops 2883584 | bytes 6818816 | tf_op jit(solution)/shard_map/reduce_sum | solution.py:50
  (11 shorter events, 0.1 us)
Async XLA Ops:
  6.5 4.7 %copy-start = (bf16[128,2048]{1,0:T(8,128)(2,1)S(1)}, bf16[128,2048]{1,0:T(8,128)(2,1)}, u32[]{:S(2)}) copy-start(bf16[128,2048]{1,0:T(8,128)(2,1)} %param.7) | copy-start | bytes 1572868
  6.5 138.0 %all-gather.6.cloned.1.call-start = ((), (), s32[]{:S(2)}) async-start(), calls=%async_computation.3 | async-start | bytes 7208960 | tf_op jit(solution)/shard_map/all_gather | solution.py:36
  7.3 171.4 %all-gather.4.cloned.1.call-start = ((), (), s32[]{:S(2)}) async-start(), calls=%async_computation.2 | async-start | bytes 7208960 | tf_op jit(solution)/shard_map/all_gather | solution.py:30
  13.9 6.4 %copy-start.2 = (s32[64]{0:T(128)S(1)}, s32[64]{0:T(128)}, u32[]{:S(2)}) copy-start(s32[64]{0:T(128)} %param.10) | copy-start | bytes 772
  32.3 112.2 %all-to-all-start = ((bf16[64,1,13,2048]{3,2,1,0:T(8,128)(2,1)}), bf16[64,1,13,2048]{3,2,1,0:T(8,128)(2,1)}, u32[]{:S(2)}, u32[]{:S(2)}) async-start(bf16[64,1,13,2048]{3,2,1,0:T(8,128)(2,1)} %bitcast.86), calls=%async_computation | async-start | bytes 8388608 | tf_op jit(solution)/shard_map/all_to_all | solution.py:26
  46.9 195.5 %all-gather.8.cloned.1.call-start = ((), (), s32[]{:S(2)}) async-start(), calls=%async_computation.4 | async-start | bytes 7208960 | tf_op jit(solution)/shard_map/all_gather | solution.py:44
  254.6 13.0 %copy-start.1 = (f32[128,6]{0,1:T(8,128)S(1)}, f32[128,6]{0,1:T(8,128)}, u32[]{:S(2)}) copy-start(f32[128,6]{0,1:T(8,128)} %param.9) | copy-start | bytes 9220
  254.6 111.1 %all-to-all-start.1 = ((bf16[64,1,13,2048]{3,2,1,0:T(8,128)(2,1)}), bf16[64,1,13,2048]{3,2,1,0:T(8,128)(2,1)}, u32[]{:S(2)}, u32[]{:S(2)}) async-start(bf16[64,1,13,2048]{3,2,1,0:T(8,128)(2,1)} %copy.21), calls=%async_computation.1 | async-start | bytes 8388608 | tf_op jit(solution)/shard_map/all_to_all | solution.py:47
Sparse Core Ops, SparseCore 0:
  9.1 87.9 all-gather.5
  99.0 79.6 all-gather.3
  180.5 61.9 all-gather.7
where the time goes:
time: 396 us; the launch traced here: 394 us
  waiting for transfers between devices  270 us (68%)
  local copies, waits for them, and re-layouts  40.6 us (10%)
  matrix products  33.3 us (8%)
  starting transfers between devices  27.8 us (7%)
  between operations  13.2 us (3%)
  other arithmetic  9.4 us (2%)
    all_to_all x1, waiting for transfers between devices, local(): lax.all_to_all(expert_out, 'ep', split_axis=0, concat_axis=0, tiled=True)  98 us
    all_to_all x1, waiting for transfers between devices, local(): lax.all_to_all(send, 'ep', split_axis=0, concat_axis=0, tiled=True)  96.9 us
    all_gather x1, waiting for transfers between devices, local(): lax.all_gather(down_weight, 'dp', axis=2, tiled=True)  51.5 us
    all_gather x1, waiting for transfers between devices, local(): lax.all_gather(gate_weight, 'dp', axis=1, tiled=True)  21.4 us
    all_to_all x1, starting transfers between devices, local(): lax.all_to_all(send, 'ep', split_axis=0, concat_axis=0, tiled=True)  14.6 us
    all_to_all x1, starting transfers between devices, local(): lax.all_to_all(expert_out, 'ep', split_axis=0, concat_axis=0, tiled=True)  13 us
    dot_general x1, matrix products, local(): jnp.einsum('secd,edf->secf', received, lax.all_gather(up_weight, 'dp', ax...  12.7 us
    dot_general x1, matrix products, local(): jnp.einsum('secd,edf->secf', received, lax.all_gather(gate_weight, 'dp',...  12.3 us
  transfers between devices with their start and end apart: 5, of which 4 were waited for; matrix products, arithmetic and copies ran while one was open for 13% of the time, Pallas kernels for 0%

commit v1 on v0

v1 whole, which is shorter than its diff:
```python
import jax
import jax.numpy as jnp
from jax import lax
from jax.sharding import PartitionSpec as P

C = 13
OFFS = (0, 2, 1, 3)


def _perm(n, m):
    return [(i, i ^ m) for i in range(n)]


def _dp_gather(ws, axis):
    n = lax.axis_size("dp")
    cross = lax.ppermute(ws, "dp", _perm(n, 2))
    near = lax.ppermute(ws, "dp", _perm(n, 1))
    far = lax.ppermute(cross, "dp", _perm(n, 1))
    return [jnp.concatenate(parts, axis=axis) for parts in zip(ws, cross, near, far)]


def _blocks(x, idx):
    rows, width = x.shape
    nb = idx.shape[0]
    return jnp.take(x.reshape(rows, nb, width // nb), idx, axis=1).reshape(rows, width)


def local(tokens, expert_ids, gate_scales, expert_slot, gate_weight, up_weight, down_weight):
    tok_rows, width = tokens.shape
    top = expert_ids.shape[1]
    experts = expert_slot.shape[0]
    n_ep = lax.axis_size("ep")
    n_dp = lax.axis_size("dp")
    assert n_dp == len(OFFS) and gate_weight.shape[0] == 1 and experts == n_ep
    cap = C
    slots = experts * cap

    wg, wu = _dp_gather((gate_weight[0], up_weight[0]), 0)
    (wd,) = _dp_gather((down_weight[0],), 1)

    d = lax.axis_index("dp")
    offs = jnp.array(OFFS, jnp.int32)
    src_blk = d ^ offs
    inv = jnp.argsort(offs).astype(jnp.int32)
    out_blk = inv[d ^ jnp.arange(n_dp, dtype=jnp.int32)]

    ids = expert_ids.reshape(-1)
    onehot = (ids[:, None] == jnp.arange(experts, dtype=jnp.int32)[None, :]).astype(jnp.int32)
    rank = jnp.sum((jnp.cumsum(onehot, 0) - onehot) * onehot, 1)
    target = jnp.sum(onehot * expert_slot[None, :], 1)
    flat = (target * cap + rank).reshape(tok_rows, top)

    rows_j = jnp.arange(slots, dtype=jnp.int32)
    pick = jnp.any(flat[None, :, :] == rows_j[:, None, None], axis=2).astype(jnp.bfloat16)
    tokens_rel = _blocks(tokens, src_blk)
    send = jnp.dot(pick, tokens_rel, preferred_element_type=jnp.float32).astype(jnp.bfloat16)
    received = lax.all_to_all(send.reshape(n_ep, 1, cap, width), "ep", 0, 0, tiled=True)
    received = received.reshape(slots, width)

    gate = jnp.dot(received, wg, preferred_element_type=jnp.float32)
    up = jnp.dot(received, wu, preferred_element_type=jnp.float32)
    hidden = (jax.nn.silu(gate) * up).astype(jnp.bfloat16)
    expert_out = jnp.dot(hidden, wd, preferred_element_type=jnp.float32).astype(jnp.bfloat16)

    returned = lax.all_to_all(expert_out.reshape(n_ep, 1, cap, width), "ep", 0, 0, tiled=True)
    returned = returned.reshape(slots, width)

    hit = flat[:, :, None] == rows_j[None, None, :]
    weights = jnp.sum(jnp.where(hit, gate_scales[:, :, None], 0.0), axis=1)
    w_hi = weights.astype(jnp.bfloat16)
    w_lo = (weights - w_hi.astype(jnp.float32)).astype(jnp.bfloat16)
    mixed = jnp.dot(w_hi, returned, preferred_element_type=jnp.float32)
    mixed = mixed + jnp.dot(w_lo, returned, preferred_element_type=jnp.float32)
    return _blocks(mixed.astype(jnp.bfloat16), out_blk)


def solution(mesh):
    in_specs = (
        P(("dp", "ep"), None),
        P(("dp", "ep"), None),
        P(("dp", "ep"), None),
        P(),
        P("ep", "dp", None),
        P("ep", "dp", None),
        P("ep", None, "dp"),
    )
    out_specs = P(("dp", "ep"), None)
    return jax.shard_map(local, mesh=mesh, in_specs=in_specs, out_specs=out_specs, check_vma=False)
```

time: 396 us -> 324 us (0.82)
  waiting for transfers between devices: 270 us -> 232 us
  local copies, waits for them, and re-layouts: 40.6 us -> 21.9 us
  between operations: 13.2 us -> 0.26 us
  other arithmetic: 9.4 us -> 5.08 us
    ppermute x0 -> x9, waiting for transfers between devices: none -> 135 us  [the longest x3 135 us: _dp_gather(): cross = lax.ppermute(ws, 'dp', _perm(n, 2))]
    all_to_all x2, waiting for transfers between devices: 195 us -> 96.6 us  [the longest x1 96.6 us: local(): lax.all_to_all(expert_out.reshape(n_ep, 1, cap, width), 'ep', 0, 0, tiled...]
    all_gather x3 -> x0, waiting for transfers between devices: 72.9 us -> none  [the longest x1 51.5 us: local(): lax.all_gather(down_weight, 'dp', axis=2, tiled=True)]
    convert_element_type x2 -> x0, local copies, waits for them, and re-layouts: 10.4 us -> none  [the longest x1 6.55 us: local(): mixed = jnp.sum(gate_scales[:, :, None] * picked.astype(jnp.float32), 1)]
    scatter x1 -> x0, local copies, waits for them, and re-layouts: 8.95 us -> none  [local(): jnp.zeros((experts * capacity, width), jnp.bfloat16).at[flat_slot]]
    reduce_sum x1, other arithmetic: 7.39 us -> 1.06 us  [local(): weights = jnp.sum(jnp.where(hit, gate_scales[:, :, None], 0.0), axis=1)]
    reshape x3 -> x7, local copies, waits for them, and re-layouts: 12.7 us -> 16 us  [the longest x1 4.93 us: local(): expert_out.reshape(n_ep, 1, cap, width)]
    dot_general x3 -> x5, matrix products: 33.3 us -> 32.3 us  [the longest x1 17.5 us: local(): jnp.dot(hidden, wd, preferred_element_type=jnp.float32).astype(jnp.bfloat16)]
  transfers between devices with their start and end apart: 5 -> 11, of which waited for: 4 -> 4; matrix products, arithmetic and copies ran while one was open for 13% -> 5% of each run, Pallas kernels for 0% -> 0%
where the time goes in v1:
time: 324 us; the launch traced here: 323 us
  waiting for transfers between devices  232 us (72%)
  matrix products  32.3 us (10%)
  starting transfers between devices  31.6 us (10%)
  local copies, waits for them, and re-layouts  21.9 us (7%)
  other arithmetic  5.08 us (2%)
    ppermute x3, waiting for transfers between devices, _dp_gather(): cross = lax.ppermute(ws, 'dp', _perm(n, 2))  135 us
    all_to_all x1, waiting for transfers between devices, local(): lax.all_to_all(expert_out.reshape(n_ep, 1, cap, width), 'ep', 0, 0, tiled...  96.6 us
    dot_general x1, matrix products, local(): jnp.dot(hidden, wd, preferred_element_type=jnp.float32).astype(jnp.bfloat16)  17.5 us
    all_to_all x1, starting transfers between devices, local(): lax.all_to_all(send.reshape(n_ep, 1, cap, width), 'ep', 0, 0, tiled=True)  14.5 us
    all_to_all x1, starting transfers between devices, local(): lax.all_to_all(expert_out.reshape(n_ep, 1, cap, width), 'ep', 0, 0, tiled...  13.7 us
    dot_general x1, matrix products, local(): up = jnp.dot(received, wu, preferred_element_type=jnp.float32)  10.2 us
  transfers between devices with their start and end apart: 11, of which 4 were waited for; matrix products, arithmetic and copies ran while one was open for 5% of the time, Pallas kernels for 0%

profile of v1, /device:TPU:38, one launch (start us, length us, event | category | flops | bytes accessed | tf_op | source)
XLA Modules:
  0.0 323.2 jit_solution(2690701885364654220)
XLA Ops:
  0.0 0.8 copy.37
  1.1 1.8 reduce-window.6
  2.9 0.3 slice_reduce_fusion
  3.2 0.8 select_reduce_fusion.1
  4.2 0.4 fusion.27
  4.7 0.7 compare_and_fusion.1
  5.3 1.3 copy.42
  6.9 0.6 gather_fusion.1
  7.6 1.0 copy.44
  8.6 2.1 convolution_convert_fusion
  10.7 2.9 reshape.90
  13.6 14.5 %all-to-all-start = ((bf16[64,1,13,2048]{3,2,1,0:T(8,128)(2,1)}), bf16[64,1,13,2048]{3,2,1,0:T(8,128)(2,1)}, u32[]{:S(2)}, u32[]{:S(2)}) async-start(bf16[64,1,13,2048]{3,2,1,0:T(8,128)(2,1)} %bitcast.44), calls=%async_computation | async-start | bytes 8388608 | tf_op jit(solution)/shard_map/all_to_all | solution.py:57
  28.1 0.8 collective-permute-start.3
  28.9 1.3 collective-permute-start
  30.2 0.7 collective-permute-start.6
  30.9 56.5 %collective-permute-done.3 = bf16[512,1408]{1,0:T(8,128)(2,1)} collective-permute-done((bf16[512,1408]{1,0:T(8,128)(2,1)S(1)}, bf16[512,1408]{1,0:T(8,128)(2,1)}, u32[]{:S(2)}, u32[]{:S(2)}) %collective-permute-start.3) | collective-permute-done | bytes 1441824 | tf_op jit(solution)/shard_map/ppermute | solution.py:16
  87.4 0.5 collective-permute-start.1
  88.0 48.2 %collective-permute-done = bf16[512,1408]{1,0:T(8,128)(2,1)} collective-permute-done((bf16[512,1408]{1,0:T(8,128)(2,1)}, bf16[512,1408]{1,0:T(8,128)(2,1)}, u32[]{:S(2)}, u32[]{:S(2)}) %collective-permute-start) | collective-permute-done | bytes 1441824 | tf_op jit(solution)/shard_map/ppermute | solution.py:16
  136.2 30.6 %collective-permute-done.6 = bf16[1408,512]{1,0:T(8,128)(2,1)} collective-permute-done((bf16[1408,512]{1,0:T(8,128)(2,1)}, bf16[1408,512]{1,0:T(8,128)(2,1)}, u32[]{:S(2)}, u32[]{:S(2)}) %collective-permute-start.6) | collective-permute-done | bytes 1441824 | tf_op jit(solution)/shard_map/ppermute | solution.py:16
  166.9 3.5 %reshape.91 = bf16[832,2048]{1,0:T(8,128)(2,1)S(1)} reshape(bf16[64,1,13,2048]{3,2,1,0:T(8,128)(2,1)} %all-to-all-done) | data formatting | bytes 6815744 | tf_op jit(solution)/shard_map/reshape | solution.py:58
  170.3 10.2 %fusion.8 = f32[832,1408]{1,0:T(8,128)} fusion(bf16[832,2048]{1,0:T(8,128)(2,1)S(1)} %reshape.91, bf16[512,1408]{1,0:T(8,128)(2,1)} %collective-permute-done.5, bf16[512,1408]{1,0:T(8,128)(2,1)} %copy-done.4, bf16[512,1408]{1,0:T(8,128)(2,1)} %collective-permute-done.3, bf16[512,1408]{1,0:T(8,128)(2,1)} %bitcast.52), kind=kOutput, calls=%fused_computation.11 | convolution fusion | flops 4821352448 | bytes 13860864 | tf_op jit(solution)/shard_map/dot_general | solution.py:61
  180.6 17.5 %fusion.24 = bf16[832,2048]{1,0:T(8,128)(2,1)} fusion(bf16[1408,512]{1,0:T(8,128)(2,1)} %collective-permute-done.8, bf16[1408,512]{1,0:T(8,128)(2,1)} %collective-permute-done.7, bf16[1408,512]{1,0:T(8,128)(2,1)} %collective-permute-done.6, bf16[1408,512]{1,0:T(8,128)(2,1)} %bitcast.8, f32[832,1408]{1,0:T(8,128)} %fusion.8, ...), kind=kOutput, calls=%fused_computation.28 | convolution fusion | flops 9651437568 | bytes 23035904 | tf_op jit(solution)/shard_map/dot_general | solution.py:63
  198.1 4.9 %reshape.92 = bf16[64,1,13,2048]{3,2,0,1:T(8,128)(2,1)} reshape(bf16[832,2048]{1,0:T(8,128)(2,1)} %fusion.24) | data formatting | bytes 6815744 | tf_op jit(solution)/shard_map/reshape | solution.py:65
  203.0 13.7 %all-to-all-start.1 = ((bf16[64,1,13,2048]{3,2,1,0:T(8,128)(2,1)}), bf16[64,1,13,2048]{3,2,1,0:T(8,128)(2,1)}, u32[]{:S(2)}, u32[]{:S(2)}) async-start(bf16[64,1,13,2048]{3,2,1,0:T(8,128)(2,1)} %bitcast.45), calls=%async_computation.1 | async-start | bytes 8388608 | tf_op jit(solution)/shard_map/all_to_all | solution.py:65
  216.8 0.6 gather_fusion
  217.4 1.1 select_reduce_fusion
  218.5 96.6 %all-to-all-done.1 = bf16[64,1,13,2048]{3,2,1,0:T(8,128)(2,1)} async-done(((bf16[64,1,13,2048]{3,2,1,0:T(8,128)(2,1)}), bf16[64,1,13,2048]{3,2,1,0:T(8,128)(2,1)}, u32[]{:S(2)}, u32[]{:S(2)}) %all-to-all-start.1) | async-done | bytes 3407904 | tf_op jit(solution)/shard_map/all_to_all | solution.py:65
  315.1 3.4 %reshape.93 = bf16[832,2048]{1,0:T(8,128)(2,1)S(1)} reshape(bf16[64,1,13,2048]{3,2,1,0:T(8,128)(2,1)} %all-to-all-done.1) | data formatting | bytes 6815744 | tf_op jit(solution)/shard_map/reshape | solution.py:66
  318.5 1.8 fusion.39
  320.4 0.7 fusion.28
  321.2 0.6 gather_fusion.2
  322.1 1.0 copy.49
  (40 shorter events, 1.4 us)
Async XLA Ops:
  13.6 14.5 %copy-start.3 = (bf16[1,512,1408]{2,1,0:T(8,128)(2,1)S(1)}, bf16[1,512,1408]{2,1,0:T(8,128)(2,1)}, u32[]{:S(2)}) copy-start(bf16[1,512,1408]{2,1,0:T(8,128)(2,1)} %param.15) | copy-start | bytes 4325380
  13.6 153.3 %all-to-all-start = ((bf16[64,1,13,2048]{3,2,1,0:T(8,128)(2,1)}), bf16[64,1,13,2048]{3,2,1,0:T(8,128)(2,1)}, u32[]{:S(2)}, u32[]{:S(2)}) async-start(bf16[64,1,13,2048]{3,2,1,0:T(8,128)(2,1)} %bitcast.44), calls=%async_computation | async-start | bytes 8388608 | tf_op jit(solution)/shard_map/all_to_all | solution.py:57
  28.1 59.3 %collective-permute-start.3 = (bf16[512,1408]{1,0:T(8,128)(2,1)S(1)}, bf16[512,1408]{1,0:T(8,128)(2,1)}, u32[]{:S(2)}, u32[]{:S(2)}) collective-permute-start(bf16[512,1408]{1,0:T(8,128)(2,1)S(1)} %bitcast.53), channel_id=1, source_target_pairs={{0,128},{64,192},{128,0},{192,64},{1,129},{65,193},{129,1},{193,65... | collective-permute-start | bytes 4325384 | tf_op jit(solution)/shard_map/ppermute | solution.py:16
  28.9 59.1 %collective-permute-start.4 = (bf16[512,1408]{1,0:T(8,128)(2,1)S(1)}, bf16[512,1408]{1,0:T(8,128)(2,1)S(1)}, u32[]{:S(2)}, u32[]{:S(2)}) collective-permute-start(bf16[512,1408]{1,0:T(8,128)(2,1)S(1)} %bitcast.54), channel_id=1, source_target_pairs={{0,64},{64,0},{128,192},{192,128},{1,65},{65,1},{129,193},{193,129... | collective-permute-start | bytes 4325384 | tf_op jit(solution)/shard_map/ppermute | solution.py:17
  28.9 107.3 %collective-permute-start = (bf16[512,1408]{1,0:T(8,128)(2,1)}, bf16[512,1408]{1,0:T(8,128)(2,1)}, u32[]{:S(2)}, u32[]{:S(2)}) collective-permute-start(bf16[512,1408]{1,0:T(8,128)(2,1)} %bitcast.6), channel_id=1, source_target_pairs={{0,128},{64,192},{128,0},{192,64},{1,129},{65,193},{129,1},{193,65... | collective-permute-start | bytes 4325384 | tf_op jit(solution)/shard_map/ppermute | solution.py:16
  30.2 136.6 %collective-permute-start.6 = (bf16[1408,512]{1,0:T(8,128)(2,1)}, bf16[1408,512]{1,0:T(8,128)(2,1)}, u32[]{:S(2)}, u32[]{:S(2)}) collective-permute-start(bf16[1408,512]{1,0:T(8,128)(2,1)} %bitcast.8), channel_id=1, source_target_pairs={{0,128},{64,192},{128,0},{192,64},{1,129},{65,193},{129,1},{193,65... | collective-permute-start | bytes 4325384 | tf_op jit(solution)/shard_map/ppermute | solution.py:16
  87.4 82.9 %collective-permute-start.5 = (bf16[512,1408]{1,0:T(8,128)(2,1)}, bf16[512,1408]{1,0:T(8,128)(2,1)}, u32[]{:S(2)}, u32[]{:S(2)}) collective-permute-start(bf16[512,1408]{1,0:T(8,128)(2,1)} %collective-permute-done.3), channel_id=1, source_target_pairs={{0,64},{64,0},{128,192},{192,128},{1,65},{65,1},{129,193},{193,129... | collective-permute-start | bytes 4325384 | tf_op jit(solution)/shard_map/ppermute | solution.py:18
  87.4 93.1 %collective-permute-start.1 = (bf16[512,1408]{1,0:T(8,128)(2,1)}, bf16[512,1408]{1,0:T(8,128)(2,1)}, u32[]{:S(2)}, u32[]{:S(2)}) collective-permute-start(bf16[512,1408]{1,0:T(8,128)(2,1)} %bitcast.6), channel_id=1, source_target_pairs={{0,64},{64,0},{128,192},{192,128},{1,65},{65,1},{129,193},{193,129... | collective-permute-start | bytes 4325384 | tf_op jit(solution)/shard_map/ppermute | solution.py:17
  87.9 78.9 %copy-start.4 = (bf16[512,1408]{1,0:T(8,128)(2,1)}, bf16[512,1408]{1,0:T(8,128)(2,1)S(1)}, u32[]{:S(2)}) copy-start(bf16[512,1408]{1,0:T(8,128)(2,1)S(1)} %collective-permute-done.4) | copy-start | bytes 4325380
  88.0 92.6 %collective-permute-start.7 = (bf16[1408,512]{1,0:T(8,128)(2,1)}, bf16[1408,512]{1,0:T(8,128)(2,1)}, u32[]{:S(2)}, u32[]{:S(2)}) collective-permute-start(bf16[1408,512]{1,0:T(8,128)(2,1)} %bitcast.8), channel_id=1, source_target_pairs={{0,64},{64,0},{128,192},{192,128},{1,65},{65,1},{129,193},{193,129... | collective-permute-start | bytes 4325384 | tf_op jit(solution)/shard_map/ppermute | solution.py:17
  136.2 44.3 %collective-permute-start.2 = (bf16[512,1408]{1,0:T(8,128)(2,1)}, bf16[512,1408]{1,0:T(8,128)(2,1)}, u32[]{:S(2)}, u32[]{:S(2)}) collective-permute-start(bf16[512,1408]{1,0:T(8,128)(2,1)} %collective-permute-done), channel_id=1, source_target_pairs={{0,64},{64,0},{128,192},{192,128},{1,65},{65,1},{129,193},{193,129... | collective-permute-start | bytes 4325384 | tf_op jit(solution)/shard_map/ppermute | solution.py:18
  166.9 13.7 %collective-permute-start.8 = (bf16[1408,512]{1,0:T(8,128)(2,1)}, bf16[1408,512]{1,0:T(8,128)(2,1)}, u32[]{:S(2)}, u32[]{:S(2)}) collective-permute-start(bf16[1408,512]{1,0:T(8,128)(2,1)} %collective-permute-done.6), channel_id=1, source_target_pairs={{0,64},{64,0},{128,192},{192,128},{1,65},{65,1},{129,193},{193,129... | collective-permute-start | bytes 4325384 | tf_op jit(solution)/shard_map/ppermute | solution.py:18
  203.0 13.8 %copy-start = (s32[4]{0:T(128)S(1)}, s32[4]{0:T(128)}, u32[]{:S(2)}) copy-start(s32[4]{0:T(128)} %constant.37.clone) | copy-start | bytes 52
  203.0 14.4 %copy-start.2 = (f32[128,6]{0,1:T(8,128)S(1)}, f32[128,6]{0,1:T(8,128)}, u32[]{:S(2)}) copy-start(f32[128,6]{0,1:T(8,128)} %param.12) | copy-start | bytes 9220
  203.0 112.1 %all-to-all-start.1 = ((bf16[64,1,13,2048]{3,2,1,0:T(8,128)(2,1)}), bf16[64,1,13,2048]{3,2,1,0:T(8,128)(2,1)}, u32[]{:S(2)}, u32[]{:S(2)}) async-start(bf16[64,1,13,2048]{3,2,1,0:T(8,128)(2,1)} %bitcast.45), calls=%async_computation.1 | async-start | bytes 8388608 | tf_op jit(solution)/shard_map/all_to_all | solution.py:65
  318.5 1.8 copy-start.1

commit v2 on v1

--- a/solution.py
+++ b/solution.py
@@ -36,7 +36,8 @@
     slots = experts * cap
 
     wg, wu = _dp_gather((gate_weight[0], up_weight[0]), 0)
-    (wd,) = _dp_gather((down_weight[0],), 1)
+    down_shard = lax.optimization_barrier((down_weight[0], wg, wu))[0]
+    (wd,) = _dp_gather((down_shard,), 1)
 
     d = lax.axis_index("dp")
     offs = jnp.array(OFFS, jnp.int32)
@@ -52,9 +53,12 @@
 
     rows_j = jnp.arange(slots, dtype=jnp.int32)
     pick = jnp.any(flat[None, :, :] == rows_j[:, None, None], axis=2).astype(jnp.bfloat16)
-    tokens_rel = _blocks(tokens, src_blk)
-    send = jnp.dot(pick, tokens_rel, preferred_element_type=jnp.float32).astype(jnp.bfloat16)
-    received = lax.all_to_all(send.reshape(n_ep, 1, cap, width), "ep", 0, 0, tiled=True)
+    lanes = 128
+    sub = width // lanes
+    tokens_rel = _blocks(tokens, src_blk).reshape(tok_rows, sub, lanes)
+    send = jnp.einsum("st,trl->srl", pick, tokens_rel, preferred_element_type=jnp.float32)
+    send = send.astype(jnp.bfloat16).reshape(n_ep, cap * sub, lanes)
+    received = lax.all_to_all(send, "ep", 0, 0, tiled=True)
     received = received.reshape(slots, width)
 
     gate = jnp.dot(received, wg, preferred_element_type=jnp.float32)
@@ -62,16 +66,18 @@
     hidden = (jax.nn.silu(gate) * up).astype(jnp.bfloat16)
     expert_out = jnp.dot(hidden, wd, preferred_element_type=jnp.float32).astype(jnp.bfloat16)
 
-    returned = lax.all_to_all(expert_out.reshape(n_ep, 1, cap, width), "ep", 0, 0, tiled=True)
-    returned = returned.reshape(slots, width)
+    expert_out = expert_out.reshape(n_ep, cap * sub, lanes)
+    returned = lax.all_to_all(expert_out, "ep", 0, 0, tiled=True)
+    returned = returned.reshape(slots, sub, lanes)
 
     hit = flat[:, :, None] == rows_j[None, None, :]
     weights = jnp.sum(jnp.where(hit, gate_scales[:, :, None], 0.0), axis=1)
-    w_hi = weights.astype(jnp.bfloat16)
-    w_lo = (weights - w_hi.astype(jnp.float32)).astype(jnp.bfloat16)
-    mixed = jnp.dot(w_hi, returned, preferred_element_type=jnp.float32)
-    mixed = mixed + jnp.dot(w_lo, returned, preferred_element_type=jnp.float32)
-    return _blocks(mixed.astype(jnp.bfloat16), out_blk)
+    w_hi32 = lax.reduce_precision(weights, exponent_bits=8, mantissa_bits=7)
+    w_hi = w_hi32.astype(jnp.bfloat16)
+    w_lo = (weights - w_hi32).astype(jnp.bfloat16)
+    mixed = jnp.einsum("ts,srl->trl", w_hi, returned, preferred_element_type=jnp.float32)
+    mixed = mixed + jnp.einsum("ts,srl->trl", w_lo, returned, preferred_element_type=jnp.float32)
+    return _blocks(mixed.astype(jnp.bfloat16).reshape(tok_rows, width), out_blk)
 
 
 def solution(mesh):

time: 324 us -> 321 us (level)
  waiting for transfers between devices: 232 us -> 209 us
  other arithmetic: 5.08 us -> 23.8 us
    concatenate x0 -> x2, other arithmetic: none -> 18.7 us  [_dp_gather(): jnp.concatenate(parts, axis=axis)]
    all_to_all x2, waiting for transfers between devices: 96.6 us -> 79.8 us  [the longest x1 79.8 us: local(): returned = lax.all_to_all(expert_out, 'ep', 0, 0, tiled=True)]
    ppermute x3, waiting for transfers between devices: 135 us -> 129 us  [_dp_gather(): cross = lax.ppermute(ws, 'dp', _perm(n, 2))]
    reshape x3 -> x1, local copies, waits for them, and re-layouts: 11.3 us -> 6.53 us  [local(): expert_out = expert_out.reshape(n_ep, cap * sub, lanes)]
    convert_element_type x0 -> x1, local copies, waits for them, and re-layouts: none -> 4 us  [local(): send = send.astype(jnp.bfloat16).reshape(n_ep, cap * sub, lanes)]
  transfers between devices with their start and end apart: 11 -> 11, of which waited for: 4 -> 4; matrix products, arithmetic and copies ran while one was open for 5% -> 11% of each run, Pallas kernels for 0% -> 0%
where the time goes in v2:
time: 321 us
  waiting for transfers between devices  209 us (65%)
  matrix products  34.8 us (11%)
  starting transfers between devices  31.9 us (10%)
  other arithmetic  23.8 us (7%)
  local copies, waits for them, and re-layouts  20.7 us (6%)
    ppermute x3, waiting for transfers between devices, _dp_gather(): cross = lax.ppermute(ws, 'dp', _perm(n, 2))  129 us
    all_to_all x1, waiting for transfers between devices, local(): returned = lax.all_to_all(expert_out, 'ep', 0, 0, tiled=True)  79.8 us
    concatenate x2, other arithmetic, _dp_gather(): jnp.concatenate(parts, axis=axis)  18.7 us
    dot_general x1, matrix products, local(): jnp.dot(hidden, wd, preferred_element_type=jnp.float32).astype(jnp.bfloat16)  18.3 us
    all_to_all x1, starting transfers between devices, local(): received = lax.all_to_all(send, 'ep', 0, 0, tiled=True)  14.2 us
    all_to_all x1, starting transfers between devices, local(): returned = lax.all_to_all(expert_out, 'ep', 0, 0, tiled=True)  13.6 us
    dot_general x1, matrix products, local(): gate = jnp.dot(received, wg, preferred_element_type=jnp.float32)  10.3 us
    reshape x1, local copies, waits for them, and re-layouts, local(): expert_out = expert_out.reshape(n_ep, cap * sub, lanes)  6.53 us
  transfers between devices with their start and end apart: 11, of which 4 were waited for; matrix products, arithmetic and copies ran while one was open for 11% of the time, Pallas kernels for 0%

profile of v2, /device:TPU:38, one launch (start us, length us, event | category | flops | bytes accessed | tf_op | source)
XLA Modules:
  0.0 320.7 jit_solution(15477411390762931393)
XLA Ops:
  0.0 0.8 copy.33
  1.1 1.8 reduce-window.6
  2.9 0.3 slice_reduce_fusion
  3.2 0.8 select_reduce_fusion.1
  4.2 0.4 fusion.15
  4.7 0.7 compare_and_fusion.1
  5.3 1.3 copy.38
  6.9 0.6 gather_fusion.1
  7.9 1.1 convolution_convert_fusion
  8.9 4.0 %copy.42 = bf16[832,16,128]{2,1,0:T(8,128)(2,1)} copy(bf16[832,16,128]{2,0,1:T(8,128)(2,1)S(1)} %convolution_convert_fusion) | data formatting | bytes 6815744 | tf_op jit(solution)/shard_map/convert_element_type | solution.py:60
  12.9 14.2 %all-to-all-start = ((bf16[64,208,128]{2,1,0:T(8,128)(2,1)}), bf16[64,208,128]{2,1,0:T(8,128)(2,1)S(1)}, u32[]{:S(2)}, u32[]{:S(2)}) async-start(bf16[64,208,128]{2,1,0:T(8,128)(2,1)} %bitcast.49), calls=%async_computation | async-start | bytes 6815744 | tf_op jit(solution)/shard_map/all_to_all | solution.py:61
  27.1 0.8 collective-permute-start
  27.9 1.3 collective-permute-start.3
  29.2 60.3 %collective-permute-done = bf16[512,1408]{1,0:T(8,128)(2,1)S(1)} collective-permute-done((bf16[512,1408]{1,0:T(8,128)(2,1)}, bf16[512,1408]{1,0:T(8,128)(2,1)S(1)}, u32[]{:S(2)}, u32[]{:S(2)}) %collective-permute-start) | collective-permute-done | bytes 1441824 | tf_op jit(solution)/shard_map/ppermute | solution.py:16
  89.6 0.5 collective-permute-start.4
  90.1 36.4 %collective-permute-done.3 = bf16[512,1408]{1,0:T(8,128)(2,1)S(1)} collective-permute-done((bf16[512,1408]{1,0:T(8,128)(2,1)}, bf16[512,1408]{1,0:T(8,128)(2,1)S(1)}, u32[]{:S(2)}, u32[]{:S(2)}) %collective-permute-start.3) | collective-permute-done | bytes 1441824 | tf_op jit(solution)/shard_map/ppermute | solution.py:16
  126.4 5.2 %pad_maximum_fusion = bf16[2048,1408]{1,0:T(8,128)(2,1)} fusion(bf16[512,1408]{1,0:T(8,128)(2,1)S(1)} %collective-permute-done.2, bf16[512,1408]{1,0:T(8,128)(2,1)S(1)} %collective-permute-done.1, bf16[512,1408]{1,0:T(8,128)(2,1)S(1)} %collective-permute-done, bf16[512,1408]{1,0:T(8,128)(2,1)} %bitcast.58), kind=kLoop, calls=%fused_computation.3 | loop fusion | flops 23068672 | bytes 11534336 | tf_op jit(solution)/shard_map/concatenate | solution.py:19
  131.7 13.5 %pad_maximum_fusion.1 = bf16[2048,1408]{1,0:T(8,128)(2,1)} fusion(bf16[512,1408]{1,0:T(8,128)(2,1)S(1)} %collective-permute-done.5, bf16[512,1408]{1,0:T(8,128)(2,1)S(1)} %collective-permute-done.4, bf16[512,1408]{1,0:T(8,128)(2,1)S(1)} %collective-permute-done.3, bf16[512,1408]{1,0:T(8,128)(2,1)S(1)} %bitcast.61), kind=kLoop, calls=%fused_computation.4 | loop fusion | flops 23068672 | bytes 11534336 | tf_op jit(solution)/shard_map/concatenate | solution.py:19
  145.2 1.3 collective-permute-start.6
  146.7 32.7 %collective-permute-done.6 = bf16[1408,512]{1,0:T(8,128)(2,1)} collective-permute-done((bf16[1408,512]{1,0:T(8,128)(2,1)}, bf16[1408,512]{1,0:T(8,128)(2,1)}, u32[]{:S(2)}, u32[]{:S(2)}) %collective-permute-start.6) | collective-permute-done | bytes 1441824 | tf_op jit(solution)/shard_map/ppermute | solution.py:16
  179.5 3.0 reshape.84
  182.4 10.3 %fusion.38 = f32[832,1408]{1,0:T(8,128)} fusion(bf16[832,2048]{1,0:T(8,128)(2,1)} %reshape.84, bf16[2048,1408]{1,0:T(8,128)(2,1)} %pad_maximum_fusion), kind=kOutput, calls=%fused_computation.58 | convolution fusion | flops 4798283776 | bytes 13860864 | tf_op jit(solution)/shard_map/dot_general | solution.py:64
  192.8 18.3 %fusion.8 = bf16[832,2048]{1,0:T(8,128)(2,1)} fusion(bf16[1408,512]{1,0:T(8,128)(2,1)} %collective-permute-done.8, bf16[1408,512]{1,0:T(8,128)(2,1)} %collective-permute-done.7, bf16[1408,512]{1,0:T(8,128)(2,1)} %collective-permute-done.6, bf16[1408,512]{1,0:T(8,128)(2,1)} %bitcast.10, f32[832,1408]{1,0:T(8,128)} %fusion.38, ...), kind=kOutput, calls=%fused_computation.14 | convolution fusion | flops 9628368896 | bytes 23035904 | tf_op jit(solution)/shard_map/dot_general | solution.py:67
  211.0 6.5 %reshape.85 = bf16[64,208,128]{2,1,0:T(8,128)(2,1)} reshape(bf16[832,2048]{1,0:T(8,128)(2,1)} %fusion.8) | data formatting | bytes 6815744 | tf_op jit(solution)/shard_map/reshape | solution.py:69
  217.6 13.6 %all-to-all-start.1 = ((bf16[64,208,128]{2,1,0:T(8,128)(2,1)}), bf16[64,208,128]{2,1,0:T(8,128)(2,1)S(1)}, u32[]{:S(2)}, u32[]{:S(2)}) async-start(bf16[64,208,128]{2,1,0:T(8,128)(2,1)} %reshape.85), calls=%async_computation.1 | async-start | bytes 6815744 | tf_op jit(solution)/shard_map/all_to_all | solution.py:70
  231.2 0.6 gather_fusion
  231.8 1.1 select_reduce_fusion
  232.9 79.8 %all-to-all-done.1 = bf16[64,208,128]{2,1,0:T(8,128)(2,1)S(1)} async-done(((bf16[64,208,128]{2,1,0:T(8,128)(2,1)}), bf16[64,208,128]{2,1,0:T(8,128)(2,1)S(1)}, u32[]{:S(2)}, u32[]{:S(2)}) %all-to-all-start.1) | async-done | bytes 3407904 | tf_op jit(solution)/shard_map/all_to_all | solution.py:70
  312.7 2.7 fusion.11
  315.4 2.4 fusion.20
  317.8 1.7 gather_fusion.2
  319.7 1.0 copy.47
  (39 shorter events, 1.5 us)
Async XLA Ops:
  12.9 166.5 %all-to-all-start = ((bf16[64,208,128]{2,1,0:T(8,128)(2,1)}), bf16[64,208,128]{2,1,0:T(8,128)(2,1)S(1)}, u32[]{:S(2)}, u32[]{:S(2)}) async-start(bf16[64,208,128]{2,1,0:T(8,128)(2,1)} %bitcast.49), calls=%async_computation | async-start | bytes 6815744 | tf_op jit(solution)/shard_map/all_to_all | solution.py:61
  27.1 62.4 %collective-permute-start = (bf16[512,1408]{1,0:T(8,128)(2,1)}, bf16[512,1408]{1,0:T(8,128)(2,1)S(1)}, u32[]{:S(2)}, u32[]{:S(2)}) collective-permute-start(bf16[512,1408]{1,0:T(8,128)(2,1)} %bitcast.56), channel_id=1, source_target_pairs={{0,128},{64,192},{128,0},{192,64},{1,129},{65,193},{129,1},{193,65... | collective-permute-start | bytes 4325384 | tf_op jit(solution)/shard_map/ppermute | solution.py:16
  27.9 103.8 %copy-start.3 = (bf16[1,512,1408]{2,1,0:T(8,128)(2,1)S(1)}, bf16[1,512,1408]{2,1,0:T(8,128)(2,1)}, u32[]{:S(2)}) copy-start(bf16[1,512,1408]{2,1,0:T(8,128)(2,1)} %param.15) | copy-start | bytes 4325380
  27.9 98.5 %collective-permute-start.3 = (bf16[512,1408]{1,0:T(8,128)(2,1)}, bf16[512,1408]{1,0:T(8,128)(2,1)S(1)}, u32[]{:S(2)}, u32[]{:S(2)}) collective-permute-start(bf16[512,1408]{1,0:T(8,128)(2,1)} %bitcast.59), channel_id=1, source_target_pairs={{0,128},{64,192},{128,0},{192,64},{1,129},{65,193},{129,1},{193,65... | collective-permute-start | bytes 4325384 | tf_op jit(solution)/shard_map/ppermute | solution.py:16
  29.2 97.2 %collective-permute-start.1 = (bf16[512,1408]{1,0:T(8,128)(2,1)}, bf16[512,1408]{1,0:T(8,128)(2,1)S(1)}, u32[]{:S(2)}, u32[]{:S(2)}) collective-permute-start(bf16[512,1408]{1,0:T(8,128)(2,1)} %bitcast.57), channel_id=1, source_target_pairs={{0,64},{64,0},{128,192},{192,128},{1,65},{65,1},{129,193},{193,129... | collective-permute-start | bytes 4325384 | tf_op jit(solution)/shard_map/ppermute | solution.py:17
  89.5 36.9 %collective-permute-start.2 = (bf16[512,1408]{1,0:T(8,128)(2,1)S(1)}, bf16[512,1408]{1,0:T(8,128)(2,1)S(1)}, u32[]{:S(2)}, u32[]{:S(2)}) collective-permute-start(bf16[512,1408]{1,0:T(8,128)(2,1)S(1)} %collective-permute-done), channel_id=1, source_target_pairs={{0,64},{64,0},{128,192},{192,128},{1,65},{65,1},{129,193},{193,129... | collective-permute-start | bytes 4325384 | tf_op jit(solution)/shard_map/ppermute | solution.py:18
  89.6 42.1 %collective-permute-start.4 = (bf16[512,1408]{1,0:T(8,128)(2,1)}, bf16[512,1408]{1,0:T(8,128)(2,1)S(1)}, u32[]{:S(2)}, u32[]{:S(2)}) collective-permute-start(bf16[512,1408]{1,0:T(8,128)(2,1)} %bitcast.60), channel_id=1, source_target_pairs={{0,64},{64,0},{128,192},{192,128},{1,65},{65,1},{129,193},{193,129... | collective-permute-start | bytes 4325384 | tf_op jit(solution)/shard_map/ppermute | solution.py:17
  126.4 5.2 %collective-permute-start.5 = (bf16[512,1408]{1,0:T(8,128)(2,1)S(1)}, bf16[512,1408]{1,0:T(8,128)(2,1)S(1)}, u32[]{:S(2)}, u32[]{:S(2)}) collective-permute-start(bf16[512,1408]{1,0:T(8,128)(2,1)S(1)} %collective-permute-done.3), channel_id=1, source_target_pairs={{0,64},{64,0},{128,192},{192,128},{1,65},{65,1},{129,193},{193,129... | collective-permute-start | bytes 4325384 | tf_op jit(solution)/shard_map/ppermute | solution.py:18
  145.2 34.3 %collective-permute-start.6 = (bf16[1408,512]{1,0:T(8,128)(2,1)}, bf16[1408,512]{1,0:T(8,128)(2,1)}, u32[]{:S(2)}, u32[]{:S(2)}) collective-permute-start(bf16[1408,512]{1,0:T(8,128)(2,1)} %bitcast.10), channel_id=1, source_target_pairs={{0,128},{64,192},{128,0},{192,64},{1,129},{65,193},{129,1},{193,65... | collective-permute-start | bytes 4325384 | tf_op jit(solution)/shard_map/ppermute | solution.py:16
  146.5 46.2 %collective-permute-start.7 = (bf16[1408,512]{1,0:T(8,128)(2,1)}, bf16[1408,512]{1,0:T(8,128)(2,1)}, u32[]{:S(2)}, u32[]{:S(2)}) collective-permute-start(bf16[1408,512]{1,0:T(8,128)(2,1)} %bitcast.10), channel_id=1, source_target_pairs={{0,64},{64,0},{128,192},{192,128},{1,65},{65,1},{129,193},{193,129... | collective-permute-start | bytes 4325384 | tf_op jit(solution)/shard_map/ppermute | solution.py:17
  179.5 13.3 %collective-permute-start.8 = (bf16[1408,512]{1,0:T(8,128)(2,1)}, bf16[1408,512]{1,0:T(8,128)(2,1)}, u32[]{:S(2)}, u32[]{:S(2)}) collective-permute-start(bf16[1408,512]{1,0:T(8,128)(2,1)} %collective-permute-done.6), channel_id=1, source_target_pairs={{0,64},{64,0},{128,192},{192,128},{1,65},{65,1},{129,193},{193,129... | collective-permute-start | bytes 4325384 | tf_op jit(solution)/shard_map/ppermute | solution.py:18
  182.4 10.3 %copy-start.1 = (bf16[832,2048]{1,0:T(8,128)(2,1)S(1)}, bf16[832,2048]{1,0:T(8,128)(2,1)}, u32[]{:S(2)}) copy-start(bf16[832,2048]{1,0:T(8,128)(2,1)} %reshape.84) | copy-start | bytes 10223620
  217.6 13.6 %copy-start = (s32[4]{0:T(128)S(1)}, s32[4]{0:T(128)}, u32[]{:S(2)}) copy-start(s32[4]{0:T(128)} %constant.37.clone) | copy-start | bytes 52
  217.6 14.3 %copy-start.4 = (f32[128,6]{0,1:T(8,128)S(1)}, f32[128,6]{0,1:T(8,128)}, u32[]{:S(2)}) copy-start(f32[128,6]{0,1:T(8,128)} %param.12) | copy-start | bytes 9220
  217.6 95.1 %all-to-all-start.1 = ((bf16[64,208,128]{2,1,0:T(8,128)(2,1)}), bf16[64,208,128]{2,1,0:T(8,128)(2,1)S(1)}, u32[]{:S(2)}, u32[]{:S(2)}) async-start(bf16[64,208,128]{2,1,0:T(8,128)(2,1)} %reshape.85), calls=%async_computation.1 | async-start | bytes 6815744 | tf_op jit(solution)/shard_map/all_to_all | solution.py:70
  312.7 2.7 copy-start.2

commit v3 on v2

--- a/solution.py
+++ b/solution.py
@@ -11,12 +11,12 @@
     return [(i, i ^ m) for i in range(n)]
 
 
-def _dp_gather(ws, axis):
+def _dp_parts(w):
     n = lax.axis_size("dp")
-    cross = lax.ppermute(ws, "dp", _perm(n, 2))
-    near = lax.ppermute(ws, "dp", _perm(n, 1))
+    cross = lax.ppermute(w, "dp", _perm(n, 2))
+    near = lax.ppermute(w, "dp", _perm(n, 1))
     far = lax.ppermute(cross, "dp", _perm(n, 1))
-    return [jnp.concatenate(parts, axis=axis) for parts in zip(ws, cross, near, far)]
+    return [w, cross, near, far]
 
 
 def _blocks(x, idx):
@@ -35,9 +35,11 @@
     cap = C
     slots = experts * cap
 
-    wg, wu = _dp_gather((gate_weight[0], up_weight[0]), 0)
-    down_shard = lax.optimization_barrier((down_weight[0], wg, wu))[0]
-    (wd,) = _dp_gather((down_shard,), 1)
+    wg = _dp_parts(gate_weight[0])
+    up_shard = lax.optimization_barrier((up_weight[0], wg[1]))[0]
+    wu = _dp_parts(up_shard)
+    down_shard = lax.optimization_barrier((down_weight[0], wu[1]))[0]
+    wd = _dp_parts(down_shard)
 
     d = lax.axis_index("dp")
     offs = jnp.array(OFFS, jnp.int32)
@@ -61,10 +63,13 @@
     received = lax.all_to_all(send, "ep", 0, 0, tiled=True)
     received = received.reshape(slots, width)
 
-    gate = jnp.dot(received, wg, preferred_element_type=jnp.float32)
-    up = jnp.dot(received, wu, preferred_element_type=jnp.float32)
+    kb = width // n_dp
+    cols = [received[:, p * kb:(p + 1) * kb] for p in range(n_dp)]
+    gate = sum(jnp.dot(c, w, preferred_element_type=jnp.float32) for c, w in zip(cols, wg))
+    up = sum(jnp.dot(c, w, preferred_element_type=jnp.float32) for c, w in zip(cols, wu))
     hidden = (jax.nn.silu(gate) * up).astype(jnp.bfloat16)
-    expert_out = jnp.dot(hidden, wd, preferred_element_type=jnp.float32).astype(jnp.bfloat16)
+    outs = [jnp.dot(hidden, w, preferred_element_type=jnp.float32).astype(jnp.bfloat16) for w in wd]
+    expert_out = jnp.concatenate(outs, axis=1)
 
     expert_out = expert_out.reshape(n_ep, cap * sub, lanes)
     returned = lax.all_to_all(expert_out, "ep", 0, 0, tiled=True)

time: 321 us -> 306 us (0.953)
  matrix products: 34.8 us -> 59.7 us
  waiting for transfers between devices: 209 us -> 189 us
  other arithmetic: 23.8 us -> 5.53 us
    dot_general x2 -> x12, matrix products: 28.6 us -> 53.5 us  [the longest x8 41.3 us: local(): jnp.dot(c, w, preferred_element_type=jnp.float32)]
    ppermute x9, waiting for transfers between devices: 129 us -> 109 us  [the longest x3 109 us: _dp_parts(): cross = lax.ppermute(w, 'dp', _perm(n, 2))]
    concatenate x2 -> x1, other arithmetic: 18.7 us -> 0.44 us  [local(): expert_out = jnp.concatenate(outs, axis=1)]
    reshape x1, local copies, waits for them, and re-layouts: 6.53 us -> 3.03 us  [local(): expert_out = expert_out.reshape(n_ep, cap * sub, lanes)]
  transfers between devices with their start and end apart: 11 -> 11, of which waited for: 4 -> 4; matrix products, arithmetic and copies ran while one was open for 11% -> 19% of each run, Pallas kernels for 0% -> 0%
where the time goes in v3:
time: 306 us; the launch traced here: 305 us
  waiting for transfers between devices  189 us (62%)
  matrix products  59.7 us (20%)
  starting transfers between devices  31.4 us (10%)
  local copies, waits for them, and re-layouts  19.2 us (6%)
  other arithmetic  5.53 us (2%)
    ppermute x3, waiting for transfers between devices, _dp_parts(): cross = lax.ppermute(w, 'dp', _perm(n, 2))  109 us
    all_to_all x1, waiting for transfers between devices, local(): returned = lax.all_to_all(expert_out, 'ep', 0, 0, tiled=True)  79.8 us
    dot_general x8, matrix products, local(): jnp.dot(c, w, preferred_element_type=jnp.float32)  41.3 us
    all_to_all x1, starting transfers between devices, local(): received = lax.all_to_all(send, 'ep', 0, 0, tiled=True)  14.3 us
    all_to_all x1, starting transfers between devices, local(): returned = lax.all_to_all(expert_out, 'ep', 0, 0, tiled=True)  12.6 us
    dot_general x4, matrix products, local(): jnp.dot(hidden, w, preferred_element_type=jnp.float32).astype(jnp.bfloat16)  12.2 us
  transfers between devices with their start and end apart: 11, of which 4 were waited for; matrix products, arithmetic and copies ran while one was open for 19% of the time, Pallas kernels for 0%

profile of v3, /device:TPU:38, one launch (start us, length us, event | category | flops | bytes accessed | tf_op | source)
XLA Modules:
  0.0 305.4 jit_solution(7457390026089291994)
XLA Ops:
  1.1 1.8 reduce-window.6
  3.2 0.8 select_reduce_fusion.1
  5.3 1.3 copy.38
  7.9 1.1 convolution_convert_fusion
  8.9 4.0 %copy.42 = bf16[832,16,128]{2,1,0:T(8,128)(2,1)} copy(bf16[832,16,128]{2,0,1:T(8,128)(2,1)S(1)} %convolution_convert_fusion) | data formatting | bytes 6815744 | tf_op jit(solution)/shard_map/convert_element_type | solution.py:62
  12.9 14.3 %all-to-all-start = ((bf16[64,208,128]{2,1,0:T(8,128)(2,1)}), bf16[64,208,128]{2,1,0:T(8,128)(2,1)}, u32[]{:S(2)}, u32[]{:S(2)}) async-start(bf16[64,208,128]{2,1,0:T(8,128)(2,1)} %bitcast.7), calls=%async_computation | async-start | bytes 6815744 | tf_op jit(solution)/shard_map/all_to_all | solution.py:63
  28.0 61.3 %collective-permute-done = bf16[512,1408]{1,0:T(8,128)(2,1)} collective-permute-done((bf16[512,1408]{1,0:T(8,128)(2,1)}, bf16[512,1408]{1,0:T(8,128)(2,1)}, u32[]{:S(2)}, u32[]{:S(2)}) %collective-permute-start) | collective-permute-done | bytes 1441824 | tf_op jit(solution)/shard_map/ppermute | solution.py:16
  89.3 1.3 collective-permute-start.3
  91.2 36.7 %collective-permute-done.3 = bf16[512,1408]{1,0:T(8,128)(2,1)} collective-permute-done((bf16[512,1408]{1,0:T(8,128)(2,1)}, bf16[512,1408]{1,0:T(8,128)(2,1)}, u32[]{:S(2)}, u32[]{:S(2)}) %collective-permute-start.3) | collective-permute-done | bytes 1441824 | tf_op jit(solution)/shard_map/ppermute | solution.py:16
  127.9 1.3 collective-permute-start.6
  129.3 4.9 %reshape.84 = bf16[832,2048]{1,0:T(8,128)(2,1)S(1)} reshape(bf16[64,208,128]{2,1,0:T(8,128)(2,1)} %all-to-all-done) | data formatting | bytes 6815744 | tf_op jit(solution)/shard_map/reshape | solution.py:64
  134.2 2.8 fusion.22
  137.1 2.8 fusion.24
  139.9 5.0 %fusion.18 = f32[832,1408]{1,0:T(8,128)} fusion(bf16[512,1408]{1,0:T(8,128)(2,1)} %collective-permute-done.3, bf16[832,2048]{1,0:T(8,128)(2,1)S(1)} %reshape.84), kind=kOutput, calls=%fused_computation.27 | convolution fusion | flops 1199570944 | bytes 6979584 | tf_op jit(solution)/shard_map/dot_general | solution.py:69
  144.9 5.0 %fusion.20 = f32[832,1408]{1,0:T(8,128)} fusion(bf16[512,1408]{1,0:T(8,128)(2,1)} %collective-permute-done, bf16[832,2048]{1,0:T(8,128)(2,1)S(1)} %reshape.84), kind=kOutput, calls=%fused_computation.29 | convolution fusion | flops 1199570944 | bytes 6979584 | tf_op jit(solution)/shard_map/dot_general | solution.py:68
  150.4 11.4 %collective-permute-done.6 = bf16[1408,512]{1,0:T(8,128)(2,1)} collective-permute-done((bf16[1408,512]{1,0:T(8,128)(2,1)}, bf16[1408,512]{1,0:T(8,128)(2,1)}, u32[]{:S(2)}, u32[]{:S(2)}) %collective-permute-start.6) | collective-permute-done | bytes 1441824 | tf_op jit(solution)/shard_map/ppermute | solution.py:16
  161.8 5.1 %fusion.14 = f32[832,1408]{1,0:T(8,128)} fusion(bf16[512,1408]{1,0:T(8,128)(2,1)} %collective-permute-done.4, bf16[832,2048]{1,0:T(8,128)(2,1)S(1)} %reshape.84), kind=kOutput, calls=%fused_computation.23 | convolution fusion | flops 1199570944 | bytes 6979584 | tf_op jit(solution)/shard_map/dot_general | solution.py:69
  166.9 4.9 %fusion.12 = f32[832,1408]{1,0:T(8,128)} fusion(bf16[512,1408]{1,0:T(8,128)(2,1)} %collective-permute-done.2, bf16[832,2048]{1,0:T(8,128)(2,1)S(1)} %reshape.84), kind=kOutput, calls=%fused_computation.21 | convolution fusion | flops 1199570944 | bytes 6979584 | tf_op jit(solution)/shard_map/dot_general | solution.py:68
  171.8 5.0 %fusion.16 = f32[832,1408]{1,0:T(8,128)} fusion(bf16[512,1408]{1,0:T(8,128)(2,1)} %collective-permute-done.1, bf16[832,2048]{1,0:T(8,128)(2,1)S(1)} %reshape.84), kind=kOutput, calls=%fused_computation.25 | convolution fusion | flops 1199570944 | bytes 6979584 | tf_op jit(solution)/shard_map/dot_general | solution.py:68
  176.8 10.6 %multiply_convert_fusion = bf16[832,1408]{1,0:T(8,128)(2,1)} fusion(f32[832,1408]{1,0:T(8,128)} %fusion.14, f32[832,1408]{1,0:T(8,128)S(1)} %fusion.22, f32[832,1408]{1,0:T(8,128)} %fusion.18, f32[832,1408]{1,0:T(8,128)} %fusion.12, f32[832,1408]{1,0:T(8,128)} %fusion.16, f32[832,1408]{1,0:T(8,128)S(1)} %fusion.24, f32[832,1408]{1,0:T(8,128)} %fusion.20, ...), kind=kOutput, calls=%fused_computation.3 | convolution fusion | flops 1213628416 | bytes 37437440 | tf_op jit(solution)/shard_map/dot_general | solution.py:69
  187.4 3.7 %convolution_convert_fusion.4 = bf16[832,512]{1,0:T(8,128)(2,1)S(1)} fusion(bf16[832,1408]{1,0:T(8,128)(2,1)} %multiply_convert_fusion, bf16[1408,512]{1,0:T(8,128)(2,1)} %bitcast.10), kind=kOutput, calls=%fused_computation.17 | convolution fusion | flops 1199996928 | bytes 4636672 | tf_op jit(solution)/shard_map/dot_general | solution.py:71
  191.1 2.8 convolution_convert_fusion.3
  194.0 2.8 convolution_convert_fusion.2
  196.9 2.8 convolution_convert_fusion.1
  200.2 3.0 reshape.85
  203.2 12.6 %all-to-all-start.1 = ((bf16[64,208,128]{2,1,0:T(8,128)(2,1)}), bf16[64,208,128]{2,1,0:T(8,128)(2,1)S(1)}, u32[]{:S(2)}, u32[]{:S(2)}) async-start(bf16[64,208,128]{2,1,0:T(8,128)(2,1)} %reshape.85), calls=%async_computation.1 | async-start | bytes 6815744 | tf_op jit(solution)/shard_map/all_to_all | solution.py:75
  216.5 1.1 select_reduce_fusion
  217.6 79.8 %all-to-all-done.1 = bf16[64,208,128]{2,1,0:T(8,128)(2,1)S(1)} async-done(((bf16[64,208,128]{2,1,0:T(8,128)(2,1)}), bf16[64,208,128]{2,1,0:T(8,128)(2,1)S(1)}, u32[]{:S(2)}, u32[]{:S(2)}) %all-to-all-start.1) | async-done | bytes 3407904 | tf_op jit(solution)/shard_map/all_to_all | solution.py:75
  297.4 2.7 fusion
  300.1 2.4 fusion.8
  302.5 1.7 gather_fusion.2
  304.3 1.0 copy.47
  (46 shorter events, 6.9 us)
Async XLA Ops:
  12.9 116.4 %all-to-all-start = ((bf16[64,208,128]{2,1,0:T(8,128)(2,1)}), bf16[64,208,128]{2,1,0:T(8,128)(2,1)}, u32[]{:S(2)}, u32[]{:S(2)}) async-start(bf16[64,208,128]{2,1,0:T(8,128)(2,1)} %bitcast.7), calls=%async_computation | async-start | bytes 6815744 | tf_op jit(solution)/shard_map/all_to_all | solution.py:63
  27.3 62.1 %collective-permute-start = (bf16[512,1408]{1,0:T(8,128)(2,1)}, bf16[512,1408]{1,0:T(8,128)(2,1)}, u32[]{:S(2)}, u32[]{:S(2)}) collective-permute-start(bf16[512,1408]{1,0:T(8,128)(2,1)} %bitcast.8), channel_id=1, source_target_pairs={{0,128},{64,192},{128,0},{192,64},{1,129},{65,193},{129,1},{193,65... | collective-permute-start | bytes 4325384 | tf_op jit(solution)/shard_map/ppermute | solution.py:16
  89.3 38.6 %collective-permute-start.3 = (bf16[512,1408]{1,0:T(8,128)(2,1)}, bf16[512,1408]{1,0:T(8,128)(2,1)}, u32[]{:S(2)}, u32[]{:S(2)}) collective-permute-start(bf16[512,1408]{1,0:T(8,128)(2,1)} %bitcast.9), channel_id=1, source_target_pairs={{0,128},{64,192},{128,0},{192,64},{1,129},{65,193},{129,1},{193,65... | collective-permute-start | bytes 4325384 | tf_op jit(solution)/shard_map/ppermute | solution.py:16
  90.7 81.1 %collective-permute-start.1 = (bf16[512,1408]{1,0:T(8,128)(2,1)}, bf16[512,1408]{1,0:T(8,128)(2,1)}, u32[]{:S(2)}, u32[]{:S(2)}) collective-permute-start(bf16[512,1408]{1,0:T(8,128)(2,1)} %bitcast.8), channel_id=1, source_target_pairs={{0,64},{64,0},{128,192},{192,128},{1,65},{65,1},{129,193},{193,129... | collective-permute-start | bytes 4325384 | tf_op jit(solution)/shard_map/ppermute | solution.py:17
  90.7 59.2 %collective-permute-start.4 = (bf16[512,1408]{1,0:T(8,128)(2,1)}, bf16[512,1408]{1,0:T(8,128)(2,1)}, u32[]{:S(2)}, u32[]{:S(2)}) collective-permute-start(bf16[512,1408]{1,0:T(8,128)(2,1)} %bitcast.9), channel_id=1, source_target_pairs={{0,64},{64,0},{128,192},{192,128},{1,65},{65,1},{129,193},{193,129... | collective-permute-start | bytes 4325384 | tf_op jit(solution)/shard_map/ppermute | solution.py:17
  91.2 75.7 %collective-permute-start.2 = (bf16[512,1408]{1,0:T(8,128)(2,1)}, bf16[512,1408]{1,0:T(8,128)(2,1)}, u32[]{:S(2)}, u32[]{:S(2)}) collective-permute-start(bf16[512,1408]{1,0:T(8,128)(2,1)} %collective-permute-done), channel_id=1, source_target_pairs={{0,64},{64,0},{128,192},{192,128},{1,65},{65,1},{129,193},{193,129... | collective-permute-start | bytes 4325384 | tf_op jit(solution)/shard_map/ppermute | solution.py:18
  127.9 33.8 %collective-permute-start.6 = (bf16[1408,512]{1,0:T(8,128)(2,1)}, bf16[1408,512]{1,0:T(8,128)(2,1)}, u32[]{:S(2)}, u32[]{:S(2)}) collective-permute-start(bf16[1408,512]{1,0:T(8,128)(2,1)} %bitcast.10), channel_id=1, source_target_pairs={{0,128},{64,192},{128,0},{192,64},{1,129},{65,193},{129,1},{193,65... | collective-permute-start | bytes 4325384 | tf_op jit(solution)/shard_map/ppermute | solution.py:16
  129.3 47.6 %collective-permute-start.5 = (bf16[512,1408]{1,0:T(8,128)(2,1)}, bf16[512,1408]{1,0:T(8,128)(2,1)}, u32[]{:S(2)}, u32[]{:S(2)}) collective-permute-start(bf16[512,1408]{1,0:T(8,128)(2,1)} %collective-permute-done.3), channel_id=1, source_target_pairs={{0,64},{64,0},{128,192},{192,128},{1,65},{65,1},{129,193},{193,129... | collective-permute-start | bytes 4325384 | tf_op jit(solution)/shard_map/ppermute | solution.py:18
  149.9 44.1 %collective-permute-start.7 = (bf16[1408,512]{1,0:T(8,128)(2,1)}, bf16[1408,512]{1,0:T(8,128)(2,1)}, u32[]{:S(2)}, u32[]{:S(2)}) collective-permute-start(bf16[1408,512]{1,0:T(8,128)(2,1)} %bitcast.10), channel_id=1, source_target_pairs={{0,64},{64,0},{128,192},{192,128},{1,65},{65,1},{129,193},{193,129... | collective-permute-start | bytes 4325384 | tf_op jit(solution)/shard_map/ppermute | solution.py:17
  161.8 35.1 %collective-permute-start.8 = (bf16[1408,512]{1,0:T(8,128)(2,1)}, bf16[1408,512]{1,0:T(8,128)(2,1)}, u32[]{:S(2)}, u32[]{:S(2)}) collective-permute-start(bf16[1408,512]{1,0:T(8,128)(2,1)} %collective-permute-done.6), channel_id=1, source_target_pairs={{0,64},{64,0},{128,192},{192,128},{1,65},{65,1},{129,193},{193,129... | collective-permute-start | bytes 4325384 | tf_op jit(solution)/shard_map/ppermute | solution.py:18
  187.4 3.7 %copy-start.1 = (bf16[832,1408]{1,0:T(8,128)(2,1)S(1)}, bf16[832,1408]{1,0:T(8,128)(2,1)}, u32[]{:S(2)}) copy-start(bf16[832,1408]{1,0:T(8,128)(2,1)} %multiply_convert_fusion) | copy-start | bytes 7028740
  203.2 12.6 %copy-start = (s32[4]{0:T(128)S(1)}, s32[4]{0:T(128)}, u32[]{:S(2)}) copy-start(s32[4]{0:T(128)} %constant.37.clone) | copy-start | bytes 52
  203.2 13.3 %copy-start.3 = (f32[128,6]{0,1:T(8,128)S(1)}, f32[128,6]{0,1:T(8,128)}, u32[]{:S(2)}) copy-start(f32[128,6]{0,1:T(8,128)} %param.12) | copy-start | bytes 9220
  203.2 94.2 %all-to-all-start.1 = ((bf16[64,208,128]{2,1,0:T(8,128)(2,1)}), bf16[64,208,128]{2,1,0:T(8,128)(2,1)S(1)}, u32[]{:S(2)}, u32[]{:S(2)}) async-start(bf16[64,208,128]{2,1,0:T(8,128)(2,1)} %reshape.85), calls=%async_computation.1 | async-start | bytes 6815744 | tf_op jit(solution)/shard_map/all_to_all | solution.py:75
  297.4 2.7 copy-start.2

commit v4 on v3

--- a/solution.py
+++ b/solution.py
@@ -38,8 +38,11 @@
     wg = _dp_parts(gate_weight[0])
     up_shard = lax.optimization_barrier((up_weight[0], wg[1]))[0]
     wu = _dp_parts(up_shard)
-    down_shard = lax.optimization_barrier((down_weight[0], wu[1]))[0]
+    wg = jnp.concatenate(wg, axis=0)
+    down_shard = lax.optimization_barrier((down_weight[0], wu[1], wg))[0]
     wd = _dp_parts(down_shard)
+    wu = jnp.concatenate(wu, axis=0)
+    wd = jnp.concatenate(wd, axis=1)
 
     d = lax.axis_index("dp")
     offs = jnp.array(OFFS, jnp.int32)
@@ -63,13 +66,10 @@
     received = lax.all_to_all(send, "ep", 0, 0, tiled=True)
     received = received.reshape(slots, width)
 
-    kb = width // n_dp
-    cols = [received[:, p * kb:(p + 1) * kb] for p in range(n_dp)]
-    gate = sum(jnp.dot(c, w, preferred_element_type=jnp.float32) for c, w in zip(cols, wg))
-    up = sum(jnp.dot(c, w, preferred_element_type=jnp.float32) for c, w in zip(cols, wu))
+    gate = jnp.dot(received, wg, preferred_element_type=jnp.float32)
+    up = jnp.dot(received, wu, preferred_element_type=jnp.float32)
     hidden = (jax.nn.silu(gate) * up).astype(jnp.bfloat16)
-    outs = [jnp.dot(hidden, w, preferred_element_type=jnp.float32).astype(jnp.bfloat16) for w in wd]
-    expert_out = jnp.concatenate(outs, axis=1)
+    expert_out = jnp.dot(hidden, wd, preferred_element_type=jnp.float32).astype(jnp.bfloat16)
 
     expert_out = expert_out.reshape(n_ep, cap * sub, lanes)
     returned = lax.all_to_all(expert_out, "ep", 0, 0, tiled=True)

time: 306 us -> 303 us (level)
  matrix products: 59.7 us -> 33.8 us
  waiting for transfers between devices: 189 us -> 205 us
  other arithmetic: 5.53 us -> 10.3 us
    dot_general x12 -> x2, matrix products: 53.5 us -> 27.6 us  [the longest x1 17.3 us: local(): jnp.dot(hidden, wd, preferred_element_type=jnp.float32).astype(jnp.bfloat16)]
    ppermute x3, waiting for transfers between devices: 109 us -> 124 us  [_dp_parts(): cross = lax.ppermute(w, 'dp', _perm(n, 2))]
    concatenate x1, other arithmetic: 0.44 us -> 5.17 us  [local(): wg = jnp.concatenate(wg, axis=0)]
    reshape x1, local copies, waits for them, and re-layouts: 3.03 us -> 6.51 us  [local(): expert_out = expert_out.reshape(n_ep, cap * sub, lanes)]
  transfers between devices with their start and end apart: 11 -> 11, of which waited for: 4 -> 5; matrix products, arithmetic and copies ran while one was open for 19% -> 7% of each run, Pallas kernels for 0% -> 0%
where the time goes in v4:
time: 303 us
  waiting for transfers between devices  205 us (68%)
  matrix products  33.8 us (11%)
  starting transfers between devices  32.3 us (11%)
  local copies, waits for them, and re-layouts  20.7 us (7%)
  other arithmetic  10.3 us (3%)
    ppermute x3, waiting for transfers between devices, _dp_parts(): cross = lax.ppermute(w, 'dp', _perm(n, 2))  124 us
    all_to_all x1, waiting for transfers between devices, local(): returned = lax.all_to_all(expert_out, 'ep', 0, 0, tiled=True)  79.8 us
    dot_general x1, matrix products, local(): jnp.dot(hidden, wd, preferred_element_type=jnp.float32).astype(jnp.bfloat16)  17.3 us
    all_to_all x1, starting transfers between devices, local(): received = lax.all_to_all(send, 'ep', 0, 0, tiled=True)  14.2 us
    all_to_all x1, starting transfers between devices, local(): returned = lax.all_to_all(expert_out, 'ep', 0, 0, tiled=True)  14.1 us
    dot_general x1, matrix products, local(): gate = jnp.dot(received, wg, preferred_element_type=jnp.float32)  10.4 us
    reshape x1, local copies, waits for them, and re-layouts, local(): expert_out = expert_out.reshape(n_ep, cap * sub, lanes)  6.51 us
  transfers between devices with their start and end apart: 11, of which 5 were waited for; matrix products, arithmetic and copies ran while one was open for 7% of the time, Pallas kernels for 0%

profile of v4, /device:TPU:38, one launch (start us, length us, event | category | flops | bytes accessed | tf_op | source)
XLA Modules:
  0.0 302.7 jit_solution(7492687123004924571)
XLA Ops:
  0.0 0.8 copy.33
  1.1 1.8 reduce-window.6
  2.9 0.3 slice_reduce_fusion
  3.2 0.8 select_reduce_fusion.1
  4.2 0.4 fusion.23
  4.7 0.7 compare_and_fusion.1
  5.3 1.3 copy.38
  6.9 0.6 gather_fusion.1
  7.9 1.1 convolution_convert_fusion
  8.9 4.0 %copy.42 = bf16[832,16,128]{2,1,0:T(8,128)(2,1)} copy(bf16[832,16,128]{2,0,1:T(8,128)(2,1)S(1)} %convolution_convert_fusion) | data formatting | bytes 6815744 | tf_op jit(solution)/shard_map/convert_element_type | solution.py:65
  12.9 14.2 %all-to-all-start = ((bf16[64,208,128]{2,1,0:T(8,128)(2,1)}), bf16[64,208,128]{2,1,0:T(8,128)(2,1)S(1)}, u32[]{:S(2)}, u32[]{:S(2)}) async-start(bf16[64,208,128]{2,1,0:T(8,128)(2,1)} %bitcast.48), calls=%async_computation | async-start | bytes 6815744 | tf_op jit(solution)/shard_map/all_to_all | solution.py:66
  27.1 0.8 collective-permute-start
  27.9 60.9 %collective-permute-done = bf16[512,1408]{1,0:T(8,128)(2,1)S(1)} collective-permute-done((bf16[512,1408]{1,0:T(8,128)(2,1)}, bf16[512,1408]{1,0:T(8,128)(2,1)S(1)}, u32[]{:S(2)}, u32[]{:S(2)}) %collective-permute-start) | collective-permute-done | bytes 1441824 | tf_op jit(solution)/shard_map/ppermute | solution.py:16
  88.8 1.3 collective-permute-start.3
  90.1 1.9 collective-permute-done.2
  92.0 5.2 %pad_maximum_fusion = bf16[2048,1408]{1,0:T(8,128)(2,1)} fusion(bf16[512,1408]{1,0:T(8,128)(2,1)S(1)} %collective-permute-done.2, bf16[512,1408]{1,0:T(8,128)(2,1)S(1)} %collective-permute-done.1, bf16[512,1408]{1,0:T(8,128)(2,1)S(1)} %collective-permute-done, bf16[512,1408]{1,0:T(8,128)(2,1)} %bitcast.57), kind=kLoop, calls=%fused_computation.3 | loop fusion | flops 23068672 | bytes 11534336 | tf_op jit(solution)/shard_map/concatenate | solution.py:41
  97.2 30.8 %collective-permute-done.3 = bf16[512,1408]{1,0:T(8,128)(2,1)} collective-permute-done((bf16[512,1408]{1,0:T(8,128)(2,1)}, bf16[512,1408]{1,0:T(8,128)(2,1)}, u32[]{:S(2)}, u32[]{:S(2)}) %collective-permute-start.3) | collective-permute-done | bytes 1441824 | tf_op jit(solution)/shard_map/ppermute | solution.py:16
  127.9 1.3 collective-permute-start.6
  129.3 0.5 collective-permute-start.7
  129.8 32.1 %collective-permute-done.6 = bf16[1408,512]{1,0:T(8,128)(2,1)} collective-permute-done((bf16[1408,512]{1,0:T(8,128)(2,1)}, bf16[1408,512]{1,0:T(8,128)(2,1)}, u32[]{:S(2)}, u32[]{:S(2)}) %collective-permute-start.6) | collective-permute-done | bytes 1441824 | tf_op jit(solution)/shard_map/ppermute | solution.py:16
  161.9 3.0 reshape.84
  164.9 10.4 %fusion.49 = f32[832,1408]{1,0:T(8,128)} fusion(bf16[832,2048]{1,0:T(8,128)(2,1)} %reshape.84, bf16[2048,1408]{1,0:T(8,128)(2,1)} %pad_maximum_fusion), kind=kOutput, calls=%fused_computation.65 | convolution fusion | flops 4798283776 | bytes 13860864 | tf_op jit(solution)/shard_map/dot_general | solution.py:69
  175.3 17.3 %fusion.16 = bf16[832,2048]{1,0:T(8,128)(2,1)} fusion(bf16[1408,512]{1,0:T(8,128)(2,1)} %collective-permute-done.8, bf16[1408,512]{1,0:T(8,128)(2,1)} %collective-permute-done.7, bf16[1408,512]{1,0:T(8,128)(2,1)} %collective-permute-done.6, bf16[1408,512]{1,0:T(8,128)(2,1)} %bitcast.10, f32[832,1408]{1,0:T(8,128)} %fusion.49, ...), kind=kOutput, calls=%fused_computation.21 | convolution fusion | flops 9651437568 | bytes 23035904 | tf_op jit(solution)/shard_map/dot_general | solution.py:72
  192.6 6.5 %reshape.85 = bf16[64,208,128]{2,1,0:T(8,128)(2,1)} reshape(bf16[832,2048]{1,0:T(8,128)(2,1)} %fusion.16) | data formatting | bytes 6815744 | tf_op jit(solution)/shard_map/reshape | solution.py:74
  199.1 14.1 %all-to-all-start.1 = ((bf16[64,208,128]{2,1,0:T(8,128)(2,1)}), bf16[64,208,128]{2,1,0:T(8,128)(2,1)S(1)}, u32[]{:S(2)}, u32[]{:S(2)}) async-start(bf16[64,208,128]{2,1,0:T(8,128)(2,1)} %reshape.85), calls=%async_computation.1 | async-start | bytes 6815744 | tf_op jit(solution)/shard_map/all_to_all | solution.py:75
  213.2 0.6 gather_fusion
  213.9 1.1 select_reduce_fusion
  215.0 79.8 %all-to-all-done.1 = bf16[64,208,128]{2,1,0:T(8,128)(2,1)S(1)} async-done(((bf16[64,208,128]{2,1,0:T(8,128)(2,1)}), bf16[64,208,128]{2,1,0:T(8,128)(2,1)S(1)}, u32[]{:S(2)}, u32[]{:S(2)}) %all-to-all-start.1) | async-done | bytes 3407904 | tf_op jit(solution)/shard_map/all_to_all | solution.py:75
  294.7 2.7 fusion.19
  297.5 2.4 fusion.28
  299.9 1.7 gather_fusion.2
  301.7 1.0 copy.47
  (36 shorter events, 1.3 us)
Async XLA Ops:
  12.9 148.9 %all-to-all-start = ((bf16[64,208,128]{2,1,0:T(8,128)(2,1)}), bf16[64,208,128]{2,1,0:T(8,128)(2,1)S(1)}, u32[]{:S(2)}, u32[]{:S(2)}) async-start(bf16[64,208,128]{2,1,0:T(8,128)(2,1)} %bitcast.48), calls=%async_computation | async-start | bytes 6815744 | tf_op jit(solution)/shard_map/all_to_all | solution.py:66
  27.1 61.7 %collective-permute-start = (bf16[512,1408]{1,0:T(8,128)(2,1)}, bf16[512,1408]{1,0:T(8,128)(2,1)S(1)}, u32[]{:S(2)}, u32[]{:S(2)}) collective-permute-start(bf16[512,1408]{1,0:T(8,128)(2,1)} %bitcast.55), channel_id=1, source_target_pairs={{0,128},{64,192},{128,0},{192,64},{1,129},{65,193},{129,1},{193,65... | collective-permute-start | bytes 4325384 | tf_op jit(solution)/shard_map/ppermute | solution.py:16
  27.9 62.3 %collective-permute-start.1 = (bf16[512,1408]{1,0:T(8,128)(2,1)}, bf16[512,1408]{1,0:T(8,128)(2,1)S(1)}, u32[]{:S(2)}, u32[]{:S(2)}) collective-permute-start(bf16[512,1408]{1,0:T(8,128)(2,1)} %bitcast.56), channel_id=1, source_target_pairs={{0,64},{64,0},{128,192},{192,128},{1,65},{65,1},{129,193},{193,129... | collective-permute-start | bytes 4325384 | tf_op jit(solution)/shard_map/ppermute | solution.py:17
  88.8 3.2 %collective-permute-start.2 = (bf16[512,1408]{1,0:T(8,128)(2,1)S(1)}, bf16[512,1408]{1,0:T(8,128)(2,1)S(1)}, u32[]{:S(2)}, u32[]{:S(2)}) collective-permute-start(bf16[512,1408]{1,0:T(8,128)(2,1)S(1)} %collective-permute-done), channel_id=1, source_target_pairs={{0,64},{64,0},{128,192},{192,128},{1,65},{65,1},{129,193},{193,129... | collective-permute-start | bytes 4325384 | tf_op jit(solution)/shard_map/ppermute | solution.py:18
  88.8 39.2 %collective-permute-start.3 = (bf16[512,1408]{1,0:T(8,128)(2,1)}, bf16[512,1408]{1,0:T(8,128)(2,1)}, u32[]{:S(2)}, u32[]{:S(2)}) collective-permute-start(bf16[512,1408]{1,0:T(8,128)(2,1)} %bitcast.9), channel_id=1, source_target_pairs={{0,128},{64,192},{128,0},{192,64},{1,129},{65,193},{129,1},{193,65... | collective-permute-start | bytes 4325384 | tf_op jit(solution)/shard_map/ppermute | solution.py:16
  127.9 33.9 %collective-permute-start.6 = (bf16[1408,512]{1,0:T(8,128)(2,1)}, bf16[1408,512]{1,0:T(8,128)(2,1)}, u32[]{:S(2)}, u32[]{:S(2)}) collective-permute-start(bf16[1408,512]{1,0:T(8,128)(2,1)} %bitcast.10), channel_id=1, source_target_pairs={{0,128},{64,192},{128,0},{192,64},{1,129},{65,193},{129,1},{193,65... | collective-permute-start | bytes 4325384 | tf_op jit(solution)/shard_map/ppermute | solution.py:16
  129.3 46.0 %collective-permute-start.4 = (bf16[512,1408]{1,0:T(8,128)(2,1)}, bf16[512,1408]{1,0:T(8,128)(2,1)}, u32[]{:S(2)}, u32[]{:S(2)}) collective-permute-start(bf16[512,1408]{1,0:T(8,128)(2,1)} %bitcast.9), channel_id=1, source_target_pairs={{0,64},{64,0},{128,192},{192,128},{1,65},{65,1},{129,193},{193,129... | collective-permute-start | bytes 4325384 | tf_op jit(solution)/shard_map/ppermute | solution.py:17
  129.3 46.0 %collective-permute-start.7 = (bf16[1408,512]{1,0:T(8,128)(2,1)}, bf16[1408,512]{1,0:T(8,128)(2,1)}, u32[]{:S(2)}, u32[]{:S(2)}) collective-permute-start(bf16[1408,512]{1,0:T(8,128)(2,1)} %bitcast.10), channel_id=1, source_target_pairs={{0,64},{64,0},{128,192},{192,128},{1,65},{65,1},{129,193},{193,129... | collective-permute-start | bytes 4325384 | tf_op jit(solution)/shard_map/ppermute | solution.py:17
  129.8 45.5 %collective-permute-start.5 = (bf16[512,1408]{1,0:T(8,128)(2,1)}, bf16[512,1408]{1,0:T(8,128)(2,1)}, u32[]{:S(2)}, u32[]{:S(2)}) collective-permute-start(bf16[512,1408]{1,0:T(8,128)(2,1)} %collective-permute-done.3), channel_id=1, source_target_pairs={{0,64},{64,0},{128,192},{192,128},{1,65},{65,1},{129,193},{193,129... | collective-permute-start | bytes 4325384 | tf_op jit(solution)/shard_map/ppermute | solution.py:18
  161.9 13.4 %collective-permute-start.8 = (bf16[1408,512]{1,0:T(8,128)(2,1)}, bf16[1408,512]{1,0:T(8,128)(2,1)}, u32[]{:S(2)}, u32[]{:S(2)}) collective-permute-start(bf16[1408,512]{1,0:T(8,128)(2,1)} %collective-permute-done.6), channel_id=1, source_target_pairs={{0,64},{64,0},{128,192},{192,128},{1,65},{65,1},{129,193},{193,129... | collective-permute-start | bytes 4325384 | tf_op jit(solution)/shard_map/ppermute | solution.py:18
  164.9 10.4 %copy-start.1 = (bf16[832,2048]{1,0:T(8,128)(2,1)S(1)}, bf16[832,2048]{1,0:T(8,128)(2,1)}, u32[]{:S(2)}) copy-start(bf16[832,2048]{1,0:T(8,128)(2,1)} %reshape.84) | copy-start | bytes 10223620
  199.1 14.2 %copy-start = (s32[4]{0:T(128)S(1)}, s32[4]{0:T(128)}, u32[]{:S(2)}) copy-start(s32[4]{0:T(128)} %constant.37.clone) | copy-start | bytes 52
  199.1 14.8 %copy-start.3 = (f32[128,6]{0,1:T(8,128)S(1)}, f32[128,6]{0,1:T(8,128)}, u32[]{:S(2)}) copy-start(f32[128,6]{0,1:T(8,128)} %param.12) | copy-start | bytes 9220
  199.1 95.7 %all-to-all-start.1 = ((bf16[64,208,128]{2,1,0:T(8,128)(2,1)}), bf16[64,208,128]{2,1,0:T(8,128)(2,1)S(1)}, u32[]{:S(2)}, u32[]{:S(2)}) async-start(bf16[64,208,128]{2,1,0:T(8,128)(2,1)} %reshape.85), calls=%async_computation.1 | async-start | bytes 6815744 | tf_op jit(solution)/shard_map/all_to_all | solution.py:75
  294.7 2.7 copy-start.2

commit v5 on v4

--- a/solution.py
+++ b/solution.py
@@ -11,11 +11,12 @@
     return [(i, i ^ m) for i in range(n)]
 
 
-def _dp_parts(w):
+def _dp_parts(w, after=None):
     n = lax.axis_size("dp")
     cross = lax.ppermute(w, "dp", _perm(n, 2))
     near = lax.ppermute(w, "dp", _perm(n, 1))
-    far = lax.ppermute(cross, "dp", _perm(n, 1))
+    relay = cross if after is None else lax.optimization_barrier((cross, after()))[0]
+    far = lax.ppermute(relay, "dp", _perm(n, 1))
     return [w, cross, near, far]
 
 
@@ -38,11 +39,10 @@
     wg = _dp_parts(gate_weight[0])
     up_shard = lax.optimization_barrier((up_weight[0], wg[1]))[0]
     wu = _dp_parts(up_shard)
+    gate_cross = wg[1]
     wg = jnp.concatenate(wg, axis=0)
     down_shard = lax.optimization_barrier((down_weight[0], wu[1], wg))[0]
-    wd = _dp_parts(down_shard)
     wu = jnp.concatenate(wu, axis=0)
-    wd = jnp.concatenate(wd, axis=1)
 
     d = lax.axis_index("dp")
     offs = jnp.array(OFFS, jnp.int32)
@@ -63,10 +63,12 @@
     tokens_rel = _blocks(tokens, src_blk).reshape(tok_rows, sub, lanes)
     send = jnp.einsum("st,trl->srl", pick, tokens_rel, preferred_element_type=jnp.float32)
     send = send.astype(jnp.bfloat16).reshape(n_ep, cap * sub, lanes)
+    send = lax.optimization_barrier((send, gate_cross))[0]
     received = lax.all_to_all(send, "ep", 0, 0, tiled=True)
     received = received.reshape(slots, width)
 
     gate = jnp.dot(received, wg, preferred_element_type=jnp.float32)
+    wd = jnp.concatenate(_dp_parts(down_shard, after=lambda: gate), axis=1)
     up = jnp.dot(received, wu, preferred_element_type=jnp.float32)
     hidden = (jax.nn.silu(gate) * up).astype(jnp.bfloat16)
     expert_out = jnp.dot(hidden, wd, preferred_element_type=jnp.float32).astype(jnp.bfloat16)

time: 303 us -> 280 us (0.924)
  waiting for transfers between devices: 205 us -> 180 us
    ppermute x3, waiting for transfers between devices: 124 us -> 75.3 us  [_dp_parts(): cross = lax.ppermute(w, 'dp', _perm(n, 2))]
    all_to_all x1, waiting for transfers between devices: 0.01 us -> 17.4 us  [local(): received = lax.all_to_all(send, 'ep', 0, 0, tiled=True)]
    ppermute x3, waiting for transfers between devices: 1.87 us -> 5.61 us  [_dp_parts(): far = lax.ppermute(relay, 'dp', _perm(n, 1))]
  transfers between devices with their start and end apart: 11 -> 11, of which waited for: 5 -> 8; matrix products, arithmetic and copies ran while one was open for 7% -> 12% of each run, Pallas kernels for 0% -> 0%
where the time goes in v5:
time: 280 us
  waiting for transfers between devices  180 us (64%)
  matrix products  34 us (12%)
  starting transfers between devices  33.6 us (12%)
  local copies, waits for them, and re-layouts  21.9 us (8%)
  other arithmetic  10.1 us (4%)
    all_to_all x1, waiting for transfers between devices, local(): returned = lax.all_to_all(expert_out, 'ep', 0, 0, tiled=True)  79.4 us
    ppermute x3, waiting for transfers between devices, _dp_parts(): cross = lax.ppermute(w, 'dp', _perm(n, 2))  75.3 us
    dot_general x1, matrix products, local(): jnp.dot(hidden, wd, preferred_element_type=jnp.float32).astype(jnp.bfloat16)  17.4 us
    all_to_all x1, waiting for transfers between devices, local(): received = lax.all_to_all(send, 'ep', 0, 0, tiled=True)  17.4 us
    all_to_all x1, starting transfers between devices, local(): returned = lax.all_to_all(expert_out, 'ep', 0, 0, tiled=True)  14.7 us
    all_to_all x1, starting transfers between devices, local(): received = lax.all_to_all(send, 'ep', 0, 0, tiled=True)  14.2 us
    dot_general x1, matrix products, local(): gate = jnp.dot(received, wg, preferred_element_type=jnp.float32)  10.4 us
    reshape x1, local copies, waits for them, and re-layouts, local(): expert_out = expert_out.reshape(n_ep, cap * sub, lanes)  6.51 us
  transfers between devices with their start and end apart: 11, of which 8 were waited for; matrix products, arithmetic and copies ran while one was open for 12% of the time, Pallas kernels for 0%

profile of v5, /device:TPU:38, one launch (start us, length us, event | category | flops | bytes accessed | tf_op | source)
XLA Modules:
  0.0 279.8 jit_solution(2924708593024634667)
XLA Ops:
  0.0 1.6 collective-permute-start
  1.6 0.8 copy.33
  2.5 1.8 reduce-window.6
  4.8 0.8 select_reduce_fusion.1
  5.8 1.3 copy.38
  7.4 0.6 gather_fusion.1
  8.8 1.1 convolution_convert_fusion
  9.9 4.0 %copy.42 = bf16[832,16,128]{2,1,0:T(8,128)(2,1)} copy(bf16[832,16,128]{2,0,1:T(8,128)(2,1)S(1)} %convolution_convert_fusion) | data formatting | bytes 6815744 | tf_op jit(solution)/shard_map/convert_element_type | solution.py:65
  13.9 19.7 %collective-permute-done = bf16[512,1408]{1,0:T(8,128)(2,1)S(1)} collective-permute-done((bf16[512,1408]{1,0:T(8,128)(2,1)}, bf16[512,1408]{1,0:T(8,128)(2,1)S(1)}, u32[]{:S(2)}, u32[]{:S(2)}) %collective-permute-start) | collective-permute-done | bytes 1441824 | tf_op jit(solution)/shard_map/ppermute | solution.py:16
  33.5 1.1 copy-done.3
  34.6 14.2 %all-to-all-start = ((bf16[64,208,128]{2,1,0:T(8,128)(2,1)}), bf16[64,208,128]{2,1,0:T(8,128)(2,1)S(1)}, u32[]{:S(2)}, u32[]{:S(2)}) async-start(bf16[64,208,128]{2,1,0:T(8,128)(2,1)} %bitcast.48), calls=%async_computation | async-start | bytes 6815744 | tf_op jit(solution)/shard_map/all_to_all | solution.py:67
  49.4 0.7 collective-permute-start.3
  50.1 2.2 collective-permute-done.1
  52.4 2.1 collective-permute-done.2
  54.4 5.7 %pad_maximum_fusion = bf16[2048,1408]{1,0:T(8,128)(2,1)} fusion(bf16[512,1408]{1,0:T(8,128)(2,1)S(1)} %collective-permute-done.2, bf16[512,1408]{1,0:T(8,128)(2,1)S(1)} %collective-permute-done.1, bf16[512,1408]{1,0:T(8,128)(2,1)} %copy-done.3, bf16[512,1408]{1,0:T(8,128)(2,1)} %bitcast.57), kind=kLoop, calls=%fused_computation.3 | loop fusion | flops 23068672 | bytes 11534336 | tf_op jit(solution)/shard_map/concatenate | solution.py:43
  60.1 49.6 %collective-permute-done.3 = bf16[512,1408]{1,0:T(8,128)(2,1)} collective-permute-done((bf16[512,1408]{1,0:T(8,128)(2,1)}, bf16[512,1408]{1,0:T(8,128)(2,1)}, u32[]{:S(2)}, u32[]{:S(2)}) %collective-permute-start.3) | collective-permute-done | bytes 1441824 | tf_op jit(solution)/shard_map/ppermute | solution.py:16
  109.8 1.3 collective-permute-start.6
  111.6 17.4 %all-to-all-done = bf16[64,208,128]{2,1,0:T(8,128)(2,1)S(1)} async-done(((bf16[64,208,128]{2,1,0:T(8,128)(2,1)}), bf16[64,208,128]{2,1,0:T(8,128)(2,1)S(1)}, u32[]{:S(2)}, u32[]{:S(2)}) %all-to-all-start) | async-done | bytes 3407904 | tf_op jit(solution)/shard_map/all_to_all | solution.py:67
  129.0 3.0 %reshape.84 = bf16[832,2048]{1,0:T(8,128)(2,1)} reshape(bf16[64,208,128]{2,1,0:T(8,128)(2,1)S(1)} %all-to-all-done) | data formatting | bytes 6815744 | tf_op jit(solution)/shard_map/reshape | solution.py:68
  132.0 10.4 %fusion.49 = f32[832,1408]{1,0:T(8,128)} fusion(bf16[832,2048]{1,0:T(8,128)(2,1)} %reshape.84, bf16[2048,1408]{1,0:T(8,128)(2,1)} %pad_maximum_fusion), kind=kOutput, calls=%fused_computation.65 | convolution fusion | flops 4798283776 | bytes 13860864 | tf_op jit(solution)/shard_map/dot_general | solution.py:70
  142.3 6.0 %collective-permute-done.6 = bf16[1408,512]{1,0:T(8,128)(2,1)} collective-permute-done((bf16[1408,512]{1,0:T(8,128)(2,1)}, bf16[1408,512]{1,0:T(8,128)(2,1)}, u32[]{:S(2)}, u32[]{:S(2)}) %collective-permute-start.6) | collective-permute-done | bytes 1441824 | tf_op jit(solution)/shard_map/ppermute | solution.py:16
  148.4 3.5 %collective-permute-done.8 = bf16[1408,512]{1,0:T(8,128)(2,1)} collective-permute-done((bf16[1408,512]{1,0:T(8,128)(2,1)}, bf16[1408,512]{1,0:T(8,128)(2,1)}, u32[]{:S(2)}, u32[]{:S(2)}) %collective-permute-start.8) | collective-permute-done | bytes 1441824 | tf_op jit(solution)/shard_map/ppermute | solution.py:19
  152.0 17.4 %fusion.16 = bf16[832,2048]{1,0:T(8,128)(2,1)} fusion(bf16[1408,512]{1,0:T(8,128)(2,1)} %collective-permute-done.8, bf16[1408,512]{1,0:T(8,128)(2,1)} %collective-permute-done.7, bf16[1408,512]{1,0:T(8,128)(2,1)} %collective-permute-done.6, bf16[1408,512]{1,0:T(8,128)(2,1)} %bitcast.10, f32[832,1408]{1,0:T(8,128)} %fusion.49, ...), kind=kOutput, calls=%fused_computation.21 | convolution fusion | flops 9651437568 | bytes 23035904 | tf_op jit(solution)/shard_map/dot_general | solution.py:74
  169.4 6.5 %reshape.85 = bf16[64,208,128]{2,1,0:T(8,128)(2,1)} reshape(bf16[832,2048]{1,0:T(8,128)(2,1)} %fusion.16) | data formatting | bytes 6815744 | tf_op jit(solution)/shard_map/reshape | solution.py:76
  175.9 14.7 %all-to-all-start.1 = ((bf16[64,208,128]{2,1,0:T(8,128)(2,1)}), bf16[64,208,128]{2,1,0:T(8,128)(2,1)S(1)}, u32[]{:S(2)}, u32[]{:S(2)}) async-start(bf16[64,208,128]{2,1,0:T(8,128)(2,1)} %reshape.85), calls=%async_computation.1 | async-start | bytes 6815744 | tf_op jit(solution)/shard_map/all_to_all | solution.py:77
  190.6 0.6 gather_fusion
  191.3 1.1 select_reduce_fusion
  192.4 79.4 %all-to-all-done.1 = bf16[64,208,128]{2,1,0:T(8,128)(2,1)S(1)} async-done(((bf16[64,208,128]{2,1,0:T(8,128)(2,1)}), bf16[64,208,128]{2,1,0:T(8,128)(2,1)S(1)}, u32[]{:S(2)}, u32[]{:S(2)}) %all-to-all-start.1) | async-done | bytes 3407904 | tf_op jit(solution)/shard_map/all_to_all | solution.py:77
  271.8 2.7 fusion.19
  274.5 2.4 fusion.28
  277.0 1.7 gather_fusion.2
  278.8 1.0 copy.47
  (38 shorter events, 3.1 us)
Async XLA Ops:
  0.0 7.4 %copy-start = (s32[4]{0:T(128)S(1)}, s32[4]{0:T(128)}, u32[]{:S(2)}) copy-start(s32[4]{0:T(128)} %constant.37.clone) | copy-start | bytes 52
  0.0 33.5 %collective-permute-start = (bf16[512,1408]{1,0:T(8,128)(2,1)}, bf16[512,1408]{1,0:T(8,128)(2,1)S(1)}, u32[]{:S(2)}, u32[]{:S(2)}) collective-permute-start(bf16[512,1408]{1,0:T(8,128)(2,1)} %bitcast.55), channel_id=1, source_target_pairs={{0,128},{64,192},{128,0},{192,64},{1,129},{65,193},{129,1},{193,65... | collective-permute-start | bytes 4325384 | tf_op jit(solution)/shard_map/ppermute | solution.py:16
  33.5 1.1 copy-start.3
  34.6 94.3 %all-to-all-start = ((bf16[64,208,128]{2,1,0:T(8,128)(2,1)}), bf16[64,208,128]{2,1,0:T(8,128)(2,1)S(1)}, u32[]{:S(2)}, u32[]{:S(2)}) async-start(bf16[64,208,128]{2,1,0:T(8,128)(2,1)} %bitcast.48), calls=%async_computation | async-start | bytes 6815744 | tf_op jit(solution)/shard_map/all_to_all | solution.py:67
  48.8 3.5 %collective-permute-start.1 = (bf16[512,1408]{1,0:T(8,128)(2,1)}, bf16[512,1408]{1,0:T(8,128)(2,1)S(1)}, u32[]{:S(2)}, u32[]{:S(2)}) collective-permute-start(bf16[512,1408]{1,0:T(8,128)(2,1)} %bitcast.56), channel_id=1, source_target_pairs={{0,64},{64,0},{128,192},{192,128},{1,65},{65,1},{129,193},{193,129... | collective-permute-start | bytes 4325384 | tf_op jit(solution)/shard_map/ppermute | solution.py:17
  48.9 5.5 %collective-permute-start.2 = (bf16[512,1408]{1,0:T(8,128)(2,1)}, bf16[512,1408]{1,0:T(8,128)(2,1)S(1)}, u32[]{:S(2)}, u32[]{:S(2)}) collective-permute-start(bf16[512,1408]{1,0:T(8,128)(2,1)} %copy-done.3), channel_id=1, source_target_pairs={{0,64},{64,0},{128,192},{192,128},{1,65},{65,1},{129,193},{193,129... | collective-permute-start | bytes 4325384 | tf_op jit(solution)/shard_map/ppermute | solution.py:19
  49.4 60.3 %collective-permute-start.3 = (bf16[512,1408]{1,0:T(8,128)(2,1)}, bf16[512,1408]{1,0:T(8,128)(2,1)}, u32[]{:S(2)}, u32[]{:S(2)}) collective-permute-start(bf16[512,1408]{1,0:T(8,128)(2,1)} %bitcast.9), channel_id=1, source_target_pairs={{0,128},{64,192},{128,0},{192,64},{1,129},{65,193},{129,1},{193,65... | collective-permute-start | bytes 4325384 | tf_op jit(solution)/shard_map/ppermute | solution.py:16
  109.8 38.6 %collective-permute-start.6 = (bf16[1408,512]{1,0:T(8,128)(2,1)}, bf16[1408,512]{1,0:T(8,128)(2,1)}, u32[]{:S(2)}, u32[]{:S(2)}) collective-permute-start(bf16[1408,512]{1,0:T(8,128)(2,1)} %bitcast.10), channel_id=1, source_target_pairs={{0,128},{64,192},{128,0},{192,64},{1,129},{65,193},{129,1},{193,65... | collective-permute-start | bytes 4325384 | tf_op jit(solution)/shard_map/ppermute | solution.py:16
  111.1 37.3 %collective-permute-start.4 = (bf16[512,1408]{1,0:T(8,128)(2,1)}, bf16[512,1408]{1,0:T(8,128)(2,1)}, u32[]{:S(2)}, u32[]{:S(2)}) collective-permute-start(bf16[512,1408]{1,0:T(8,128)(2,1)} %bitcast.9), channel_id=1, source_target_pairs={{0,64},{64,0},{128,192},{192,128},{1,65},{65,1},{129,193},{193,129... | collective-permute-start | bytes 4325384 | tf_op jit(solution)/shard_map/ppermute | solution.py:17
  111.1 37.3 %collective-permute-start.7 = (bf16[1408,512]{1,0:T(8,128)(2,1)}, bf16[1408,512]{1,0:T(8,128)(2,1)}, u32[]{:S(2)}, u32[]{:S(2)}) collective-permute-start(bf16[1408,512]{1,0:T(8,128)(2,1)} %bitcast.10), channel_id=1, source_target_pairs={{0,64},{64,0},{128,192},{192,128},{1,65},{65,1},{129,193},{193,129... | collective-permute-start | bytes 4325384 | tf_op jit(solution)/shard_map/ppermute | solution.py:17
  111.6 36.8 %collective-permute-start.5 = (bf16[512,1408]{1,0:T(8,128)(2,1)}, bf16[512,1408]{1,0:T(8,128)(2,1)}, u32[]{:S(2)}, u32[]{:S(2)}) collective-permute-start(bf16[512,1408]{1,0:T(8,128)(2,1)} %collective-permute-done.3), channel_id=1, source_target_pairs={{0,64},{64,0},{128,192},{192,128},{1,65},{65,1},{129,193},{193,129... | collective-permute-start | bytes 4325384 | tf_op jit(solution)/shard_map/ppermute | solution.py:19
  132.0 20.0 %copy-start.1 = (bf16[832,2048]{1,0:T(8,128)(2,1)S(1)}, bf16[832,2048]{1,0:T(8,128)(2,1)}, u32[]{:S(2)}) copy-start(bf16[832,2048]{1,0:T(8,128)(2,1)} %reshape.84) | copy-start | bytes 10223620
  148.4 3.6 %collective-permute-start.8 = (bf16[1408,512]{1,0:T(8,128)(2,1)}, bf16[1408,512]{1,0:T(8,128)(2,1)}, u32[]{:S(2)}, u32[]{:S(2)}) collective-permute-start(bf16[1408,512]{1,0:T(8,128)(2,1)} %collective-permute-done.6), channel_id=1, source_target_pairs={{0,64},{64,0},{128,192},{192,128},{1,65},{65,1},{129,193},{193,129... | collective-permute-start | bytes 4325384 | tf_op jit(solution)/shard_map/ppermute | solution.py:19
  175.9 15.4 %copy-start.4 = (f32[128,6]{0,1:T(8,128)S(1)}, f32[128,6]{0,1:T(8,128)}, u32[]{:S(2)}) copy-start(f32[128,6]{0,1:T(8,128)} %param.12) | copy-start | bytes 9220
  175.9 95.9 %all-to-all-start.1 = ((bf16[64,208,128]{2,1,0:T(8,128)(2,1)}), bf16[64,208,128]{2,1,0:T(8,128)(2,1)S(1)}, u32[]{:S(2)}, u32[]{:S(2)}) async-start(bf16[64,208,128]{2,1,0:T(8,128)(2,1)} %reshape.85), calls=%async_computation.1 | async-start | bytes 6815744 | tf_op jit(solution)/shard_map/all_to_all | solution.py:77
  271.8 2.7 copy-start.2

commit v6 on v5

--- a/solution.py
+++ b/solution.py
@@ -68,9 +68,9 @@
     received = received.reshape(slots, width)
 
     gate = jnp.dot(received, wg, preferred_element_type=jnp.float32)
-    wd = jnp.concatenate(_dp_parts(down_shard, after=lambda: gate), axis=1)
     up = jnp.dot(received, wu, preferred_element_type=jnp.float32)
     hidden = (jax.nn.silu(gate) * up).astype(jnp.bfloat16)
+    wd = jnp.concatenate(_dp_parts(down_shard, after=lambda: hidden), axis=1)
     expert_out = jnp.dot(hidden, wd, preferred_element_type=jnp.float32).astype(jnp.bfloat16)
 
     expert_out = expert_out.reshape(n_ep, cap * sub, lanes)
@@ -82,8 +82,9 @@
     w_hi32 = lax.reduce_precision(weights, exponent_bits=8, mantissa_bits=7)
     w_hi = w_hi32.astype(jnp.bfloat16)
     w_lo = (weights - w_hi32).astype(jnp.bfloat16)
-    mixed = jnp.einsum("ts,srl->trl", w_hi, returned, preferred_element_type=jnp.float32)
-    mixed = mixed + jnp.einsum("ts,srl->trl", w_lo, returned, preferred_element_type=jnp.float32)
+    both = jnp.einsum("ts,srl->trl", jnp.concatenate([w_hi, w_lo], axis=0), returned,
+                      preferred_element_type=jnp.float32)
+    mixed = both[:tok_rows] + both[tok_rows:]
     return _blocks(mixed.astype(jnp.bfloat16).reshape(tok_rows, width), out_blk)
 
 

time: 280 us -> 269 us (0.961)
  matrix products: 34 us -> 28.8 us
  local copies, waits for them, and re-layouts: 21.9 us -> 17.4 us
  waiting for transfers between devices: 180 us -> 177 us
    dot_general x1, matrix products: 17.4 us -> 7.66 us  [local(): jnp.dot(hidden, wd, preferred_element_type=jnp.float32).astype(jnp.bfloat16)]
    ppermute x3, waiting for transfers between devices: 75.3 us -> 82.1 us  [_dp_parts(): cross = lax.ppermute(w, 'dp', _perm(n, 2))]
    all_to_all x1, waiting for transfers between devices: 17.4 us -> 11.9 us  [local(): received = lax.all_to_all(send, 'ep', 0, 0, tiled=True)]
    dot_general x2, matrix products: 5.14 us -> 10.5 us  [the longest x1 7.72 us: local(): up = jnp.dot(received, wu, preferred_element_type=jnp.float32)]
    reshape x1, local copies, waits for them, and re-layouts: 6.51 us -> 3.02 us  [local(): expert_out = expert_out.reshape(n_ep, cap * sub, lanes)]
  transfers between devices with their start and end apart: 11 -> 11, of which waited for: 8 -> 6; matrix products, arithmetic and copies ran while one was open for 12% -> 15% of each run, Pallas kernels for 0% -> 0%
where the time goes in v6:
time: 269 us
  waiting for transfers between devices  177 us (66%)
  starting transfers between devices  35.3 us (13%)
  matrix products  28.8 us (11%)
  local copies, waits for them, and re-layouts  17.4 us (6%)
  other arithmetic  10.3 us (4%)
    ppermute x3, waiting for transfers between devices, _dp_parts(): cross = lax.ppermute(w, 'dp', _perm(n, 2))  82.1 us
    all_to_all x1, waiting for transfers between devices, local(): returned = lax.all_to_all(expert_out, 'ep', 0, 0, tiled=True)  79.4 us
    all_to_all x1, starting transfers between devices, local(): returned = lax.all_to_all(expert_out, 'ep', 0, 0, tiled=True)  16.6 us
    all_to_all x1, starting transfers between devices, local(): received = lax.all_to_all(send, 'ep', 0, 0, tiled=True)  14.2 us
    all_to_all x1, waiting for transfers between devices, local(): received = lax.all_to_all(send, 'ep', 0, 0, tiled=True)  11.9 us
    dot_general x1, matrix products, local(): gate = jnp.dot(received, wg, preferred_element_type=jnp.float32)  9.53 us
    dot_general x1, matrix products, local(): up = jnp.dot(received, wu, preferred_element_type=jnp.float32)  7.72 us
    dot_general x1, matrix products, local(): jnp.dot(hidden, wd, preferred_element_type=jnp.float32).astype(jnp.bfloat16)  7.66 us
  transfers between devices with their start and end apart: 11, of which 6 were waited for; matrix products, arithmetic and copies ran while one was open for 15% of the time, Pallas kernels for 0%

profile of v6, /device:TPU:38, one launch (start us, length us, event | category | flops | bytes accessed | tf_op | source)
XLA Modules:
  0.0 268.7 jit_solution(18389981323042784542)
XLA Ops:
  0.0 1.6 collective-permute-start
  1.6 0.8 copy.31
  2.5 1.8 reduce-window.6
  4.8 0.8 select_reduce_fusion.1
  5.8 1.3 copy.36
  7.4 0.6 gather_fusion.1
  8.4 0.4 fusion.21
  8.8 1.1 convolution_convert_fusion
  9.9 4.0 %copy.40 = bf16[832,16,128]{2,1,0:T(8,128)(2,1)} copy(bf16[832,16,128]{2,0,1:T(8,128)(2,1)S(1)} %convolution_convert_fusion) | data formatting | bytes 6815744 | tf_op jit(solution)/shard_map/convert_element_type | solution.py:65
  13.9 19.7 %collective-permute-done = bf16[512,1408]{1,0:T(8,128)(2,1)S(1)} collective-permute-done((bf16[512,1408]{1,0:T(8,128)(2,1)}, bf16[512,1408]{1,0:T(8,128)(2,1)S(1)}, u32[]{:S(2)}, u32[]{:S(2)}) %collective-permute-start) | collective-permute-done | bytes 1441824 | tf_op jit(solution)/shard_map/ppermute | solution.py:16
  33.5 1.1 copy-done.2
  34.6 14.2 %all-to-all-start = ((bf16[64,208,128]{2,1,0:T(8,128)(2,1)}), bf16[64,208,128]{2,1,0:T(8,128)(2,1)S(1)}, u32[]{:S(2)}, u32[]{:S(2)}) async-start(bf16[64,208,128]{2,1,0:T(8,128)(2,1)} %bitcast.46), calls=%async_computation | async-start | bytes 6815744 | tf_op jit(solution)/shard_map/all_to_all | solution.py:67
  48.8 0.8 collective-permute-start.3
  49.6 0.5 collective-permute-start.2
  50.1 59.6 %collective-permute-done.3 = bf16[512,1408]{1,0:T(8,128)(2,1)} collective-permute-done((bf16[512,1408]{1,0:T(8,128)(2,1)}, bf16[512,1408]{1,0:T(8,128)(2,1)}, u32[]{:S(2)}, u32[]{:S(2)}) %collective-permute-start.3) | collective-permute-done | bytes 1441824 | tf_op jit(solution)/shard_map/ppermute | solution.py:16
  109.8 5.8 %pad_maximum_fusion = bf16[2048,1408]{1,0:T(8,128)(2,1)} fusion(bf16[512,1408]{1,0:T(8,128)(2,1)S(1)} %collective-permute-done.2, bf16[512,1408]{1,0:T(8,128)(2,1)S(1)} %collective-permute-done.1, bf16[512,1408]{1,0:T(8,128)(2,1)} %copy-done.2, bf16[512,1408]{1,0:T(8,128)(2,1)} %bitcast.54), kind=kLoop, calls=%fused_computation.3 | loop fusion | flops 23068672 | bytes 11534336 | tf_op jit(solution)/shard_map/concatenate | solution.py:43
  115.5 1.3 collective-permute-start.6
  117.1 11.9 %all-to-all-done = bf16[64,208,128]{2,1,0:T(8,128)(2,1)S(1)} async-done(((bf16[64,208,128]{2,1,0:T(8,128)(2,1)}), bf16[64,208,128]{2,1,0:T(8,128)(2,1)S(1)}, u32[]{:S(2)}, u32[]{:S(2)}) %all-to-all-start) | async-done | bytes 3407904 | tf_op jit(solution)/shard_map/all_to_all | solution.py:67
  129.0 3.0 %reshape.84 = bf16[832,2048]{1,0:T(8,128)(2,1)} reshape(bf16[64,208,128]{2,1,0:T(8,128)(2,1)S(1)} %all-to-all-done) | data formatting | bytes 6815744 | tf_op jit(solution)/shard_map/reshape | solution.py:68
  132.0 9.5 %fusion.37 = f32[832,1408]{1,0:T(8,128)S(1)} fusion(bf16[832,2048]{1,0:T(8,128)(2,1)} %reshape.84, bf16[2048,1408]{1,0:T(8,128)(2,1)} %pad_maximum_fusion), kind=kOutput, calls=%fused_computation.63 | convolution fusion | flops 4798283776 | bytes 13860864 | tf_op jit(solution)/shard_map/dot_general | solution.py:70
  141.5 7.7 %multiply_convert_fusion = bf16[832,1408]{1,0:T(8,128)(2,1)S(1)} fusion(f32[832,1408]{1,0:T(8,128)S(1)} %fusion.37, bf16[832,2048]{1,0:T(8,128)(2,1)S(1)} %copy-done.1, bf16[512,1408]{1,0:T(8,128)(2,1)} %collective-permute-done.5, bf16[512,1408]{1,0:T(8,128)(2,1)} %collective-permute-done.4, bf16[512,1408]{1,0:T(8,128)(2,1)} %collective-permute-done.3, ...), kind=kOutput, calls=%fused_computation.20 | convolution fusion | flops 4828381184 | bytes 16203776 | tf_op jit(solution)/shard_map/dot_general | solution.py:71
  149.3 2.8 %collective-permute-done.6 = bf16[1408,512]{1,0:T(8,128)(2,1)} collective-permute-done((bf16[1408,512]{1,0:T(8,128)(2,1)}, bf16[1408,512]{1,0:T(8,128)(2,1)}, u32[]{:S(2)}, u32[]{:S(2)}) %collective-permute-start.6) | collective-permute-done | bytes 1441824 | tf_op jit(solution)/shard_map/ppermute | solution.py:16
  152.1 3.4 %collective-permute-done.8 = bf16[1408,512]{1,0:T(8,128)(2,1)S(1)} collective-permute-done((bf16[1408,512]{1,0:T(8,128)(2,1)}, bf16[1408,512]{1,0:T(8,128)(2,1)S(1)}, u32[]{:S(2)}, u32[]{:S(2)}) %collective-permute-start.8) | collective-permute-done | bytes 1441824 | tf_op jit(solution)/shard_map/ppermute | solution.py:19
  155.5 7.7 %fusion.16 = bf16[832,2048]{1,0:T(8,128)(2,1)S(1)} fusion(bf16[832,1408]{1,0:T(8,128)(2,1)S(1)} %multiply_convert_fusion, bf16[1408,512]{1,0:T(8,128)(2,1)S(1)} %collective-permute-done.8, bf16[1408,512]{1,0:T(8,128)(2,1)} %collective-permute-done.7, bf16[1408,512]{1,0:T(8,128)(2,1)} %collective-permute-done.6, bf16[1408,512]{1,0:T(8,128)(2,1)} %bitcast.10), kind=kOutput, calls=%fused_computation.21 | convolution fusion | flops 4823056384 | bytes 11517952 | tf_op jit(solution)/shard_map/dot_general | solution.py:74
  163.1 3.0 %reshape.85 = bf16[64,208,128]{2,1,0:T(8,128)(2,1)} reshape(bf16[832,2048]{1,0:T(8,128)(2,1)S(1)} %fusion.16) | data formatting | bytes 6815744 | tf_op jit(solution)/shard_map/reshape | solution.py:76
  166.2 16.6 %all-to-all-start.1 = ((bf16[64,208,128]{2,1,0:T(8,128)(2,1)}), bf16[64,208,128]{2,1,0:T(8,128)(2,1)S(1)}, u32[]{:S(2)}, u32[]{:S(2)}) async-start(bf16[64,208,128]{2,1,0:T(8,128)(2,1)} %reshape.85), calls=%async_computation.1 | async-start | bytes 6815744 | tf_op jit(solution)/shard_map/all_to_all | solution.py:77
  182.8 0.6 gather_fusion
  183.8 0.8 reduce-precision_convert_fusion
  184.7 79.4 %all-to-all-done.1 = bf16[64,208,128]{2,1,0:T(8,128)(2,1)S(1)} async-done(((bf16[64,208,128]{2,1,0:T(8,128)(2,1)}), bf16[64,208,128]{2,1,0:T(8,128)(2,1)S(1)}, u32[]{:S(2)}, u32[]{:S(2)}) %all-to-all-start.1) | async-done | bytes 3407904 | tf_op jit(solution)/shard_map/all_to_all | solution.py:77
  264.0 2.8 %fusion.19 = f32[256,16,128]{0,2,1:T(8,128)S(1)} fusion(bf16[832,16,128]{2,1,0:T(8,128)(2,1)S(1)} %bitcast.47, bf16[128,832]{0,1:T(8,128)(2,1)} %get-tuple-element.21, bf16[128,832]{0,1:T(8,128)(2,1)} %get-tuple-element.20), kind=kOutput, calls=%fused_computation.22 | convolution fusion | flops 873267200 | bytes 5931008 | tf_op jit(solution)/shard_map/ts,srl->trl/dot_general | solution.py:85
  266.9 0.6 gather_fusion.2
  267.7 1.0 copy.44
  (40 shorter events, 2.3 us)
Async XLA Ops:
  0.0 7.4 %copy-start = (s32[4]{0:T(128)S(1)}, s32[4]{0:T(128)}, u32[]{:S(2)}) copy-start(s32[4]{0:T(128)} %constant.37.clone) | copy-start | bytes 52
  0.0 33.5 %collective-permute-start = (bf16[512,1408]{1,0:T(8,128)(2,1)}, bf16[512,1408]{1,0:T(8,128)(2,1)S(1)}, u32[]{:S(2)}, u32[]{:S(2)}) collective-permute-start(bf16[512,1408]{1,0:T(8,128)(2,1)} %bitcast.52), channel_id=1, source_target_pairs={{0,128},{64,192},{128,0},{192,64},{1,129},{65,193},{129,1},{193,65... | collective-permute-start | bytes 4325384 | tf_op jit(solution)/shard_map/ppermute | solution.py:16
  33.5 1.1 copy-start.2
  34.6 94.3 %all-to-all-start = ((bf16[64,208,128]{2,1,0:T(8,128)(2,1)}), bf16[64,208,128]{2,1,0:T(8,128)(2,1)S(1)}, u32[]{:S(2)}, u32[]{:S(2)}) async-start(bf16[64,208,128]{2,1,0:T(8,128)(2,1)} %bitcast.46), calls=%async_computation | async-start | bytes 6815744 | tf_op jit(solution)/shard_map/all_to_all | solution.py:67
  48.8 60.9 %collective-permute-start.3 = (bf16[512,1408]{1,0:T(8,128)(2,1)}, bf16[512,1408]{1,0:T(8,128)(2,1)}, u32[]{:S(2)}, u32[]{:S(2)}) collective-permute-start(bf16[512,1408]{1,0:T(8,128)(2,1)} %bitcast.56), channel_id=1, source_target_pairs={{0,128},{64,192},{128,0},{192,64},{1,129},{65,193},{129,1},{193,65... | collective-permute-start | bytes 4325384 | tf_op jit(solution)/shard_map/ppermute | solution.py:16
  49.6 60.2 %collective-permute-start.1 = (bf16[512,1408]{1,0:T(8,128)(2,1)}, bf16[512,1408]{1,0:T(8,128)(2,1)S(1)}, u32[]{:S(2)}, u32[]{:S(2)}) collective-permute-start(bf16[512,1408]{1,0:T(8,128)(2,1)} %bitcast.53), channel_id=1, source_target_pairs={{0,64},{64,0},{128,192},{192,128},{1,65},{65,1},{129,193},{193,129... | collective-permute-start | bytes 4325384 | tf_op jit(solution)/shard_map/ppermute | solution.py:17
  49.6 60.2 %collective-permute-start.2 = (bf16[512,1408]{1,0:T(8,128)(2,1)}, bf16[512,1408]{1,0:T(8,128)(2,1)S(1)}, u32[]{:S(2)}, u32[]{:S(2)}) collective-permute-start(bf16[512,1408]{1,0:T(8,128)(2,1)} %copy-done.2), channel_id=1, source_target_pairs={{0,64},{64,0},{128,192},{192,128},{1,65},{65,1},{129,193},{193,129... | collective-permute-start | bytes 4325384 | tf_op jit(solution)/shard_map/ppermute | solution.py:19
  50.1 91.4 %collective-permute-start.4 = (bf16[512,1408]{1,0:T(8,128)(2,1)}, bf16[512,1408]{1,0:T(8,128)(2,1)}, u32[]{:S(2)}, u32[]{:S(2)}) collective-permute-start(bf16[512,1408]{1,0:T(8,128)(2,1)} %bitcast.57), channel_id=1, source_target_pairs={{0,64},{64,0},{128,192},{192,128},{1,65},{65,1},{129,193},{193,129... | collective-permute-start | bytes 4325384 | tf_op jit(solution)/shard_map/ppermute | solution.py:17
  109.8 31.8 %collective-permute-start.5 = (bf16[512,1408]{1,0:T(8,128)(2,1)}, bf16[512,1408]{1,0:T(8,128)(2,1)}, u32[]{:S(2)}, u32[]{:S(2)}) collective-permute-start(bf16[512,1408]{1,0:T(8,128)(2,1)} %collective-permute-done.3), channel_id=1, source_target_pairs={{0,64},{64,0},{128,192},{192,128},{1,65},{65,1},{129,193},{193,129... | collective-permute-start | bytes 4325384 | tf_op jit(solution)/shard_map/ppermute | solution.py:19
  115.5 36.5 %collective-permute-start.6 = (bf16[1408,512]{1,0:T(8,128)(2,1)}, bf16[1408,512]{1,0:T(8,128)(2,1)}, u32[]{:S(2)}, u32[]{:S(2)}) collective-permute-start(bf16[1408,512]{1,0:T(8,128)(2,1)} %bitcast.10), channel_id=1, source_target_pairs={{0,128},{64,192},{128,0},{192,64},{1,129},{65,193},{129,1},{193,65... | collective-permute-start | bytes 4325384 | tf_op jit(solution)/shard_map/ppermute | solution.py:16
  116.9 35.2 %collective-permute-start.7 = (bf16[1408,512]{1,0:T(8,128)(2,1)}, bf16[1408,512]{1,0:T(8,128)(2,1)}, u32[]{:S(2)}, u32[]{:S(2)}) collective-permute-start(bf16[1408,512]{1,0:T(8,128)(2,1)} %bitcast.10), channel_id=1, source_target_pairs={{0,64},{64,0},{128,192},{192,128},{1,65},{65,1},{129,193},{193,129... | collective-permute-start | bytes 4325384 | tf_op jit(solution)/shard_map/ppermute | solution.py:17
  132.0 9.6 %copy-start.1 = (bf16[832,2048]{1,0:T(8,128)(2,1)S(1)}, bf16[832,2048]{1,0:T(8,128)(2,1)}, u32[]{:S(2)}) copy-start(bf16[832,2048]{1,0:T(8,128)(2,1)} %reshape.84) | copy-start | bytes 10223620
  132.0 9.6 %copy-start.4 = (bf16[1,512,1408]{2,1,0:T(8,128)(2,1)S(1)}, bf16[1,512,1408]{2,1,0:T(8,128)(2,1)}, u32[]{:S(2)}) copy-start(bf16[1,512,1408]{2,1,0:T(8,128)(2,1)} %param.15) | copy-start | bytes 4325380
  152.0 3.4 %collective-permute-start.8 = (bf16[1408,512]{1,0:T(8,128)(2,1)}, bf16[1408,512]{1,0:T(8,128)(2,1)S(1)}, u32[]{:S(2)}, u32[]{:S(2)}) collective-permute-start(bf16[1408,512]{1,0:T(8,128)(2,1)} %collective-permute-done.6), channel_id=1, source_target_pairs={{0,64},{64,0},{128,192},{192,128},{1,65},{65,1},{129,193},{193,129... | collective-permute-start | bytes 4325384 | tf_op jit(solution)/shard_map/ppermute | solution.py:19
  166.2 17.3 %copy-start.3 = (f32[128,6]{0,1:T(8,128)S(1)}, f32[128,6]{0,1:T(8,128)}, u32[]{:S(2)}) copy-start(f32[128,6]{0,1:T(8,128)} %param.12) | copy-start | bytes 9220
  166.2 97.8 %all-to-all-start.1 = ((bf16[64,208,128]{2,1,0:T(8,128)(2,1)}), bf16[64,208,128]{2,1,0:T(8,128)(2,1)S(1)}, u32[]{:S(2)}, u32[]{:S(2)}) async-start(bf16[64,208,128]{2,1,0:T(8,128)(2,1)} %reshape.85), calls=%async_computation.1 | async-start | bytes 6815744 | tf_op jit(solution)/shard_map/all_to_all | solution.py:77

commit v7 on v6

--- a/solution.py
+++ b/solution.py
@@ -41,7 +41,7 @@
     wu = _dp_parts(up_shard)
     gate_cross = wg[1]
     wg = jnp.concatenate(wg, axis=0)
-    down_shard = lax.optimization_barrier((down_weight[0], wu[1], wg))[0]
+    down_shard = lax.optimization_barrier((down_weight[0], wu[1]))[0]
     wu = jnp.concatenate(wu, axis=0)
 
     d = lax.axis_index("dp")

time: 269 us -> 263 us (0.978)
  other arithmetic: 10.3 us -> 4.58 us
  starting transfers between devices: 35.3 us -> 32.2 us
  waiting for transfers between devices: 177 us -> 180 us
    all_to_all x1, waiting for transfers between devices: 11.9 us -> 17.9 us  [local(): received = lax.all_to_all(send, 'ep', 0, 0, tiled=True)]
    concatenate x1 -> x0, other arithmetic: 5.75 us -> none  [local(): wg = jnp.concatenate(wg, axis=0)]
    all_to_all x1, starting transfers between devices: 16.6 us -> 13.5 us  [local(): returned = lax.all_to_all(expert_out, 'ep', 0, 0, tiled=True)]
    ppermute x3, waiting for transfers between devices: 82.1 us -> 79.4 us  [_dp_parts(): cross = lax.ppermute(w, 'dp', _perm(n, 2))]
  transfers between devices with their start and end apart: 11 -> 11, of which waited for: 6 -> 5; matrix products, arithmetic and copies ran while one was open for 15% -> 13% of each run, Pallas kernels for 0% -> 0%
where the time goes in v7:
time: 263 us
  waiting for transfers between devices  180 us (68%)
  starting transfers between devices  32.2 us (12%)
  matrix products  28.6 us (11%)
  local copies, waits for them, and re-layouts  17.3 us (7%)
  other arithmetic  4.58 us (2%)
    ppermute x3, waiting for transfers between devices, _dp_parts(): cross = lax.ppermute(w, 'dp', _perm(n, 2))  79.4 us
    all_to_all x1, waiting for transfers between devices, local(): returned = lax.all_to_all(expert_out, 'ep', 0, 0, tiled=True)  79.4 us
    all_to_all x1, waiting for transfers between devices, local(): received = lax.all_to_all(send, 'ep', 0, 0, tiled=True)  17.9 us
    all_to_all x1, starting transfers between devices, local(): received = lax.all_to_all(send, 'ep', 0, 0, tiled=True)  14.2 us
    all_to_all x1, starting transfers between devices, local(): returned = lax.all_to_all(expert_out, 'ep', 0, 0, tiled=True)  13.5 us
    dot_general x1, matrix products, local(): gate = jnp.dot(received, wg, preferred_element_type=jnp.float32)  9.51 us
    dot_general x1, matrix products, local(): up = jnp.dot(received, wu, preferred_element_type=jnp.float32)  7.81 us
    dot_general x1, matrix products, local(): jnp.dot(hidden, wd, preferred_element_type=jnp.float32).astype(jnp.bfloat16)  7.4 us
  transfers between devices with their start and end apart: 11, of which 5 were waited for; matrix products, arithmetic and copies ran while one was open for 13% of the time, Pallas kernels for 0%

profile of v7, /device:TPU:38, one launch (start us, length us, event | category | flops | bytes accessed | tf_op | source)
XLA Modules:
  0.0 263.0 jit_solution(5754546719527873756)
XLA Ops:
  0.0 1.6 collective-permute-start
  1.6 0.8 copy.31
  2.5 1.8 reduce-window.6
  4.3 0.3 slice_reduce_fusion
  4.8 0.8 select_reduce_fusion.1
  5.8 1.3 copy.36
  7.4 0.6 gather_fusion.1
  8.4 0.4 fusion.29
  8.8 1.1 convolution_convert_fusion
  9.9 3.9 %copy.40 = bf16[832,16,128]{2,1,0:T(8,128)(2,1)} copy(bf16[832,16,128]{2,0,1:T(8,128)(2,1)S(1)} %convolution_convert_fusion) | data formatting | bytes 6815744 | tf_op jit(solution)/shard_map/convert_element_type | solution.py:65
  13.8 19.7 %collective-permute-done = bf16[512,1408]{1,0:T(8,128)(2,1)S(1)} collective-permute-done((bf16[512,1408]{1,0:T(8,128)(2,1)}, bf16[512,1408]{1,0:T(8,128)(2,1)S(1)}, u32[]{:S(2)}, u32[]{:S(2)}) %collective-permute-start) | collective-permute-done | bytes 1441824 | tf_op jit(solution)/shard_map/ppermute | solution.py:16
  33.5 1.1 copy-done.5
  34.6 14.2 %all-to-all-start = ((bf16[64,208,128]{2,1,0:T(8,128)(2,1)}), bf16[64,208,128]{2,1,0:T(8,128)(2,1)S(1)}, u32[]{:S(2)}, u32[]{:S(2)}) async-start(bf16[64,208,128]{2,1,0:T(8,128)(2,1)} %bitcast.45), calls=%async_computation | async-start | bytes 6815744 | tf_op jit(solution)/shard_map/all_to_all | solution.py:67
  48.8 0.8 collective-permute-start.3
  49.6 0.5 collective-permute-start.2
  50.1 59.6 %collective-permute-done.3 = bf16[512,1408]{1,0:T(8,128)(2,1)} collective-permute-done((bf16[512,1408]{1,0:T(8,128)(2,1)}, bf16[512,1408]{1,0:T(8,128)(2,1)}, u32[]{:S(2)}, u32[]{:S(2)}) %collective-permute-start.3) | collective-permute-done | bytes 1441824 | tf_op jit(solution)/shard_map/ppermute | solution.py:16
  109.8 1.3 collective-permute-start.6
  111.1 17.9 %all-to-all-done = bf16[64,208,128]{2,1,0:T(8,128)(2,1)S(1)} async-done(((bf16[64,208,128]{2,1,0:T(8,128)(2,1)}), bf16[64,208,128]{2,1,0:T(8,128)(2,1)S(1)}, u32[]{:S(2)}, u32[]{:S(2)}) %all-to-all-start) | async-done | bytes 3407904 | tf_op jit(solution)/shard_map/all_to_all | solution.py:67
  129.0 2.9 %reshape.84 = bf16[832,2048]{1,0:T(8,128)(2,1)} reshape(bf16[64,208,128]{2,1,0:T(8,128)(2,1)S(1)} %all-to-all-done) | data formatting | bytes 6815744 | tf_op jit(solution)/shard_map/reshape | solution.py:68
  132.2 9.5 %fusion = f32[832,1408]{1,0:T(8,128)S(1)} fusion(bf16[832,2048]{1,0:T(8,128)(2,1)} %reshape.84, bf16[512,1408]{1,0:T(8,128)(2,1)} %collective-permute-done.2, bf16[512,1408]{1,0:T(8,128)(2,1)} %collective-permute-done.1, bf16[512,1408]{1,0:T(8,128)(2,1)} %copy-done.5, bf16[512,1408]{1,0:T(8,128)(2,1)} %bitcast.54), kind=kOutput, calls=%fused_computation.3 | convolution fusion | flops 4821352448 | bytes 13860864 | tf_op jit(solution)/shard_map/dot_general | solution.py:70
  141.8 7.8 %multiply_convert_fusion = bf16[832,1408]{1,0:T(8,128)(2,1)S(1)} fusion(f32[832,1408]{1,0:T(8,128)S(1)} %fusion, bf16[832,2048]{1,0:T(8,128)(2,1)S(1)} %copy-done.1, bf16[512,1408]{1,0:T(8,128)(2,1)} %collective-permute-done.5, bf16[512,1408]{1,0:T(8,128)(2,1)} %collective-permute-done.4, bf16[512,1408]{1,0:T(8,128)(2,1)} %collective-permute-done.3, ...), kind=kOutput, calls=%fused_computation.27 | convolution fusion | flops 4828381184 | bytes 16203776 | tf_op jit(solution)/shard_map/dot_general | solution.py:71
  149.7 3.4 %collective-permute-done.8 = bf16[1408,512]{1,0:T(8,128)(2,1)S(1)} collective-permute-done((bf16[1408,512]{1,0:T(8,128)(2,1)}, bf16[1408,512]{1,0:T(8,128)(2,1)S(1)}, u32[]{:S(2)}, u32[]{:S(2)}) %collective-permute-start.8) | collective-permute-done | bytes 1441824 | tf_op jit(solution)/shard_map/ppermute | solution.py:19
  153.1 7.4 %fusion.24 = bf16[832,2048]{1,0:T(8,128)(2,1)S(1)} fusion(bf16[832,1408]{1,0:T(8,128)(2,1)S(1)} %multiply_convert_fusion, bf16[1408,512]{1,0:T(8,128)(2,1)S(1)} %collective-permute-done.8, bf16[1408,512]{1,0:T(8,128)(2,1)S(1)} %collective-permute-done.7, bf16[1408,512]{1,0:T(8,128)(2,1)} %collective-permute-done.6, bf16[1408,512]{1,0:T(8,128)(2,1)S(1)} %bitcast.60), kind=kOutput, calls=%fused_computation.28 | convolution fusion | flops 4823056384 | bytes 11517952 | tf_op jit(solution)/shard_map/dot_general | solution.py:74
  160.5 3.0 %reshape.85 = bf16[64,208,128]{2,1,0:T(8,128)(2,1)} reshape(bf16[832,2048]{1,0:T(8,128)(2,1)S(1)} %fusion.24) | data formatting | bytes 6815744 | tf_op jit(solution)/shard_map/reshape | solution.py:76
  163.6 13.5 %all-to-all-start.1 = ((bf16[64,208,128]{2,1,0:T(8,128)(2,1)}), bf16[64,208,128]{2,1,0:T(8,128)(2,1)S(1)}, u32[]{:S(2)}, u32[]{:S(2)}) async-start(bf16[64,208,128]{2,1,0:T(8,128)(2,1)} %reshape.85), calls=%async_computation.1 | async-start | bytes 6815744 | tf_op jit(solution)/shard_map/all_to_all | solution.py:77
  177.1 0.6 gather_fusion
  177.8 0.3 select_reduce_fusion
  178.1 0.8 reduce-precision_convert_fusion
  178.9 79.4 %all-to-all-done.1 = bf16[64,208,128]{2,1,0:T(8,128)(2,1)S(1)} async-done(((bf16[64,208,128]{2,1,0:T(8,128)(2,1)}), bf16[64,208,128]{2,1,0:T(8,128)(2,1)S(1)}, u32[]{:S(2)}, u32[]{:S(2)}) %all-to-all-start.1) | async-done | bytes 3407904 | tf_op jit(solution)/shard_map/all_to_all | solution.py:77
  258.3 2.8 %fusion.27 = f32[256,16,128]{0,2,1:T(8,128)S(1)} fusion(bf16[832,16,128]{2,1,0:T(8,128)(2,1)S(1)} %bitcast.46, bf16[128,832]{0,1:T(8,128)(2,1)} %get-tuple-element.21, bf16[128,832]{0,1:T(8,128)(2,1)} %get-tuple-element.20), kind=kOutput, calls=%fused_computation.29 | convolution fusion | flops 873267200 | bytes 5931008 | tf_op jit(solution)/shard_map/ts,srl->trl/dot_general | solution.py:85
  261.2 0.6 gather_fusion.2
  262.0 1.0 copy.44
  (41 shorter events, 1.8 us)
Async XLA Ops:
  0.0 7.4 %copy-start = (s32[4]{0:T(128)S(1)}, s32[4]{0:T(128)}, u32[]{:S(2)}) copy-start(s32[4]{0:T(128)} %constant.37.clone) | copy-start | bytes 52
  0.0 33.5 %collective-permute-start = (bf16[512,1408]{1,0:T(8,128)(2,1)}, bf16[512,1408]{1,0:T(8,128)(2,1)S(1)}, u32[]{:S(2)}, u32[]{:S(2)}) collective-permute-start(bf16[512,1408]{1,0:T(8,128)(2,1)} %bitcast.52), channel_id=1, source_target_pairs={{0,128},{64,192},{128,0},{192,64},{1,129},{65,193},{129,1},{193,65... | collective-permute-start | bytes 4325384 | tf_op jit(solution)/shard_map/ppermute | solution.py:16
  33.5 1.1 copy-start.5
  34.6 94.3 %all-to-all-start = ((bf16[64,208,128]{2,1,0:T(8,128)(2,1)}), bf16[64,208,128]{2,1,0:T(8,128)(2,1)S(1)}, u32[]{:S(2)}, u32[]{:S(2)}) async-start(bf16[64,208,128]{2,1,0:T(8,128)(2,1)} %bitcast.45), calls=%async_computation | async-start | bytes 6815744 | tf_op jit(solution)/shard_map/all_to_all | solution.py:67
  48.8 60.9 %collective-permute-start.3 = (bf16[512,1408]{1,0:T(8,128)(2,1)}, bf16[512,1408]{1,0:T(8,128)(2,1)}, u32[]{:S(2)}, u32[]{:S(2)}) collective-permute-start(bf16[512,1408]{1,0:T(8,128)(2,1)} %bitcast.55), channel_id=1, source_target_pairs={{0,128},{64,192},{128,0},{192,64},{1,129},{65,193},{129,1},{193,65... | collective-permute-start | bytes 4325384 | tf_op jit(solution)/shard_map/ppermute | solution.py:16
  49.6 82.3 %collective-permute-start.1 = (bf16[512,1408]{1,0:T(8,128)(2,1)}, bf16[512,1408]{1,0:T(8,128)(2,1)}, u32[]{:S(2)}, u32[]{:S(2)}) collective-permute-start(bf16[512,1408]{1,0:T(8,128)(2,1)} %bitcast.53), channel_id=1, source_target_pairs={{0,64},{64,0},{128,192},{192,128},{1,65},{65,1},{129,193},{193,129... | collective-permute-start | bytes 4325384 | tf_op jit(solution)/shard_map/ppermute | solution.py:17
  49.6 82.6 %collective-permute-start.2 = (bf16[512,1408]{1,0:T(8,128)(2,1)}, bf16[512,1408]{1,0:T(8,128)(2,1)}, u32[]{:S(2)}, u32[]{:S(2)}) collective-permute-start(bf16[512,1408]{1,0:T(8,128)(2,1)} %copy-done.5), channel_id=1, source_target_pairs={{0,64},{64,0},{128,192},{192,128},{1,65},{65,1},{129,193},{193,129... | collective-permute-start | bytes 4325384 | tf_op jit(solution)/shard_map/ppermute | solution.py:19
  50.1 91.6 %collective-permute-start.4 = (bf16[512,1408]{1,0:T(8,128)(2,1)}, bf16[512,1408]{1,0:T(8,128)(2,1)}, u32[]{:S(2)}, u32[]{:S(2)}) collective-permute-start(bf16[512,1408]{1,0:T(8,128)(2,1)} %bitcast.56), channel_id=1, source_target_pairs={{0,64},{64,0},{128,192},{192,128},{1,65},{65,1},{129,193},{193,129... | collective-permute-start | bytes 4325384 | tf_op jit(solution)/shard_map/ppermute | solution.py:17
  109.8 32.0 %collective-permute-start.5 = (bf16[512,1408]{1,0:T(8,128)(2,1)}, bf16[512,1408]{1,0:T(8,128)(2,1)}, u32[]{:S(2)}, u32[]{:S(2)}) collective-permute-start(bf16[512,1408]{1,0:T(8,128)(2,1)} %collective-permute-done.3), channel_id=1, source_target_pairs={{0,64},{64,0},{128,192},{192,128},{1,65},{65,1},{129,193},{193,129... | collective-permute-start | bytes 4325384 | tf_op jit(solution)/shard_map/ppermute | solution.py:19
  109.8 39.8 %collective-permute-start.6 = (bf16[1408,512]{1,0:T(8,128)(2,1)}, bf16[1408,512]{1,0:T(8,128)(2,1)}, u32[]{:S(2)}, u32[]{:S(2)}) collective-permute-start(bf16[1408,512]{1,0:T(8,128)(2,1)} %bitcast.58), channel_id=1, source_target_pairs={{0,128},{64,192},{128,0},{192,64},{1,129},{65,193},{129,1},{193,65... | collective-permute-start | bytes 4325384 | tf_op jit(solution)/shard_map/ppermute | solution.py:16
  131.9 9.9 %copy-start.1 = (bf16[832,2048]{1,0:T(8,128)(2,1)S(1)}, bf16[832,2048]{1,0:T(8,128)(2,1)}, u32[]{:S(2)}) copy-start(bf16[832,2048]{1,0:T(8,128)(2,1)} %reshape.84) | copy-start | bytes 10223620
  131.9 9.9 %copy-start.3 = (bf16[1,512,1408]{2,1,0:T(8,128)(2,1)S(1)}, bf16[1,512,1408]{2,1,0:T(8,128)(2,1)}, u32[]{:S(2)}) copy-start(bf16[1,512,1408]{2,1,0:T(8,128)(2,1)} %param.15) | copy-start | bytes 4325380
  131.9 17.8 %collective-permute-start.7 = (bf16[1408,512]{1,0:T(8,128)(2,1)}, bf16[1408,512]{1,0:T(8,128)(2,1)S(1)}, u32[]{:S(2)}, u32[]{:S(2)}) collective-permute-start(bf16[1408,512]{1,0:T(8,128)(2,1)} %bitcast.59), channel_id=1, source_target_pairs={{0,64},{64,0},{128,192},{192,128},{1,65},{65,1},{129,193},{193,129... | collective-permute-start | bytes 4325384 | tf_op jit(solution)/shard_map/ppermute | solution.py:17
  141.7 11.4 %copy-start.4 = (bf16[1,1408,512]{2,1,0:T(8,128)(2,1)S(1)}, bf16[1,1408,512]{2,1,0:T(8,128)(2,1)}, u32[]{:S(2)}) copy-start(bf16[1,1408,512]{2,1,0:T(8,128)(2,1)} %param.16) | copy-start | bytes 4325380
  149.6 3.5 %collective-permute-start.8 = (bf16[1408,512]{1,0:T(8,128)(2,1)}, bf16[1408,512]{1,0:T(8,128)(2,1)S(1)}, u32[]{:S(2)}, u32[]{:S(2)}) collective-permute-start(bf16[1408,512]{1,0:T(8,128)(2,1)} %collective-permute-done.6), channel_id=1, source_target_pairs={{0,64},{64,0},{128,192},{192,128},{1,65},{65,1},{129,193},{193,129... | collective-permute-start | bytes 4325384 | tf_op jit(solution)/shard_map/ppermute | solution.py:19
  163.6 14.2 %copy-start.2 = (f32[128,6]{0,1:T(8,128)S(1)}, f32[128,6]{0,1:T(8,128)}, u32[]{:S(2)}) copy-start(f32[128,6]{0,1:T(8,128)} %param.12) | copy-start | bytes 9220
  163.6 94.7 %all-to-all-start.1 = ((bf16[64,208,128]{2,1,0:T(8,128)(2,1)}), bf16[64,208,128]{2,1,0:T(8,128)(2,1)S(1)}, u32[]{:S(2)}, u32[]{:S(2)}) async-start(bf16[64,208,128]{2,1,0:T(8,128)(2,1)} %reshape.85), calls=%async_computation.1 | async-start | bytes 6815744 | tf_op jit(solution)/shard_map/all_to_all | solution.py:77

commit v8 on v7

--- a/solution.py
+++ b/solution.py
@@ -36,11 +36,13 @@
     cap = C
     slots = experts * cap
 
-    wg = _dp_parts(gate_weight[0])
-    up_shard = lax.optimization_barrier((up_weight[0], wg[1]))[0]
+    half = gate_weight.shape[1] // 2
+    wg_a = _dp_parts(gate_weight[0, :half])
+    gate_cross = wg_a[1]
+    wg_b = _dp_parts(lax.optimization_barrier((gate_weight[0, half:], gate_cross))[0])
+    up_shard = lax.optimization_barrier((up_weight[0], wg_b[1]))[0]
     wu = _dp_parts(up_shard)
-    gate_cross = wg[1]
-    wg = jnp.concatenate(wg, axis=0)
+    wg = jnp.concatenate([x for pair in zip(wg_a, wg_b) for x in pair], axis=0)
     down_shard = lax.optimization_barrier((down_weight[0], wu[1]))[0]
     wu = jnp.concatenate(wu, axis=0)
 

time: 263 us -> 268 us (1.019)
  local copies, waits for them, and re-layouts: 17.3 us -> 24.1 us
  waiting for transfers between devices: 180 us -> 175 us
    all_to_all x1, waiting for transfers between devices: 17.9 us -> 0.01 us  [local(): received = lax.all_to_all(send, 'ep', 0, 0, tiled=True)]
    ppermute x3 -> x4, waiting for transfers between devices: 79.4 us -> 91.2 us  [_dp_parts(): cross = lax.ppermute(w, 'dp', _perm(n, 2))]
    unnamed x14 -> x23, local copies, waits for them, and re-layouts: 3.24 us -> 6.93 us
  transfers between devices with their start and end apart: 11 -> 14, of which waited for: 5 -> 6; matrix products, arithmetic and copies ran while one was open for 13% -> 14% of each run, Pallas kernels for 0% -> 0%
where the time goes in v8:
time: 268 us
  waiting for transfers between devices  175 us (65%)
  starting transfers between devices  34.7 us (13%)
  matrix products  28.8 us (11%)
  local copies, waits for them, and re-layouts  24.1 us (9%)
  other arithmetic  5.23 us (2%)
    ppermute x4, waiting for transfers between devices, _dp_parts(): cross = lax.ppermute(w, 'dp', _perm(n, 2))  91.2 us
    all_to_all x1, waiting for transfers between devices, local(): returned = lax.all_to_all(expert_out, 'ep', 0, 0, tiled=True)  80.1 us
    all_to_all x1, starting transfers between devices, local(): received = lax.all_to_all(send, 'ep', 0, 0, tiled=True)  14.2 us
    all_to_all x1, starting transfers between devices, local(): returned = lax.all_to_all(expert_out, 'ep', 0, 0, tiled=True)  13.6 us
    dot_general x1, matrix products, local(): gate = jnp.dot(received, wg, preferred_element_type=jnp.float32)  9.46 us
    dot_general x1, matrix products, local(): up = jnp.dot(received, wu, preferred_element_type=jnp.float32)  7.78 us
    dot_general x1, matrix products, local(): jnp.dot(hidden, wd, preferred_element_type=jnp.float32).astype(jnp.bfloat16)  7.69 us
    unnamed x23, local copies, waits for them, and re-layouts  6.93 us
  transfers between devices with their start and end apart: 14, of which 6 were waited for; matrix products, arithmetic and copies ran while one was open for 14% of the time, Pallas kernels for 0%

profile of v8, /device:TPU:38, one launch (start us, length us, event | category | flops | bytes accessed | tf_op | source)
XLA Modules:
  0.0 267.9 jit_solution(1543155441116172493)
XLA Ops:
  0.0 2.4 slice_bitcast_fusion
  2.4 1.6 collective-permute-start
  3.9 0.8 copy.31
  5.0 1.8 reduce-window.6
  7.8 1.3 gather_fusion
  9.1 0.8 select_reduce_fusion.1
  12.1 1.0 convolution_convert_fusion
  13.2 4.0 %copy.40 = bf16[832,16,128]{2,1,0:T(8,128)(2,1)} copy(bf16[832,16,128]{2,0,1:T(8,128)(2,1)S(1)} %convolution_convert_fusion) | data formatting | bytes 6815744 | tf_op jit(solution)/shard_map/convert_element_type | solution.py:67
  17.1 3.1 %collective-permute-done = bf16[256,1408]{1,0:T(8,128)(2,1)S(1)} collective-permute-done((bf16[256,1408]{1,0:T(8,128)(2,1)S(1)}, bf16[256,1408]{1,0:T(8,128)(2,1)S(1)}, u32[]{:S(2)}, u32[]{:S(2)}) %collective-permute-start) | collective-permute-done | bytes 720928 | tf_op jit(solution)/shard_map/ppermute | solution.py:16
  20.2 0.9 copy-done.1
  21.1 14.2 %all-to-all-start = ((bf16[64,208,128]{2,1,0:T(8,128)(2,1)}), bf16[64,208,128]{2,1,0:T(8,128)(2,1)S(1)}, u32[]{:S(2)}, u32[]{:S(2)}) async-start(bf16[64,208,128]{2,1,0:T(8,128)(2,1)} %bitcast.51), calls=%async_computation | async-start | bytes 6815744 | tf_op jit(solution)/shard_map/all_to_all | solution.py:69
  35.3 0.8 collective-permute-start.1
  36.1 28.2 %collective-permute-done.1 = bf16[256,1408]{1,0:T(8,128)(2,1)S(1)} collective-permute-done((bf16[256,1408]{1,0:T(8,128)(2,1)}, bf16[256,1408]{1,0:T(8,128)(2,1)S(1)}, u32[]{:S(2)}, u32[]{:S(2)}) %collective-permute-start.1) | collective-permute-done | bytes 720928 | tf_op jit(solution)/shard_map/ppermute | solution.py:16
  64.3 1.3 collective-permute-start.6
  65.6 1.2 constant_dynamic-update-slice_fusion.7
  67.4 1.2 constant_dynamic-update-slice_fusion.6
  68.6 1.2 constant_dynamic-update-slice_fusion.5
  70.8 48.8 %collective-permute-done.6 = bf16[512,1408]{1,0:T(8,128)(2,1)} collective-permute-done((bf16[512,1408]{1,0:T(8,128)(2,1)}, bf16[512,1408]{1,0:T(8,128)(2,1)}, u32[]{:S(2)}, u32[]{:S(2)}) %collective-permute-start.6) | collective-permute-done | bytes 1441824 | tf_op jit(solution)/shard_map/ppermute | solution.py:16
  119.7 1.4 collective-permute-start.9
  121.2 1.0 copy-done.4
  122.7 3.0 %reshape.84 = bf16[832,2048]{1,0:T(8,128)(2,1)} reshape(bf16[64,208,128]{2,1,0:T(8,128)(2,1)S(1)} %all-to-all-done) | data formatting | bytes 6815744 | tf_op jit(solution)/shard_map/reshape | solution.py:70
  125.7 9.5 %fusion.37 = f32[832,1408]{1,0:T(8,128)S(1)} fusion(bf16[832,2048]{1,0:T(8,128)(2,1)} %reshape.84, bf16[2048,1408]{1,0:T(8,128)(2,1)} %copy-done.4), kind=kOutput, calls=%fused_computation.72 | convolution fusion | flops 4798283776 | bytes 13860864 | tf_op jit(solution)/shard_map/dot_general | solution.py:72
  135.2 7.8 %multiply_convert_fusion = bf16[832,1408]{1,0:T(8,128)(2,1)S(1)} fusion(f32[832,1408]{1,0:T(8,128)S(1)} %fusion.37, bf16[832,2048]{1,0:T(8,128)(2,1)S(1)} %copy-done, bf16[512,1408]{1,0:T(8,128)(2,1)} %collective-permute-done.8, bf16[512,1408]{1,0:T(8,128)(2,1)} %collective-permute-done.7, bf16[512,1408]{1,0:T(8,128)(2,1)} %collective-permute-done.6, ...), kind=kOutput, calls=%fused_computation.19 | convolution fusion | flops 4828381184 | bytes 16203776 | tf_op jit(solution)/shard_map/dot_general | solution.py:73
  143.0 11.1 %collective-permute-done.9 = bf16[1408,512]{1,0:T(8,128)(2,1)} collective-permute-done((bf16[1408,512]{1,0:T(8,128)(2,1)}, bf16[1408,512]{1,0:T(8,128)(2,1)}, u32[]{:S(2)}, u32[]{:S(2)}) %collective-permute-start.9) | collective-permute-done | bytes 1441824 | tf_op jit(solution)/shard_map/ppermute | solution.py:16
  154.1 3.4 %collective-permute-done.11 = bf16[1408,512]{1,0:T(8,128)(2,1)S(1)} collective-permute-done((bf16[1408,512]{1,0:T(8,128)(2,1)}, bf16[1408,512]{1,0:T(8,128)(2,1)S(1)}, u32[]{:S(2)}, u32[]{:S(2)}) %collective-permute-start.11) | collective-permute-done | bytes 1441824 | tf_op jit(solution)/shard_map/ppermute | solution.py:19
  157.6 7.7 %fusion.16 = bf16[832,2048]{1,0:T(8,128)(2,1)S(1)} fusion(bf16[832,1408]{1,0:T(8,128)(2,1)S(1)} %multiply_convert_fusion, bf16[1408,512]{1,0:T(8,128)(2,1)S(1)} %collective-permute-done.11, bf16[1408,512]{1,0:T(8,128)(2,1)} %collective-permute-done.10, bf16[1408,512]{1,0:T(8,128)(2,1)} %collective-permute-done.9, bf16[1408,512]{1,0:T(8,128)(2,1)} %bitcast.11), kind=kOutput, calls=%fused_computation.20 | convolution fusion | flops 4823056384 | bytes 11517952 | tf_op jit(solution)/shard_map/dot_general | solution.py:76
  165.3 3.1 %reshape.85 = bf16[64,208,128]{2,1,0:T(8,128)(2,1)} reshape(bf16[832,2048]{1,0:T(8,128)(2,1)S(1)} %fusion.16) | data formatting | bytes 6815744 | tf_op jit(solution)/shard_map/reshape | solution.py:78
  168.3 13.6 %all-to-all-start.1 = ((bf16[64,208,128]{2,1,0:T(8,128)(2,1)}), bf16[64,208,128]{2,1,0:T(8,128)(2,1)S(1)}, u32[]{:S(2)}, u32[]{:S(2)}) async-start(bf16[64,208,128]{2,1,0:T(8,128)(2,1)} %reshape.85), calls=%async_computation.1 | async-start | bytes 6815744 | tf_op jit(solution)/shard_map/all_to_all | solution.py:79
  182.3 0.8 reduce-precision_convert_fusion
  183.1 80.1 %all-to-all-done.1 = bf16[64,208,128]{2,1,0:T(8,128)(2,1)S(1)} async-done(((bf16[64,208,128]{2,1,0:T(8,128)(2,1)}), bf16[64,208,128]{2,1,0:T(8,128)(2,1)S(1)}, u32[]{:S(2)}, u32[]{:S(2)}) %all-to-all-start.1) | async-done | bytes 3407904 | tf_op jit(solution)/shard_map/all_to_all | solution.py:79
  263.2 2.8 %fusion.19 = f32[256,16,128]{0,2,1:T(8,128)S(1)} fusion(bf16[832,16,128]{2,1,0:T(8,128)(2,1)S(1)} %bitcast.52, bf16[128,832]{0,1:T(8,128)(2,1)} %get-tuple-element.25, bf16[128,832]{0,1:T(8,128)(2,1)} %get-tuple-element.24), kind=kOutput, calls=%fused_computation.21 | convolution fusion | flops 873267200 | bytes 5931008 | tf_op jit(solution)/shard_map/ts,srl->trl/dot_general | solution.py:87
  266.9 1.0 copy.44
  (57 shorter events, 6.8 us)
Async XLA Ops:
  0.0 10.2 %copy-start.3 = (bf16[128,2048]{1,0:T(8,128)(2,1)S(1)}, bf16[128,2048]{1,0:T(8,128)(2,1)}, u32[]{:S(2)}) copy-start(bf16[128,2048]{1,0:T(8,128)(2,1)} %param.10) | copy-start | bytes 1572868
  2.4 10.8 %copy-start.2 = (bf16[256,1408]{1,0:T(8,128)(2,1)}, bf16[256,1408]{1,0:T(8,128)(2,1)S(1)}, u32[]{:S(2)}) copy-start(bf16[256,1408]{1,0:T(8,128)(2,1)S(1)} %get-tuple-element.23) | copy-start | bytes 2162692
  2.4 17.9 %collective-permute-start = (bf16[256,1408]{1,0:T(8,128)(2,1)S(1)}, bf16[256,1408]{1,0:T(8,128)(2,1)S(1)}, u32[]{:S(2)}, u32[]{:S(2)}) collective-permute-start(bf16[256,1408]{1,0:T(8,128)(2,1)S(1)} %get-tuple-element.23), channel_id=1, source_target_pairs={{0,128},{64,192},{128,0},{192,64},{1,129},{65,193},{129,1},{193,65... | collective-permute-start | bytes 2162696 | tf_op jit(solution)/shard_map/ppermute | solution.py:16
  20.2 0.9 copy-start.1
  21.1 101.6 %all-to-all-start = ((bf16[64,208,128]{2,1,0:T(8,128)(2,1)}), bf16[64,208,128]{2,1,0:T(8,128)(2,1)S(1)}, u32[]{:S(2)}, u32[]{:S(2)}) async-start(bf16[64,208,128]{2,1,0:T(8,128)(2,1)} %bitcast.51), calls=%async_computation | async-start | bytes 6815744 | tf_op jit(solution)/shard_map/all_to_all | solution.py:69
  35.3 28.9 %collective-permute-start.1 = (bf16[256,1408]{1,0:T(8,128)(2,1)}, bf16[256,1408]{1,0:T(8,128)(2,1)S(1)}, u32[]{:S(2)}, u32[]{:S(2)}) collective-permute-start(bf16[256,1408]{1,0:T(8,128)(2,1)} %get-tuple-element.13), channel_id=1, source_target_pairs={{0,128},{64,192},{128,0},{192,64},{1,129},{65,193},{129,1},{193,65... | collective-permute-start | bytes 2162696 | tf_op jit(solution)/shard_map/ppermute | solution.py:16
  36.1 34.0 %collective-permute-start.2 = (bf16[256,1408]{1,0:T(8,128)(2,1)}, bf16[256,1408]{1,0:T(8,128)(2,1)S(1)}, u32[]{:S(2)}, u32[]{:S(2)}) collective-permute-start(bf16[256,1408]{1,0:T(8,128)(2,1)} %copy-done.2), channel_id=1, source_target_pairs={{0,64},{64,0},{128,192},{192,128},{1,65},{65,1},{129,193},{193,129... | collective-permute-start | bytes 2162696 | tf_op jit(solution)/shard_map/ppermute | solution.py:17
  64.3 55.3 %collective-permute-start.6 = (bf16[512,1408]{1,0:T(8,128)(2,1)}, bf16[512,1408]{1,0:T(8,128)(2,1)}, u32[]{:S(2)}, u32[]{:S(2)}) collective-permute-start(bf16[512,1408]{1,0:T(8,128)(2,1)} %bitcast.58), channel_id=1, source_target_pairs={{0,128},{64,192},{128,0},{192,64},{1,129},{65,193},{129,1},{193,65... | collective-permute-start | bytes 4325384 | tf_op jit(solution)/shard_map/ppermute | solution.py:16
  66.8 3.9 %collective-permute-start.3 = (bf16[256,1408]{1,0:T(8,128)(2,1)}, bf16[256,1408]{1,0:T(8,128)(2,1)S(1)}, u32[]{:S(2)}, u32[]{:S(2)}) collective-permute-start(bf16[256,1408]{1,0:T(8,128)(2,1)} %get-tuple-element.13), channel_id=1, source_target_pairs={{0,64},{64,0},{128,192},{192,128},{1,65},{65,1},{129,193},{193,129... | collective-permute-start | bytes 2162696 | tf_op jit(solution)/shard_map/ppermute | solution.py:17
  66.9 52.6 %collective-permute-start.4 = (bf16[256,1408]{1,0:T(8,128)(2,1)}, bf16[256,1408]{1,0:T(8,128)(2,1)S(1)}, u32[]{:S(2)}, u32[]{:S(2)}) collective-permute-start(bf16[256,1408]{1,0:T(8,128)(2,1)} %copy-done.1), channel_id=1, source_target_pairs={{0,64},{64,0},{128,192},{192,128},{1,65},{65,1},{129,193},{193,129... | collective-permute-start | bytes 2162696 | tf_op jit(solution)/shard_map/ppermute | solution.py:19
  69.8 65.4 %collective-permute-start.7 = (bf16[512,1408]{1,0:T(8,128)(2,1)}, bf16[512,1408]{1,0:T(8,128)(2,1)}, u32[]{:S(2)}, u32[]{:S(2)}) collective-permute-start(bf16[512,1408]{1,0:T(8,128)(2,1)} %bitcast.59), channel_id=1, source_target_pairs={{0,64},{64,0},{128,192},{192,128},{1,65},{65,1},{129,193},{193,129... | collective-permute-start | bytes 4325384 | tf_op jit(solution)/shard_map/ppermute | solution.py:17
  70.1 49.6 %collective-permute-start.5 = (bf16[256,1408]{1,0:T(8,128)(2,1)S(1)}, bf16[256,1408]{1,0:T(8,128)(2,1)S(1)}, u32[]{:S(2)}, u32[]{:S(2)}) collective-permute-start(bf16[256,1408]{1,0:T(8,128)(2,1)S(1)} %collective-permute-done.1), channel_id=1, source_target_pairs={{0,64},{64,0},{128,192},{192,128},{1,65},{65,1},{129,193},{193,129... | collective-permute-start | bytes 2162696 | tf_op jit(solution)/shard_map/ppermute | solution.py:19
  119.5 15.7 %collective-permute-start.8 = (bf16[512,1408]{1,0:T(8,128)(2,1)}, bf16[512,1408]{1,0:T(8,128)(2,1)}, u32[]{:S(2)}, u32[]{:S(2)}) collective-permute-start(bf16[512,1408]{1,0:T(8,128)(2,1)} %collective-permute-done.6), channel_id=1, source_target_pairs={{0,64},{64,0},{128,192},{192,128},{1,65},{65,1},{129,193},{193,129... | collective-permute-start | bytes 4325384 | tf_op jit(solution)/shard_map/ppermute | solution.py:19
  119.7 2.5 copy-start.4
  119.7 34.4 %collective-permute-start.9 = (bf16[1408,512]{1,0:T(8,128)(2,1)}, bf16[1408,512]{1,0:T(8,128)(2,1)}, u32[]{:S(2)}, u32[]{:S(2)}) collective-permute-start(bf16[1408,512]{1,0:T(8,128)(2,1)} %bitcast.11), channel_id=1, source_target_pairs={{0,128},{64,192},{128,0},{192,64},{1,129},{65,193},{129,1},{193,65... | collective-permute-start | bytes 4325384 | tf_op jit(solution)/shard_map/ppermute | solution.py:16
  122.2 31.9 %collective-permute-start.10 = (bf16[1408,512]{1,0:T(8,128)(2,1)}, bf16[1408,512]{1,0:T(8,128)(2,1)}, u32[]{:S(2)}, u32[]{:S(2)}) collective-permute-start(bf16[1408,512]{1,0:T(8,128)(2,1)} %bitcast.11), channel_id=1, source_target_pairs={{0,64},{64,0},{128,192},{192,128},{1,65},{65,1},{129,193},{193,129... | collective-permute-start | bytes 4325384 | tf_op jit(solution)/shard_map/ppermute | solution.py:17
  125.7 9.5 %copy-start = (bf16[832,2048]{1,0:T(8,128)(2,1)S(1)}, bf16[832,2048]{1,0:T(8,128)(2,1)}, u32[]{:S(2)}) copy-start(bf16[832,2048]{1,0:T(8,128)(2,1)} %reshape.84) | copy-start | bytes 10223620
  125.7 9.5 %copy-start.6 = (bf16[1,512,1408]{2,1,0:T(8,128)(2,1)S(1)}, bf16[1,512,1408]{2,1,0:T(8,128)(2,1)}, u32[]{:S(2)}) copy-start(bf16[1,512,1408]{2,1,0:T(8,128)(2,1)} %param.15) | copy-start | bytes 4325380
  154.1 3.4 %collective-permute-start.11 = (bf16[1408,512]{1,0:T(8,128)(2,1)}, bf16[1408,512]{1,0:T(8,128)(2,1)S(1)}, u32[]{:S(2)}, u32[]{:S(2)}) collective-permute-start(bf16[1408,512]{1,0:T(8,128)(2,1)} %collective-permute-done.9), channel_id=1, source_target_pairs={{0,64},{64,0},{128,192},{192,128},{1,65},{65,1},{129,193},{193,129... | collective-permute-start | bytes 4325384 | tf_op jit(solution)/shard_map/ppermute | solution.py:19
  168.3 13.6 %copy-start.5 = (f32[128,6]{0,1:T(8,128)S(1)}, f32[128,6]{0,1:T(8,128)}, u32[]{:S(2)}) copy-start(f32[128,6]{0,1:T(8,128)} %param.12) | copy-start | bytes 9220
  168.3 94.8 %all-to-all-start.1 = ((bf16[64,208,128]{2,1,0:T(8,128)(2,1)}), bf16[64,208,128]{2,1,0:T(8,128)(2,1)S(1)}, u32[]{:S(2)}, u32[]{:S(2)}) async-start(bf16[64,208,128]{2,1,0:T(8,128)(2,1)} %reshape.85), calls=%async_computation.1 | async-start | bytes 6815744 | tf_op jit(solution)/shard_map/all_to_all | solution.py:79

commit v9 on v7

--- a/solution.py
+++ b/solution.py
@@ -70,8 +70,10 @@
     gate = jnp.dot(received, wg, preferred_element_type=jnp.float32)
     up = jnp.dot(received, wu, preferred_element_type=jnp.float32)
     hidden = (jax.nn.silu(gate) * up).astype(jnp.bfloat16)
-    wd = jnp.concatenate(_dp_parts(down_shard, after=lambda: hidden), axis=1)
-    expert_out = jnp.dot(hidden, wd, preferred_element_type=jnp.float32).astype(jnp.bfloat16)
+    wd = _dp_parts(down_shard, after=lambda: hidden)
+    first = jnp.dot(hidden, jnp.concatenate(wd[:3], axis=1), preferred_element_type=jnp.float32)
+    last = jnp.dot(hidden, wd[3], preferred_element_type=jnp.float32)
+    expert_out = jnp.concatenate([first, last], axis=1).astype(jnp.bfloat16)
 
     expert_out = expert_out.reshape(n_ep, cap * sub, lanes)
     returned = lax.all_to_all(expert_out, "ep", 0, 0, tiled=True)

time: 263 us -> 260 us (0.989)
  waiting for transfers between devices: 180 us -> 177 us
    ppermute x3, waiting for transfers between devices: 3.41 us -> 0.01 us  [_dp_parts(): far = lax.ppermute(relay, 'dp', _perm(n, 1))]
    convert_element_type x0 -> x1, local copies, waits for them, and re-layouts: none -> 3.03 us  [local(): expert_out = jnp.concatenate([first, last], axis=1).astype(jnp.bfloat16)]
    reshape x1 -> x0, local copies, waits for them, and re-layouts: 3.03 us -> none  [local(): expert_out = expert_out.reshape(n_ep, cap * sub, lanes)]
    dot_general x1 -> x2, matrix products: 7.4 us -> 6.96 us  [the longest x1 5.48 us: local(): jnp.dot(hidden, jnp.concatenate(wd[:3], axis=1), preferred_element_type=j...]
  transfers between devices with their start and end apart: 11 -> 11, of which waited for: 5 -> 4; matrix products, arithmetic and copies ran while one was open for 13% -> 15% of each run, Pallas kernels for 0% -> 0%
where the time goes in v9:
time: 260 us
  waiting for transfers between devices  177 us (68%)
  starting transfers between devices  32.2 us (12%)
  matrix products  28.1 us (11%)
  local copies, waits for them, and re-layouts  17.3 us (7%)
  other arithmetic  4.99 us (2%)
    all_to_all x1, waiting for transfers between devices, local(): returned = lax.all_to_all(expert_out, 'ep', 0, 0, tiled=True)  79.7 us
    ppermute x3, waiting for transfers between devices, _dp_parts(): cross = lax.ppermute(w, 'dp', _perm(n, 2))  79.4 us
    all_to_all x1, waiting for transfers between devices, local(): received = lax.all_to_all(send, 'ep', 0, 0, tiled=True)  17.9 us
    all_to_all x1, starting transfers between devices, local(): received = lax.all_to_all(send, 'ep', 0, 0, tiled=True)  14.2 us
    all_to_all x1, starting transfers between devices, local(): returned = lax.all_to_all(expert_out, 'ep', 0, 0, tiled=True)  13.5 us
    dot_general x1, matrix products, local(): gate = jnp.dot(received, wg, preferred_element_type=jnp.float32)  9.51 us
    dot_general x1, matrix products, local(): up = jnp.dot(received, wu, preferred_element_type=jnp.float32)  7.81 us
    dot_general x1, matrix products, local(): jnp.dot(hidden, jnp.concatenate(wd[:3], axis=1), preferred_element_type=j...  5.48 us
  transfers between devices with their start and end apart: 11, of which 4 were waited for; matrix products, arithmetic and copies ran while one was open for 15% of the time, Pallas kernels for 0%

profile of v9, /device:TPU:38, one launch (start us, length us, event | category | flops | bytes accessed | tf_op | source)
XLA Modules:
  0.0 259.9 jit_solution(6872736560559214366)
XLA Ops:
  0.0 1.6 collective-permute-start
  1.6 0.8 copy.31
  2.5 1.8 reduce-window.6
  4.8 0.8 select_reduce_fusion.1
  5.8 1.3 copy.36
  7.4 0.6 gather_fusion.1
  8.4 0.4 fusion.27
  8.8 1.1 convolution_convert_fusion
  9.9 3.9 %copy.40 = bf16[832,16,128]{2,1,0:T(8,128)(2,1)} copy(bf16[832,16,128]{2,0,1:T(8,128)(2,1)S(1)} %convolution_convert_fusion) | data formatting | bytes 6815744 | tf_op jit(solution)/shard_map/convert_element_type | solution.py:65
  13.8 19.7 %collective-permute-done = bf16[512,1408]{1,0:T(8,128)(2,1)S(1)} collective-permute-done((bf16[512,1408]{1,0:T(8,128)(2,1)}, bf16[512,1408]{1,0:T(8,128)(2,1)S(1)}, u32[]{:S(2)}, u32[]{:S(2)}) %collective-permute-start) | collective-permute-done | bytes 1441824 | tf_op jit(solution)/shard_map/ppermute | solution.py:16
  33.5 1.1 copy-done.5
  34.6 14.2 %all-to-all-start = ((bf16[64,208,128]{2,1,0:T(8,128)(2,1)}), bf16[64,208,128]{2,1,0:T(8,128)(2,1)S(1)}, u32[]{:S(2)}, u32[]{:S(2)}) async-start(bf16[64,208,128]{2,1,0:T(8,128)(2,1)} %bitcast.47), calls=%async_computation | async-start | bytes 6815744 | tf_op jit(solution)/shard_map/all_to_all | solution.py:67
  48.8 0.8 collective-permute-start.3
  49.6 0.5 collective-permute-start.2
  50.1 59.6 %collective-permute-done.3 = bf16[512,1408]{1,0:T(8,128)(2,1)} collective-permute-done((bf16[512,1408]{1,0:T(8,128)(2,1)}, bf16[512,1408]{1,0:T(8,128)(2,1)}, u32[]{:S(2)}, u32[]{:S(2)}) %collective-permute-start.3) | collective-permute-done | bytes 1441824 | tf_op jit(solution)/shard_map/ppermute | solution.py:16
  109.8 1.3 collective-permute-start.6
  111.1 17.9 %all-to-all-done = bf16[64,208,128]{2,1,0:T(8,128)(2,1)S(1)} async-done(((bf16[64,208,128]{2,1,0:T(8,128)(2,1)}), bf16[64,208,128]{2,1,0:T(8,128)(2,1)S(1)}, u32[]{:S(2)}, u32[]{:S(2)}) %all-to-all-start) | async-done | bytes 3407904 | tf_op jit(solution)/shard_map/all_to_all | solution.py:67
  129.0 2.9 %reshape.84 = bf16[832,2048]{1,0:T(8,128)(2,1)} reshape(bf16[64,208,128]{2,1,0:T(8,128)(2,1)S(1)} %all-to-all-done) | data formatting | bytes 6815744 | tf_op jit(solution)/shard_map/reshape | solution.py:68
  132.2 9.5 %fusion = f32[832,1408]{1,0:T(8,128)S(1)} fusion(bf16[832,2048]{1,0:T(8,128)(2,1)} %reshape.84, bf16[512,1408]{1,0:T(8,128)(2,1)} %collective-permute-done.2, bf16[512,1408]{1,0:T(8,128)(2,1)} %collective-permute-done.1, bf16[512,1408]{1,0:T(8,128)(2,1)} %copy-done.5, bf16[512,1408]{1,0:T(8,128)(2,1)} %bitcast.56), kind=kOutput, calls=%fused_computation.3 | convolution fusion | flops 4821352448 | bytes 13860864 | tf_op jit(solution)/shard_map/dot_general | solution.py:70
  141.8 7.8 %multiply_convert_fusion = bf16[832,1408]{1,0:T(8,128)(2,1)S(1)} fusion(f32[832,1408]{1,0:T(8,128)S(1)} %fusion, bf16[832,2048]{1,0:T(8,128)(2,1)S(1)} %copy-done.1, bf16[512,1408]{1,0:T(8,128)(2,1)} %collective-permute-done.5, bf16[512,1408]{1,0:T(8,128)(2,1)} %collective-permute-done.4, bf16[512,1408]{1,0:T(8,128)(2,1)} %collective-permute-done.3, ...), kind=kOutput, calls=%fused_computation.19 | convolution fusion | flops 4828381184 | bytes 16203776 | tf_op jit(solution)/shard_map/dot_general | solution.py:71
  149.7 5.5 %fusion.22 = bf16[832,1536]{1,0:T(8,128)(2,1)S(1)} fusion(bf16[832,1408]{1,0:T(8,128)(2,1)S(1)} %multiply_convert_fusion, bf16[1408,512]{1,0:T(8,128)(2,1)S(1)} %collective-permute-done.7, bf16[1408,512]{1,0:T(8,128)(2,1)} %collective-permute-done.6, bf16[1408,512]{1,0:T(8,128)(2,1)S(1)} %bitcast.62), kind=kOutput, calls=%fused_computation.26 | convolution fusion | flops 3612966912 | bytes 9224192 | tf_op jit(solution)/shard_map/dot_general | solution.py:74
  155.2 1.5 convolution_convert_fusion.1
  156.7 0.4 pad_maximum_fusion
  157.1 3.0 %convert_element_type.34 = bf16[64,208,128]{2,1,0:T(8,128)(2,1)} reshape(bf16[832,2048]{1,0:T(8,128)(2,1)S(1)} %pad_maximum_fusion) | data formatting | bytes 6815744 | tf_op jit(solution)/shard_map/convert_element_type | solution.py:76
  160.2 13.5 %all-to-all-start.1 = ((bf16[64,208,128]{2,1,0:T(8,128)(2,1)}), bf16[64,208,128]{2,1,0:T(8,128)(2,1)S(1)}, u32[]{:S(2)}, u32[]{:S(2)}) async-start(bf16[64,208,128]{2,1,0:T(8,128)(2,1)} %convert_element_type.34), calls=%async_computation.1 | async-start | bytes 6815744 | tf_op jit(solution)/shard_map/all_to_all | solution.py:79
  173.7 0.6 gather_fusion
  174.3 0.3 select_reduce_fusion
  174.7 0.8 reduce-precision_convert_fusion
  175.5 79.7 %all-to-all-done.1 = bf16[64,208,128]{2,1,0:T(8,128)(2,1)S(1)} async-done(((bf16[64,208,128]{2,1,0:T(8,128)(2,1)}), bf16[64,208,128]{2,1,0:T(8,128)(2,1)S(1)}, u32[]{:S(2)}, u32[]{:S(2)}) %all-to-all-start.1) | async-done | bytes 3407904 | tf_op jit(solution)/shard_map/all_to_all | solution.py:79
  255.2 2.8 %fusion.25 = f32[256,16,128]{0,2,1:T(8,128)S(1)} fusion(bf16[832,16,128]{2,1,0:T(8,128)(2,1)S(1)} %bitcast.48, bf16[128,832]{0,1:T(8,128)(2,1)} %get-tuple-element.21, bf16[128,832]{0,1:T(8,128)(2,1)} %get-tuple-element.20), kind=kOutput, calls=%fused_computation.28 | convolution fusion | flops 873267200 | bytes 5931008 | tf_op jit(solution)/shard_map/ts,srl->trl/dot_general | solution.py:87
  258.1 0.6 gather_fusion.2
  258.9 1.0 copy.44
  (43 shorter events, 2.1 us)
Async XLA Ops:
  0.0 7.4 %copy-start = (s32[4]{0:T(128)S(1)}, s32[4]{0:T(128)}, u32[]{:S(2)}) copy-start(s32[4]{0:T(128)} %constant.37.clone) | copy-start | bytes 52
  0.0 33.5 %collective-permute-start = (bf16[512,1408]{1,0:T(8,128)(2,1)}, bf16[512,1408]{1,0:T(8,128)(2,1)S(1)}, u32[]{:S(2)}, u32[]{:S(2)}) collective-permute-start(bf16[512,1408]{1,0:T(8,128)(2,1)} %bitcast.54), channel_id=1, source_target_pairs={{0,128},{64,192},{128,0},{192,64},{1,129},{65,193},{129,1},{193,65... | collective-permute-start | bytes 4325384 | tf_op jit(solution)/shard_map/ppermute | solution.py:16
  33.5 1.1 copy-start.5
  34.6 94.3 %all-to-all-start = ((bf16[64,208,128]{2,1,0:T(8,128)(2,1)}), bf16[64,208,128]{2,1,0:T(8,128)(2,1)S(1)}, u32[]{:S(2)}, u32[]{:S(2)}) async-start(bf16[64,208,128]{2,1,0:T(8,128)(2,1)} %bitcast.47), calls=%async_computation | async-start | bytes 6815744 | tf_op jit(solution)/shard_map/all_to_all | solution.py:67
  48.8 60.9 %collective-permute-start.3 = (bf16[512,1408]{1,0:T(8,128)(2,1)}, bf16[512,1408]{1,0:T(8,128)(2,1)}, u32[]{:S(2)}, u32[]{:S(2)}) collective-permute-start(bf16[512,1408]{1,0:T(8,128)(2,1)} %bitcast.57), channel_id=1, source_target_pairs={{0,128},{64,192},{128,0},{192,64},{1,129},{65,193},{129,1},{193,65... | collective-permute-start | bytes 4325384 | tf_op jit(solution)/shard_map/ppermute | solution.py:16
  49.6 82.3 %collective-permute-start.1 = (bf16[512,1408]{1,0:T(8,128)(2,1)}, bf16[512,1408]{1,0:T(8,128)(2,1)}, u32[]{:S(2)}, u32[]{:S(2)}) collective-permute-start(bf16[512,1408]{1,0:T(8,128)(2,1)} %bitcast.55), channel_id=1, source_target_pairs={{0,64},{64,0},{128,192},{192,128},{1,65},{65,1},{129,193},{193,129... | collective-permute-start | bytes 4325384 | tf_op jit(solution)/shard_map/ppermute | solution.py:17
  49.6 82.6 %collective-permute-start.2 = (bf16[512,1408]{1,0:T(8,128)(2,1)}, bf16[512,1408]{1,0:T(8,128)(2,1)}, u32[]{:S(2)}, u32[]{:S(2)}) collective-permute-start(bf16[512,1408]{1,0:T(8,128)(2,1)} %copy-done.5), channel_id=1, source_target_pairs={{0,64},{64,0},{128,192},{192,128},{1,65},{65,1},{129,193},{193,129... | collective-permute-start | bytes 4325384 | tf_op jit(solution)/shard_map/ppermute | solution.py:19
  50.1 91.6 %collective-permute-start.4 = (bf16[512,1408]{1,0:T(8,128)(2,1)}, bf16[512,1408]{1,0:T(8,128)(2,1)}, u32[]{:S(2)}, u32[]{:S(2)}) collective-permute-start(bf16[512,1408]{1,0:T(8,128)(2,1)} %bitcast.58), channel_id=1, source_target_pairs={{0,64},{64,0},{128,192},{192,128},{1,65},{65,1},{129,193},{193,129... | collective-permute-start | bytes 4325384 | tf_op jit(solution)/shard_map/ppermute | solution.py:17
  109.8 32.0 %collective-permute-start.5 = (bf16[512,1408]{1,0:T(8,128)(2,1)}, bf16[512,1408]{1,0:T(8,128)(2,1)}, u32[]{:S(2)}, u32[]{:S(2)}) collective-permute-start(bf16[512,1408]{1,0:T(8,128)(2,1)} %collective-permute-done.3), channel_id=1, source_target_pairs={{0,64},{64,0},{128,192},{192,128},{1,65},{65,1},{129,193},{193,129... | collective-permute-start | bytes 4325384 | tf_op jit(solution)/shard_map/ppermute | solution.py:19
  109.8 39.8 %collective-permute-start.6 = (bf16[1408,512]{1,0:T(8,128)(2,1)}, bf16[1408,512]{1,0:T(8,128)(2,1)}, u32[]{:S(2)}, u32[]{:S(2)}) collective-permute-start(bf16[1408,512]{1,0:T(8,128)(2,1)} %bitcast.60), channel_id=1, source_target_pairs={{0,128},{64,192},{128,0},{192,64},{1,129},{65,193},{129,1},{193,65... | collective-permute-start | bytes 4325384 | tf_op jit(solution)/shard_map/ppermute | solution.py:16
  131.9 9.9 %copy-start.1 = (bf16[832,2048]{1,0:T(8,128)(2,1)S(1)}, bf16[832,2048]{1,0:T(8,128)(2,1)}, u32[]{:S(2)}) copy-start(bf16[832,2048]{1,0:T(8,128)(2,1)} %reshape.84) | copy-start | bytes 10223620
  131.9 9.9 %copy-start.3 = (bf16[1,512,1408]{2,1,0:T(8,128)(2,1)S(1)}, bf16[1,512,1408]{2,1,0:T(8,128)(2,1)}, u32[]{:S(2)}) copy-start(bf16[1,512,1408]{2,1,0:T(8,128)(2,1)} %param.15) | copy-start | bytes 4325380
  131.9 17.8 %collective-permute-start.7 = (bf16[1408,512]{1,0:T(8,128)(2,1)}, bf16[1408,512]{1,0:T(8,128)(2,1)S(1)}, u32[]{:S(2)}, u32[]{:S(2)}) collective-permute-start(bf16[1408,512]{1,0:T(8,128)(2,1)} %bitcast.61), channel_id=1, source_target_pairs={{0,64},{64,0},{128,192},{192,128},{1,65},{65,1},{129,193},{193,129... | collective-permute-start | bytes 4325384 | tf_op jit(solution)/shard_map/ppermute | solution.py:17
  141.7 8.0 %copy-start.4 = (bf16[1,1408,512]{2,1,0:T(8,128)(2,1)S(1)}, bf16[1,1408,512]{2,1,0:T(8,128)(2,1)}, u32[]{:S(2)}) copy-start(bf16[1,1408,512]{2,1,0:T(8,128)(2,1)} %param.16) | copy-start | bytes 4325380
  149.6 5.6 %collective-permute-start.8 = (bf16[1408,512]{1,0:T(8,128)(2,1)}, bf16[1408,512]{1,0:T(8,128)(2,1)S(1)}, u32[]{:S(2)}, u32[]{:S(2)}) collective-permute-start(bf16[1408,512]{1,0:T(8,128)(2,1)} %collective-permute-done.6), channel_id=1, source_target_pairs={{0,64},{64,0},{128,192},{192,128},{1,65},{65,1},{129,193},{193,129... | collective-permute-start | bytes 4325384 | tf_op jit(solution)/shard_map/ppermute | solution.py:19
  160.2 14.2 %copy-start.2 = (f32[128,6]{0,1:T(8,128)S(1)}, f32[128,6]{0,1:T(8,128)}, u32[]{:S(2)}) copy-start(f32[128,6]{0,1:T(8,128)} %param.12) | copy-start | bytes 9220
  160.2 95.0 %all-to-all-start.1 = ((bf16[64,208,128]{2,1,0:T(8,128)(2,1)}), bf16[64,208,128]{2,1,0:T(8,128)(2,1)S(1)}, u32[]{:S(2)}, u32[]{:S(2)}) async-start(bf16[64,208,128]{2,1,0:T(8,128)(2,1)} %convert_element_type.34), calls=%async_computation.1 | async-start | bytes 6815744 | tf_op jit(solution)/shard_map/all_to_all | solution.py:79

commit v10 on v9

--- a/solution.py
+++ b/solution.py
@@ -65,10 +65,10 @@
     send = send.astype(jnp.bfloat16).reshape(n_ep, cap * sub, lanes)
     send = lax.optimization_barrier((send, gate_cross))[0]
     received = lax.all_to_all(send, "ep", 0, 0, tiled=True)
-    received = received.reshape(slots, width)
+    received = received.reshape(slots, sub, lanes)
 
-    gate = jnp.dot(received, wg, preferred_element_type=jnp.float32)
-    up = jnp.dot(received, wu, preferred_element_type=jnp.float32)
+    gate = jnp.einsum("srl,rlf->sf", received, wg.reshape(sub, lanes, -1), preferred_element_type=jnp.float32)
+    up = jnp.einsum("srl,rlf->sf", received, wu.reshape(sub, lanes, -1), preferred_element_type=jnp.float32)
     hidden = (jax.nn.silu(gate) * up).astype(jnp.bfloat16)
     wd = _dp_parts(down_shard, after=lambda: hidden)
     first = jnp.dot(hidden, jnp.concatenate(wd[:3], axis=1), preferred_element_type=jnp.float32)

time: 260 us -> 262 us (level)
  other arithmetic: 4.99 us -> 24.2 us
  waiting for transfers between devices: 177 us -> 162 us
  local copies, waits for them, and re-layouts: 17.3 us -> 14.4 us
    concatenate x0 -> x2, other arithmetic: none -> 19.2 us  [the longest x1 13.5 us: local(): wu = jnp.concatenate(wu, axis=0)]
    all_to_all x1, waiting for transfers between devices: 17.9 us -> 0.01 us  [local(): received = lax.all_to_all(send, 'ep', 0, 0, tiled=True)]
    ppermute x3, waiting for transfers between devices: 79.4 us -> 82.9 us  [_dp_parts(): cross = lax.ppermute(w, 'dp', _perm(n, 2))]
    dot_general x2, matrix products: 17.3 us -> 14.2 us  [the longest x1 8.21 us: local(): jnp.einsum('srl,rlf->sf', received, wg.reshape(sub, lanes, -1), preferred...]
    reshape x1 -> x0, local copies, waits for them, and re-layouts: 2.93 us -> none  [local(): received = received.reshape(slots, width)]
  transfers between devices with their start and end apart: 11 -> 11, of which waited for: 4 -> 4; matrix products, arithmetic and copies ran while one was open for 15% -> 20% of each run, Pallas kernels for 0% -> 0%
where the time goes in v10:
time: 262 us; the launch traced here: 261 us
  waiting for transfers between devices  162 us (62%)
  starting transfers between devices  34.5 us (13%)
  matrix products  25.5 us (10%)
  other arithmetic  24.2 us (9%)
  local copies, waits for them, and re-layouts  14.4 us (5%)
    ppermute x3, waiting for transfers between devices, _dp_parts(): cross = lax.ppermute(w, 'dp', _perm(n, 2))  82.9 us
    all_to_all x1, waiting for transfers between devices, local(): returned = lax.all_to_all(expert_out, 'ep', 0, 0, tiled=True)  79.5 us
    all_to_all x1, starting transfers between devices, local(): returned = lax.all_to_all(expert_out, 'ep', 0, 0, tiled=True)  15.8 us
    all_to_all x1, starting transfers between devices, local(): received = lax.all_to_all(send, 'ep', 0, 0, tiled=True)  14.2 us
    concatenate x1, other arithmetic, local(): wu = jnp.concatenate(wu, axis=0)  13.5 us
    dot_general x1, matrix products, local(): jnp.einsum('srl,rlf->sf', received, wg.reshape(sub, lanes, -1), preferred...  8.21 us
    dot_general x1, matrix products, local(): jnp.einsum('srl,rlf->sf', received, wu.reshape(sub, lanes, -1), preferred...  6.01 us
    dot_general x1, matrix products, local(): jnp.dot(hidden, jnp.concatenate(wd[:3], axis=1), preferred_element_type=j...  5.92 us
  transfers between devices with their start and end apart: 11, of which 4 were waited for; matrix products, arithmetic and copies ran while one was open for 20% of the time, Pallas kernels for 0%

profile of v10, /device:TPU:38, one launch (start us, length us, event | category | flops | bytes accessed | tf_op | source)
XLA Modules:
  0.0 261.3 jit_solution(15003663064905750066)
XLA Ops:
  0.0 1.6 collective-permute-start
  1.6 0.8 copy.35
  2.5 1.8 reduce-window.6
  4.8 0.8 select_reduce_fusion.1
  5.8 1.3 copy.40
  7.4 0.6 gather_fusion.1
  8.4 0.4 fusion.18
  8.8 1.1 convolution_convert_fusion
  9.9 4.0 %copy.44 = bf16[832,16,128]{2,1,0:T(8,128)(2,1)} copy(bf16[832,16,128]{2,0,1:T(8,128)(2,1)S(1)} %convolution_convert_fusion) | data formatting | bytes 6815744 | tf_op jit(solution)/shard_map/convert_element_type | solution.py:65
  13.9 19.6 %collective-permute-done = bf16[512,1408]{1,0:T(8,128)(2,1)S(1)} collective-permute-done((bf16[512,1408]{1,0:T(8,128)(2,1)}, bf16[512,1408]{1,0:T(8,128)(2,1)S(1)}, u32[]{:S(2)}, u32[]{:S(2)}) %collective-permute-start) | collective-permute-done | bytes 1441824 | tf_op jit(solution)/shard_map/ppermute | solution.py:16
  33.5 1.1 copy-done.3
  34.7 14.2 %all-to-all-start = ((bf16[64,208,128]{2,1,0:T(8,128)(2,1)}), bf16[64,208,128]{2,1,0:T(8,128)(2,1)S(1)}, u32[]{:S(2)}, u32[]{:S(2)}) async-start(bf16[64,208,128]{2,1,0:T(8,128)(2,1)} %bitcast.7), calls=%async_computation | async-start | bytes 6815744 | tf_op jit(solution)/shard_map/all_to_all | solution.py:67
  48.9 0.8 collective-permute-start.3
  49.6 0.5 collective-permute-start.2
  50.1 59.5 %collective-permute-done.3 = bf16[512,1408]{1,0:T(8,128)(2,1)S(1)} collective-permute-done((bf16[512,1408]{1,0:T(8,128)(2,1)}, bf16[512,1408]{1,0:T(8,128)(2,1)S(1)}, u32[]{:S(2)}, u32[]{:S(2)}) %collective-permute-start.3) | collective-permute-done | bytes 1441824 | tf_op jit(solution)/shard_map/ppermute | solution.py:16
  109.7 1.3 collective-permute-start.6
  111.3 5.7 %pad_maximum_fusion = bf16[2048,1408]{1,0:T(8,128)(2,1)} fusion(bf16[512,1408]{1,0:T(8,128)(2,1)S(1)} %collective-permute-done.2, bf16[512,1408]{1,0:T(8,128)(2,1)S(1)} %collective-permute-done.1, bf16[512,1408]{1,0:T(8,128)(2,1)} %copy-done.3, bf16[512,1408]{1,0:T(8,128)(2,1)} %bitcast.78), kind=kLoop, calls=%fused_computation.3 | loop fusion | flops 23068672 | bytes 11534336 | tf_op jit(solution)/shard_map/concatenate | solution.py:43
  117.0 13.5 %pad_maximum_fusion.1 = bf16[2048,1408]{1,0:T(8,128)(2,1)} fusion(bf16[512,1408]{1,0:T(8,128)(2,1)S(1)} %collective-permute-done.5, bf16[512,1408]{1,0:T(8,128)(2,1)S(1)} %collective-permute-done.4, bf16[512,1408]{1,0:T(8,128)(2,1)S(1)} %collective-permute-done.3, bf16[512,1408]{1,0:T(8,128)(2,1)S(1)} %bitcast.81), kind=kLoop, calls=%fused_computation.4 | loop fusion | flops 23068672 | bytes 11534336 | tf_op jit(solution)/shard_map/concatenate | solution.py:45
  130.5 8.2 %fusion.16 = f32[832,1408,1]{1,0,2:T(8,128)S(1)} fusion(bf16[16,128,1408]{2,1,0:T(8,128)(2,1)} %bitcast.67, bf16[832,16,128]{2,1,0:T(8,128)(2,1)S(1)} %bitcast.69), kind=kOutput, calls=%fused_computation.23 | convolution fusion | flops 4798283776 | bytes 13860864 | tf_op jit(solution)/shard_map/srl,rlf->sf/dot_general | solution.py:70
  138.8 6.0 %fusion = bf16[832,1408]{1,0:T(8,128)(2,1)S(1)} fusion(f32[832,1408,1]{1,0,2:T(8,128)S(1)} %fusion.16, bf16[16,128,1408]{2,1,0:T(8,128)(2,1)S(1)} %bitcast.68, bf16[832,16,128]{2,1,0:T(8,128)(2,1)S(1)} %bitcast.70), kind=kOutput, calls=%fused_computation.6 | convolution fusion | flops 4805312512 | bytes 16203776 | tf_op jit(solution)/shard_map/srl,rlf->sf/dot_general | solution.py:71
  144.8 3.7 %collective-permute-done.6 = bf16[1408,512]{1,0:T(8,128)(2,1)} collective-permute-done((bf16[1408,512]{1,0:T(8,128)(2,1)}, bf16[1408,512]{1,0:T(8,128)(2,1)}, u32[]{:S(2)}, u32[]{:S(2)}) %collective-permute-start.6) | collective-permute-done | bytes 1441824 | tf_op jit(solution)/shard_map/ppermute | solution.py:16
  148.5 5.9 %fusion.10 = bf16[832,1536]{1,0:T(8,128)(2,1)S(1)} fusion(bf16[832,1408]{1,0:T(8,128)(2,1)S(1)} %fusion, bf16[1408,512]{1,0:T(8,128)(2,1)} %collective-permute-done.7, bf16[1408,512]{1,0:T(8,128)(2,1)} %collective-permute-done.6, bf16[1408,512]{1,0:T(8,128)(2,1)S(1)} %bitcast.85), kind=kOutput, calls=%fused_computation.18 | convolution fusion | flops 3612966912 | bytes 9224192 | tf_op jit(solution)/shard_map/dot_general | solution.py:74
  154.4 1.5 convolution_convert_fusion.1
  155.9 0.4 pad_maximum_fusion.2
  156.4 3.0 %convert_element_type.34 = bf16[64,208,128]{2,1,0:T(8,128)(2,1)} reshape(bf16[832,2048]{1,0:T(8,128)(2,1)S(1)} %pad_maximum_fusion.2) | data formatting | bytes 6815744 | tf_op jit(solution)/shard_map/convert_element_type | solution.py:76
  159.4 15.8 %all-to-all-start.1 = ((bf16[64,208,128]{2,1,0:T(8,128)(2,1)}), bf16[64,208,128]{2,1,0:T(8,128)(2,1)S(1)}, u32[]{:S(2)}, u32[]{:S(2)}) async-start(bf16[64,208,128]{2,1,0:T(8,128)(2,1)} %convert_element_type.34), calls=%async_computation.1 | async-start | bytes 6815744 | tf_op jit(solution)/shard_map/all_to_all | solution.py:79
  175.3 0.6 gather_fusion
  176.3 0.8 reduce-precision_convert_fusion
  177.1 79.5 %all-to-all-done.1 = bf16[64,208,128]{2,1,0:T(8,128)(2,1)S(1)} async-done(((bf16[64,208,128]{2,1,0:T(8,128)(2,1)}), bf16[64,208,128]{2,1,0:T(8,128)(2,1)S(1)}, u32[]{:S(2)}, u32[]{:S(2)}) %all-to-all-start.1) | async-done | bytes 3407904 | tf_op jit(solution)/shard_map/all_to_all | solution.py:79
  256.6 2.8 %fusion.13 = f32[256,16,128]{0,2,1:T(8,128)S(1)} fusion(bf16[832,16,128]{2,1,0:T(8,128)(2,1)S(1)} %bitcast.71, bf16[128,832]{0,1:T(8,128)(2,1)} %get-tuple-element.21, bf16[128,832]{0,1:T(8,128)(2,1)} %get-tuple-element.20), kind=kOutput, calls=%fused_computation.20 | convolution fusion | flops 873267200 | bytes 5931008 | tf_op jit(solution)/shard_map/ts,srl->trl/dot_general | solution.py:87
  259.5 0.6 gather_fusion.2
  260.3 1.0 copy.50
  (44 shorter events, 2.3 us)
Async XLA Ops:
  0.0 7.4 %copy-start = (s32[4]{0:T(128)S(1)}, s32[4]{0:T(128)}, u32[]{:S(2)}) copy-start(s32[4]{0:T(128)} %constant.37.clone) | copy-start | bytes 52
  0.0 33.5 %collective-permute-start = (bf16[512,1408]{1,0:T(8,128)(2,1)}, bf16[512,1408]{1,0:T(8,128)(2,1)S(1)}, u32[]{:S(2)}, u32[]{:S(2)}) collective-permute-start(bf16[512,1408]{1,0:T(8,128)(2,1)} %bitcast.76), channel_id=1, source_target_pairs={{0,128},{64,192},{128,0},{192,64},{1,129},{65,193},{129,1},{193,65... | collective-permute-start | bytes 4325384 | tf_op jit(solution)/shard_map/ppermute | solution.py:16
  33.5 1.1 copy-start.3
  34.7 95.9 %all-to-all-start = ((bf16[64,208,128]{2,1,0:T(8,128)(2,1)}), bf16[64,208,128]{2,1,0:T(8,128)(2,1)S(1)}, u32[]{:S(2)}, u32[]{:S(2)}) async-start(bf16[64,208,128]{2,1,0:T(8,128)(2,1)} %bitcast.7), calls=%async_computation | async-start | bytes 6815744 | tf_op jit(solution)/shard_map/all_to_all | solution.py:67
  48.9 60.8 %collective-permute-start.3 = (bf16[512,1408]{1,0:T(8,128)(2,1)}, bf16[512,1408]{1,0:T(8,128)(2,1)S(1)}, u32[]{:S(2)}, u32[]{:S(2)}) collective-permute-start(bf16[512,1408]{1,0:T(8,128)(2,1)} %bitcast.79), channel_id=1, source_target_pairs={{0,128},{64,192},{128,0},{192,64},{1,129},{65,193},{129,1},{193,65... | collective-permute-start | bytes 4325384 | tf_op jit(solution)/shard_map/ppermute | solution.py:16
  49.6 61.4 %collective-permute-start.1 = (bf16[512,1408]{1,0:T(8,128)(2,1)}, bf16[512,1408]{1,0:T(8,128)(2,1)S(1)}, u32[]{:S(2)}, u32[]{:S(2)}) collective-permute-start(bf16[512,1408]{1,0:T(8,128)(2,1)} %bitcast.77), channel_id=1, source_target_pairs={{0,64},{64,0},{128,192},{192,128},{1,65},{65,1},{129,193},{193,129... | collective-permute-start | bytes 4325384 | tf_op jit(solution)/shard_map/ppermute | solution.py:17
  49.6 61.6 %collective-permute-start.2 = (bf16[512,1408]{1,0:T(8,128)(2,1)}, bf16[512,1408]{1,0:T(8,128)(2,1)S(1)}, u32[]{:S(2)}, u32[]{:S(2)}) collective-permute-start(bf16[512,1408]{1,0:T(8,128)(2,1)} %copy-done.3), channel_id=1, source_target_pairs={{0,64},{64,0},{128,192},{192,128},{1,65},{65,1},{129,193},{193,129... | collective-permute-start | bytes 4325384 | tf_op jit(solution)/shard_map/ppermute | solution.py:19
  50.1 66.8 %collective-permute-start.4 = (bf16[512,1408]{1,0:T(8,128)(2,1)}, bf16[512,1408]{1,0:T(8,128)(2,1)S(1)}, u32[]{:S(2)}, u32[]{:S(2)}) collective-permute-start(bf16[512,1408]{1,0:T(8,128)(2,1)} %bitcast.80), channel_id=1, source_target_pairs={{0,64},{64,0},{128,192},{192,128},{1,65},{65,1},{129,193},{193,129... | collective-permute-start | bytes 4325384 | tf_op jit(solution)/shard_map/ppermute | solution.py:17
  109.7 7.3 %collective-permute-start.5 = (bf16[512,1408]{1,0:T(8,128)(2,1)S(1)}, bf16[512,1408]{1,0:T(8,128)(2,1)S(1)}, u32[]{:S(2)}, u32[]{:S(2)}) collective-permute-start(bf16[512,1408]{1,0:T(8,128)(2,1)S(1)} %collective-permute-done.3), channel_id=1, source_target_pairs={{0,64},{64,0},{128,192},{192,128},{1,65},{65,1},{129,193},{193,129... | collective-permute-start | bytes 4325384 | tf_op jit(solution)/shard_map/ppermute | solution.py:19
  109.7 7.3 %copy-start.2 = (bf16[1,512,1408]{2,1,0:T(8,128)(2,1)S(1)}, bf16[1,512,1408]{2,1,0:T(8,128)(2,1)}, u32[]{:S(2)}) copy-start(bf16[1,512,1408]{2,1,0:T(8,128)(2,1)} %param.15) | copy-start | bytes 4325380
  109.7 38.8 %collective-permute-start.6 = (bf16[1408,512]{1,0:T(8,128)(2,1)}, bf16[1408,512]{1,0:T(8,128)(2,1)}, u32[]{:S(2)}, u32[]{:S(2)}) collective-permute-start(bf16[1408,512]{1,0:T(8,128)(2,1)} %bitcast.83), channel_id=1, source_target_pairs={{0,128},{64,192},{128,0},{192,64},{1,129},{65,193},{129,1},{193,65... | collective-permute-start | bytes 4325384 | tf_op jit(solution)/shard_map/ppermute | solution.py:16
  111.0 37.5 %collective-permute-start.7 = (bf16[1408,512]{1,0:T(8,128)(2,1)}, bf16[1408,512]{1,0:T(8,128)(2,1)}, u32[]{:S(2)}, u32[]{:S(2)}) collective-permute-start(bf16[1408,512]{1,0:T(8,128)(2,1)} %bitcast.84), channel_id=1, source_target_pairs={{0,64},{64,0},{128,192},{192,128},{1,65},{65,1},{129,193},{193,129... | collective-permute-start | bytes 4325384 | tf_op jit(solution)/shard_map/ppermute | solution.py:17
  130.5 8.2 %copy-start.1 = (bf16[2048,1408]{1,0:T(8,128)(2,1)S(1)}, bf16[2048,1408]{1,0:T(8,128)(2,1)}, u32[]{:S(2)}) copy-start(bf16[2048,1408]{1,0:T(8,128)(2,1)} %pad_maximum_fusion.1) | copy-start | bytes 17301508
  138.8 9.8 %copy-start.5 = (bf16[1,1408,512]{2,1,0:T(8,128)(2,1)S(1)}, bf16[1,1408,512]{2,1,0:T(8,128)(2,1)}, u32[]{:S(2)}) copy-start(bf16[1,1408,512]{2,1,0:T(8,128)(2,1)} %param.16) | copy-start | bytes 4325380
  148.5 5.9 %collective-permute-start.8 = (bf16[1408,512]{1,0:T(8,128)(2,1)}, bf16[1408,512]{1,0:T(8,128)(2,1)S(1)}, u32[]{:S(2)}, u32[]{:S(2)}) collective-permute-start(bf16[1408,512]{1,0:T(8,128)(2,1)} %collective-permute-done.6), channel_id=1, source_target_pairs={{0,64},{64,0},{128,192},{192,128},{1,65},{65,1},{129,193},{193,129... | collective-permute-start | bytes 4325384 | tf_op jit(solution)/shard_map/ppermute | solution.py:19
  159.4 16.5 %copy-start.4 = (f32[128,6]{0,1:T(8,128)S(1)}, f32[128,6]{0,1:T(8,128)}, u32[]{:S(2)}) copy-start(f32[128,6]{0,1:T(8,128)} %param.12) | copy-start | bytes 9220
  159.4 97.2 %all-to-all-start.1 = ((bf16[64,208,128]{2,1,0:T(8,128)(2,1)}), bf16[64,208,128]{2,1,0:T(8,128)(2,1)S(1)}, u32[]{:S(2)}, u32[]{:S(2)}) async-start(bf16[64,208,128]{2,1,0:T(8,128)(2,1)} %convert_element_type.34), calls=%async_computation.1 | async-start | bytes 6815744 | tf_op jit(solution)/shard_map/all_to_all | solution.py:79
